TPU v7x, 32 devices: a whole 2x2x4 slice. The times are simulated.
32 devices in a mesh: parts: 2 (over y), aux: 4 (over x, core), pair: 4 (over z).
Axes of the slice: x: 2, y: 2, z: 4, core: 2. Of those that a mesh axis runs over, the one named last changes fastest.
Arguments:
- cholesky: bfloat16 [96, 832, 832], P(('parts', 'aux', 'pair')), parts along dimension 0, may hold values from -1.5 to 1.5
- occ_coef: bfloat16 [2, 2, 832, 128], replicated, may hold values from -0.15625 to 0.15625
- vir_coef: bfloat16 [2, 2, 832, 1536], P(None, None, None, 'pair'), may hold values from -0.15625 to 0.15625
- occ_energy: float32 [128], replicated, may hold values from -3 to -0.3
- vir_energy: float32 [1536], replicated, may hold values from 0.2 to 3
- batch_occ: int32 [3], replicated, may hold values from 0 to 127, as said below
Outputs:
- pair_vectors: bfloat16 [96, 128, 2, 1536], P(('parts', 'aux', 'pair')), parts along dimension 0
- amplitudes: float32 [3072, 2, 3, 3, 1536], P(('parts', 'aux'), None, None, None, 'pair'), parts along dimension 0
There are 2 independent parts, one for each index of `parts`. A program takes and returns all parts, laid end to end along the dimension named above; an argument that names none is the same for every part. Nothing has to cross between parts.
Inputs may be any that keep to these rules, and one draw needn't show every extreme that they name: `batch_occ`: 3 distinct occupied indices, the highest occupied spinor 128 - 1 always among them.
All inputs are finite; a program needn't handle non-finite values.
Results may differ from a plain program's by a relative error of at most 0.0064.
Values may be sent and summed in bfloat16 or wider, within the bound.
No kernel may reach another device: no remote copies, remote signals or barrier semaphores. Data moves between devices by JAX's collectives and lax.ppermute only.
A program may use at most 192 MiB of HBM per device.

v0:
```python
import jax
import jax.numpy as jnp
from jax import lax
from jax.sharding import PartitionSpec as P


def stacked_right(coef_rows):
    middle = coef_rows.shape[0] // 2
    real_rows = coef_rows[:middle]
    imag_rows = coef_rows[middle:]
    real_side = jnp.concatenate([real_rows, -imag_rows], 0)
    imag_side = jnp.concatenate([imag_rows, real_rows], 0)
    return jnp.concatenate([real_side, imag_side], 1)


def pair_terms(batch_rows, column_rows):
    left = jnp.concatenate([batch_rows[:, :, 0, :], batch_rows[:, :, 1, :]], 0)
    real_right = jnp.concatenate([column_rows[:, :, 0, :], -column_rows[:, :, 1, :]], 0)
    imag_right = jnp.concatenate([column_rows[:, :, 1, :], column_rows[:, :, 0, :]], 0)
    right = jnp.stack([real_right, imag_right], 1)
    return jnp.einsum("pjb,pcia->bcija", left, right, preferred_element_type=jnp.float32)


def on_device(cholesky, occ_coef, vir_coef, occ_energy, vir_energy, batch_occ):
    vectors = cholesky.shape[0]
    orbitals = cholesky.shape[1]
    occupied = occ_coef.shape[3]
    occ_left = jnp.concatenate([occ_coef[0], -occ_coef[1]], 0)
    half = jnp.einsum(
        "kmj,pmn->pjkn", occ_left, cholesky, preferred_element_type=jnp.float32
    ).astype(jnp.bfloat16)
    flat = half.reshape(vectors * occupied, 4 * orbitals)
    piece = lax.all_gather(vir_coef, "pair", axis=3, tiled=True)
    count = piece.shape[3]
    right = stacked_right(piece.reshape(4 * orbitals, count))
    full = jnp.dot(flat, right, preferred_element_type=jnp.float32).astype(jnp.bfloat16)
    pair_vectors = full.reshape(vectors, occupied, 2, count)
    selected = jnp.take(pair_vectors, batch_occ, axis=1)
    virtuals = pair_vectors.shape[3]
    a_width = vir_coef.shape[3]
    a_start = lax.axis_index("pair") * a_width
    b_width = virtuals // lax.axis_size("aux")
    b_start = lax.axis_index("aux") * b_width
    group = lax.all_gather(selected, "pair", axis=0, tiled=True)
    own_block = lax.dynamic_slice_in_dim(group, a_start, a_width, 3)
    summed = lax.psum_scatter(pair_terms(group, own_block), "aux", scatter_dimension=0, tiled=True)
    paired = summed - jnp.swapaxes(summed, 2, 3)
    occ_sel = jnp.take(occ_energy, batch_occ)
    vir_first = lax.dynamic_slice_in_dim(vir_energy, a_start, a_width)
    vir_second = lax.dynamic_slice_in_dim(vir_energy, b_start, b_width)
    denominator = (
        (occ_sel[:, None] + occ_sel[None, :])[None, None, :, :, None]
        - vir_first[None, None, None, None, :]
        - vir_second[:, None, None, None, None]
    )
    return (pair_vectors, paired / denominator)


def solution(mesh):
    return jax.shard_map(
        on_device,
        mesh=mesh,
        in_specs=(
            P(("parts", "aux", "pair"), None, None),
            P(),
            P(None, None, None, "pair"),
            P(),
            P(),
            P(),
        ),
        out_specs=(
            P(("parts", "aux", "pair"), None, None, None),
            P(("parts", "aux"), None, None, None, "pair"),
        ),
        check_vma=False,
    )
```

profile of v0, /device:TPU:29, one launch (start us, length us, event | category | flops | bytes accessed | tf_op | source)
XLA Modules:
  0.0 592.9 jit_solution(4900267249441975278)
XLA Ops:
  7.2 0.0 copy-start
  7.2 0.0 all-gather.2.cloned.1.call-start
  7.2 0.7 all-gather.2.cloned.1.call-update
  7.9 0.0 reduce-scatter.2.cloned.1.call-start
  8.0 1.2 slice_bitcast_fusion
  9.2 7.5 %convert_bitcast_fusion = bf16[3,128,4,832]{1,3,0,2:T(8,128)(2,1)} fusion(bf16[3,832,832]{2,1,0:T(8,128)(2,1)} %param.6, bf16[2,832,128]{2,1,0:T(8,128)(2,1)S(1)} %get-tuple-element.15, bf16[2,832,128]{2,1,0:T(8,128)(2,1)S(1)} %get-tuple-element.14), kind=kOutput, calls=%fused_computation.17 | convolution fusion | flops 2129494016 | bytes 7561216 | tf_op jit(solution)/shard_map/kmj,pmn->pjkn/dot_general | solution.py:29
  16.7 0.0 copy-start.5
  16.7 5.2 copy.17
  21.9 3.4 reshape.74
  25.3 0.0 copy-done.5
  25.3 0.0 copy-done
  25.3 0.6 gather_fusion.1
  25.9 161.7 %all-gather.2.cloned.1.call-done = bf16[2,2,832,1536]{3,2,1,0:T(8,128)(2,1)} async-done(((bf16[2,2,832,384]{3,2,1,0:T(8,128)(2,1)}), bf16[2,2,832,1536]{3,2,1,0:T(8,128)(2,1)}) %all-gather.2.cloned.1.call-update) | async-done | bytes 10223632 | tf_op jit(solution)/shard_map/all_gather | solution.py:33
  187.6 7.0 %fusion.27 = (bf16[1,2,832,1536]{3,2,1,0:T(8,128)(2,1)S(1)}, bf16[1,2,832,1536]{3,2,1,0:T(8,128)(2,1)}) fusion(bf16[2,2,832,1536]{3,2,1,0:T(8,128)(2,1)} %all-gather.2.cloned.1.call-done), kind=kLoop, calls=%fused_computation.50 | loop fusion | bytes 20447232 | tf_op jit(solution)/shard_map/slice | solution.py:10
  194.6 0.0 copy-start.2
  194.6 3.3 bitcast_negate_fusion
  197.9 0.6 copy-done.2
  198.5 23.3 %fusion.11 = bf16[384,3072]{1,0:T(8,128)(2,1)} fusion(bf16[384,3328]{1,0:T(8,128)(2,1)} %reshape.74, bf16[1664,1536]{1,0:T(8,128)(2,1)} %bitcast.53, bf16[1664,1536]{1,0:T(8,128)(2,1)} %bitcast.52, bf16[1664,1536]{1,0:T(8,128)(2,1)} %bitcast_negate_fusion), kind=kOutput, calls=%fused_computation.15 | convolution fusion | flops 7934705664 | bytes 20250624 | tf_op jit(solution)/shard_map/dot_general | solution.py:36
  221.7 5.6 reshape.75
  227.3 0.0 copy-start.3
  227.3 0.7 gather_fusion
  228.0 0.1 fusion.22
  228.1 12.1 %all_gather.7 = bf16[12,3,2,1536]{3,2,1,0:T(2,128)(2,1)S(1)} all-gather(bf16[3,3,2,1536]{3,2,1,0:T(2,128)(2,1)S(1)} %copy.18), channel_id=1, replica_groups=mesh['parts'=2,'aux'=4,'pair'=4] {'pair'}, dimensions={0}, use_global_device_ids=true | all-gather | bytes 276480 | tf_op jit(solution)/shard_map/all_gather | solution.py:44
  240.2 0.3 fusion.28
  240.5 0.2 constant_dynamic-slice_fusion.1
  240.8 16.7 %convolution_bitcast_fusion = f32[1536,2,3,3,384]{0,4,3,2,1:T(8,128)} fusion(bf16[12,3,1536]{2,0,1:T(8,128)(2,1)S(1)} %get-tuple-element.24, bf16[12,3,1536]{2,0,1:T(8,128)(2,1)S(1)} %get-tuple-element.25, bf16[24,1,3,384]{3,0,2,1:T(8,128)(2,1)S(1)} %get-tuple-element.21, bf16[24,1,3,384]{3,0,2,1:T(8,128)(2,1)S(1)} %get-tuple-element.20), kind=kOutput, calls=%fused_computation.2 | convolution fusion | flops 510271488 | bytes 42799104 | tf_op jit(solution)/shard_map/pjb,pcia->bcija/dot_general | solution.py:21
  257.5 0.0 copy-done.3
  257.5 0.0 copy-start.4
  257.5 0.0 reduce-scatter.2.cloned.1.call-update
  257.5 0.7 copy-done.4
  258.2 0.1 fusion.29
  258.3 0.1 broadcast_add_fusion
  258.3 0.1 broadcast_subtract_fusion.1
  258.4 2.9 broadcast_subtract_fusion
  261.3 291.4 %reduce-scatter.2.cloned.1.call-done = f32[384,2,3,3,384]{0,4,3,2,1:T(8,128)} async-done(((f32[1536,2,3,3,384]{0,4,3,2,1:T(8,128)}), f32[384,2,3,3,384]{0,4,3,2,1:T(8,128)}) %reduce-scatter.2.cloned.1.call-update) | async-done | bytes 10616848 | tf_op jit(solution)/shard_map/reduce_scatter | solution.py:46
  552.7 13.5 %fusion.8 = f32[384,2,3,3,384]{0,4,3,2,1:T(8,128)} fusion(f32[384,2,3,3,384]{0,4,3,2,1:T(8,128)} %reduce-scatter.2.cloned.1.call-done, f32[384,3,3,384]{0,3,2,1:T(8,128)} %broadcast_subtract_fusion), kind=kLoop, calls=%fused_computation.12 | loop fusion | flops 5308416 | bytes 26542080 | tf_op jit(solution)/shard_map/div | solution.py:56
  566.3 0.0 copy-start.1
  566.3 19.7 %copy.23 = f32[384,2,3,3,384]{4,1,3,2,0:T(2,128)} copy(f32[384,2,3,3,384]{0,4,3,2,1:T(8,128)} %fusion.8) | data formatting | bytes 21233664
  586.0 0.0 copy-done.1
  (8 shorter events, 0.2 us)
Async XLA Ops:
  7.2 18.1 %copy-start = (f32[128]{0:T(128)S(1)}, f32[128]{0:T(128)}, u32[]{:S(2)}) copy-start(f32[128]{0:T(128)} %param.9) | copy-start | bytes 1540
  7.2 180.4 %all-gather.2.cloned.1.call-start = ((), (), s32[]{:S(2)}) async-start(), calls=%async_computation.1 | async-start | bytes 12779520 | tf_op jit(solution)/shard_map/all_gather | solution.py:33
  7.9 544.8 %reduce-scatter.2.cloned.1.call-start = ((), (), s32[]{:S(2)}) async-start(), calls=%async_computation.2 | async-start | bytes 53084160 | tf_op jit(solution)/shard_map/reduce_scatter | solution.py:46
  16.7 8.6 %copy-start.5 = (s32[3]{0:T(128)S(1)}, s32[3]{0:T(128)}, u32[]{:S(2)}) copy-start(s32[3]{0:T(128)} %param.11) | copy-start | bytes 40
  194.6 3.9 copy-start.2
  227.3 30.2 %copy-start.3 = (bf16[3,128,2,1536]{3,2,1,0:T(2,128)(2,1)}, bf16[3,128,2,1536]{3,2,1,0:T(2,128)(2,1)S(1)}, u32[]{:S(2)}) copy-start(bf16[3,128,2,1536]{3,2,1,0:T(2,128)(2,1)S(1)} %reshape.75) | copy-start | bytes 7077892
  257.5 0.7 copy-start.4
  566.3 19.7 %copy-start.1 = (f32[128]{0:T(128)S(1)}, f32[128]{0:T(128)}, u32[]{:S(2)}) copy-start(f32[128]{0:T(128)} %param.9) | copy-start | bytes 1540
Sparse Core Ops, SparseCore 0:
  9.6 177.9 all-gather.1
  257.6 295.0 reduce-scatter.1
where the time goes:
time: 595 us; the launch traced here: 593 us
  waiting for transfers between devices  454 us (76%)
  matrix products  47.4 us (8%)
  local copies, waits for them, and re-layouts  44 us (7%)
  other arithmetic  21.3 us (4%)
  between operations  14.2 us (2%)
  blocking collectives  12.1 us (2%)
    reduce_scatter x1, waiting for transfers between devices, on_device(): lax.psum_scatter(pair_terms(group, own_block), 'aux', scatter_dimension=0...  291 us
    all_gather x1, waiting for transfers between devices, on_device(): piece = lax.all_gather(vir_coef, 'pair', axis=3, tiled=True)  162 us
    dot_general x1, matrix products, on_device(): jnp.dot(flat, right, preferred_element_type=jnp.float32)  23.3 us
    unnamed x14, local copies, waits for them, and re-layouts  21 us
    dot_general x1, matrix products, pair_terms(): jnp.einsum('pjb,pcia->bcija', left, right, preferred_element_type=jnp.flo...  16.7 us
    div x1, other arithmetic, on_device(): return (pair_vectors, paired / denominator)  13.5 us
    all_gather x1, blocking collectives, on_device(): group = lax.all_gather(selected, 'pair', axis=0, tiled=True)  12.1 us
  transfers between devices with their start and end apart: 2, of which 2 were waited for; matrix products, arithmetic and copies ran while one was open for 4% of the time, Pallas kernels for 0%

commit v1 on v0

v1 whole, which is shorter than its diff:
```python
import jax
import jax.numpy as jnp
from jax import lax
from jax.sharding import PartitionSpec as P


def complex_rows(half):
    real_part, imag_part = half[..., :2, :], half[..., 2:, :]
    c0 = jnp.concatenate([real_part, -imag_part], -2)
    c1 = jnp.concatenate([imag_part, real_part], -2)
    return jnp.stack([c0, c1], -3)


def pair_terms(batch_rows, column_rows):
    left = jnp.concatenate([batch_rows[:, :, 0, :], batch_rows[:, :, 1, :]], 0)
    real_right = jnp.concatenate([column_rows[:, :, 0, :], -column_rows[:, :, 1, :]], 0)
    imag_right = jnp.concatenate([column_rows[:, :, 1, :], column_rows[:, :, 0, :]], 0)
    right = jnp.stack([real_right, imag_right], 1)
    return jnp.einsum("pjb,pcia->bcija", left, right, preferred_element_type=jnp.float32)


def on_device(cholesky, occ_coef, vir_coef, occ_energy, vir_energy, batch_occ):
    vectors = cholesky.shape[0]
    orbitals = cholesky.shape[1]
    occupied = occ_coef.shape[3]
    a_width = vir_coef.shape[3]
    n_pair = lax.axis_size("pair")
    n_aux = lax.axis_size("aux")
    n_parts = lax.axis_size("parts")
    rows = 4 * orbitals
    virtuals = n_pair * a_width

    occ_left = jnp.concatenate([occ_coef[0], -occ_coef[1]], 0)
    v_local = vir_coef.reshape(rows, a_width)

    occ_sel = jnp.take(occ_left, batch_occ, axis=2)
    half_sel = jnp.einsum(
        "kmi,pmn->pikn", occ_sel, cholesky, preferred_element_type=jnp.float32
    ).astype(jnp.bfloat16)
    half_sel_all = lax.all_gather(half_sel, ("aux", "pair"), axis=0, tiled=True)
    count = half_sel_all.shape[0]
    batch = half_sel_all.shape[1]
    lhs_sel = complex_rows(half_sel_all).reshape(count * batch * 2, rows)
    sel_own = jnp.dot(lhs_sel, v_local, preferred_element_type=jnp.float32).astype(jnp.bfloat16)
    sel_own = sel_own.reshape(count, batch, 2, a_width)

    n_q = n_parts * n_aux
    rows_q = rows // n_q
    q = lax.axis_index("parts") * n_aux + lax.axis_index("aux")
    piece = lax.dynamic_slice_in_dim(v_local, q * rows_q, rows_q, 0)
    stage1 = lax.all_gather(piece, "pair", axis=0)
    stage2 = lax.all_gather(stage1, ("parts", "aux"), axis=1)
    v_full = stage2.reshape(n_pair, rows, a_width)

    half = jnp.einsum(
        "kmj,pmn->pjkn", occ_left, cholesky, preferred_element_type=jnp.float32
    ).astype(jnp.bfloat16)
    lhs = complex_rows(half).reshape(vectors * occupied * 2, rows)
    full = jnp.einsum("mk,bkn->mbn", lhs, v_full, preferred_element_type=jnp.float32)
    pair_vectors = full.astype(jnp.bfloat16).reshape(vectors, occupied, 2, virtuals)

    a_start = lax.axis_index("pair") * a_width
    b_width = virtuals // n_aux
    b_start = lax.axis_index("aux") * b_width
    sel_full = lax.all_gather(sel_own, "pair", axis=3, tiled=True)
    sel_b = lax.dynamic_slice_in_dim(sel_full, b_start, b_width, 3)
    coulomb = pair_terms(sel_b, sel_own)
    paired = coulomb - jnp.swapaxes(coulomb, 2, 3)
    occ_e = jnp.take(occ_energy, batch_occ)
    vir_first = lax.dynamic_slice_in_dim(vir_energy, a_start, a_width)
    vir_second = lax.dynamic_slice_in_dim(vir_energy, b_start, b_width)
    denominator = (
        (occ_e[:, None] + occ_e[None, :])[None, None, :, :, None]
        - vir_first[None, None, None, None, :]
        - vir_second[:, None, None, None, None]
    )
    return (pair_vectors, paired / denominator)


def solution(mesh):
    return jax.shard_map(
        on_device,
        mesh=mesh,
        in_specs=(
            P(("parts", "aux", "pair"), None, None),
            P(),
            P(None, None, None, "pair"),
            P(),
            P(),
            P(),
        ),
        out_specs=(
            P(("parts", "aux", "pair"), None, None, None),
            P(("parts", "aux"), None, None, None, "pair"),
        ),
        check_vma=False,
    )
```

time: 595 us -> 215 us (0.36)
  the two profiles are of different devices: /device:TPU:29 before, /device:TPU:0 now
where the time goes in v1:
time: 215 us; the launch traced here: 214 us
  local copies, waits for them, and re-layouts  63.7 us (30%)
  blocking collectives  59 us (27%)
  waiting for transfers between devices  35.3 us (16%)
  matrix products  26.1 us (12%)
  other arithmetic  15.1 us (7%)
  between operations  14.3 us (7%)
    all_gather x1, blocking collectives, on_device(): half_sel_all = lax.all_gather(half_sel, ('aux', 'pair'), axis=0, tiled=True)  40.3 us
    all_gather x1, waiting for transfers between devices, on_device(): stage1 = lax.all_gather(piece, 'pair', axis=0)  35.3 us
    unnamed x21, local copies, waits for them, and re-layouts  22.4 us
    all_gather x1, blocking collectives, on_device(): sel_full = lax.all_gather(sel_own, 'pair', axis=3, tiled=True)  18.8 us
    another operation x2, local copies, waits for them, and re-layouts, complex_rows(): return jnp.stack([c0, c1], -3)  13.2 us
    dot_general x1, matrix products, on_device(): jnp.einsum('mk,bkn->mbn', lhs, v_full, preferred_element_type=jnp.float32)  12.3 us
    reshape x1, local copies, waits for them, and re-layouts, on_device(): lhs = complex_rows(half).reshape(vectors * occupied * 2, rows)  10.2 us
    another operation x4, other arithmetic, complex_rows(): return jnp.stack([c0, c1], -3)  7.01 us
  transfers between devices with their start and end apart: 2, of which 1 were waited for; matrix products, arithmetic and copies ran while one was open for 38% of the time, Pallas kernels for 0%

profile of v1, /device:TPU:0, one launch (start us, length us, event | category | flops | bytes accessed | tf_op | source)
XLA Modules:
  0.0 213.7 jit_solution(11137517444144872280)
XLA Ops:
  7.2 0.0 copy-start
  7.2 0.0 copy-start.7
  7.2 0.0 all-gather.5.cloned.1.call-start
  7.2 1.6 copy-done
  8.9 0.8 constant_dynamic-slice_fusion
  9.6 0.0 all-gather.5.cloned.1.call-update
  9.7 0.0 all-gather.7.cloned.1.call-start
  9.7 35.3 %all-gather.5.cloned.1.call-done = bf16[1664,384]{1,0:T(8,128)(2,1)} async-done(((bf16[416,384]{1,0:T(8,128)(2,1)}), bf16[1664,384]{1,0:T(8,128)(2,1)}) %all-gather.5.cloned.1.call-update) | async-done | bytes 1277968 | tf_op jit(solution)/shard_map/all_gather | solution.py:51
  45.0 0.0 all-gather.7.cloned.1.call-update
  45.1 0.0 copy-done.7
  45.1 0.0 copy-start.9
  45.1 0.1 slice_bitcast_fusion
  45.2 0.0 copy-start.3
  45.2 0.8 copy-done.3
  46.0 0.1 copy-done.5
  46.1 1.0 pad_maximum_fusion.2
  47.1 2.0 copy.18
  49.0 0.0 copy-done.9
  49.1 0.6 gather_fusion
  49.7 0.6 gather_fusion.1
  50.3 3.2 %fusion.10 = bf16[3,3,4,832]{3,2,0,1:T(4,128)(2,1)S(1)} fusion(bf16[3,832,832]{2,1,0:T(8,128)(2,1)} %param.6, bf16[3,4,832]{2,1,0:T(4,128)(2,1)S(1)} %gather_fusion, pred[3]{0:T(512)(128)(4,1)S(1)} %get-tuple-element.7), kind=kOutput, calls=%fused_computation.17 | convolution fusion | flops 49880064 | bytes 4233219 | tf_op jit(solution)/shard_map/kmi,pmn->pikn/dot_general | solution.py:37
  53.5 40.3 %all_gather.22 = bf16[48,3,4,832]{3,2,0,1:T(4,128)(2,1)S(1)} all-gather(bf16[3,3,4,832]{3,2,0,1:T(4,128)(2,1)S(1)} %fusion.10), channel_id=1, replica_groups=mesh['parts'=2,'aux'=4,'pair'=4] {'aux','pair'}, dimensions={0}, use_global_device_ids=true | all-gather | bytes 1018368 | tf_op jit(solution)/shard_map/all_gather | solution.py:40
  93.8 1.3 slice_negate_fusion.1
  95.0 2.2 %maximum_bitcast_fusion.2 = (bf16[48,3,1,4,832]{4,3,0,1,2:T(4,128)(2,1)S(1)}, bf16[48,3,1,4,832]{4,3,0,1,2:T(4,128)(2,1)S(1)}) fusion(bf16[48,3,2,832]{3,2,0,1:T(2,128)(2,1)S(1)} %get-tuple-element.13, bf16[48,3,2,832]{3,2,0,1:T(2,128)(2,1)S(1)} %get-tuple-element.15, bf16[48,3,2,832]{3,2,0,1:T(2,128)(2,1)S(1)} %get-tuple-element.14), kind=kLoop, calls=%fused_computation.18 | loop fusion | flops 3833856 | bytes 3354624 | tf_op jit(solution)/shard_map/stack | solution.py:11
  97.2 1.5 pad_maximum_fusion.1
  98.8 2.0 copy.19
  100.8 4.6 %reshape.87 = bf16[288,3328]{1,0:T(8,128)(2,1)} reshape(bf16[48,3,2,4,832]{4,3,2,1,0:T(4,128)(2,1)} %copy.19) | data formatting | bytes 3833856 | tf_op jit(solution)/shard_map/reshape | solution.py:43
  105.4 2.7 %convolution_convert_fusion.1 = bf16[288,384]{1,0:T(8,128)(2,1)S(1)} fusion(bf16[288,3328]{1,0:T(8,128)(2,1)} %reshape.87, bf16[3328,384]{1,0:T(8,128)(2,1)S(1)} %bitcast.77), kind=kOutput, calls=%fused_computation.15 | convolution fusion | flops 736210944 | bytes 4694016 | tf_op jit(solution)/shard_map/dot_general | solution.py:44
  108.1 0.1 reshape.88
  108.2 0.1 fusion.26
  108.3 18.8 %all_gather.23 = bf16[48,3,2,1536]{3,0,1,2:T(8,128)(2,1)S(1)} all-gather(bf16[48,3,2,384]{3,0,1,2:T(8,128)(2,1)S(1)} %copy.20), channel_id=1, replica_groups=mesh['parts'=2,'aux'=4,'pair'=4] {'pair'}, dimensions={3}, use_global_device_ids=true | all-gather | bytes 1105920 | tf_op jit(solution)/shard_map/all_gather | solution.py:65
  127.2 0.1 broadcast_add_fusion
  127.3 0.1 broadcast_subtract_fusion.1
  127.4 0.5 broadcast_subtract_fusion
  127.9 1.6 fusion.14
  129.5 4.7 %fusion = f32[384,2,3,3,384]{0,4,2,3,1:T(8,128)} fusion(f32[2,3,384,3,384]{4,2,3,1,0:T(8,128)S(1)} %fusion.14, f32[384,3,3,384]{0,3,1,2:T(8,128)S(1)} %broadcast_subtract_fusion), kind=kLoop, calls=%fused_computation.3 | loop fusion | flops 5308416 | bytes 26542080 | tf_op jit(solution)/shard_map/div | solution.py:77
  134.2 19.8 %copy.24 = f32[384,2,3,3,384]{4,1,3,2,0:T(2,128)} copy(f32[384,2,3,3,384]{0,4,2,3,1:T(8,128)} %fusion) | data formatting | bytes 21233664
  154.0 6.4 %convert_bitcast_fusion = bf16[3,128,4,832]{1,3,0,2:T(8,128)(2,1)S(1)} fusion(bf16[3,832,832]{2,1,0:T(8,128)(2,1)} %param.6, bf16[2,832,128]{2,1,0:T(8,128)(2,1)S(1)} %copy-done.6, bf16[2,832,128]{2,1,0:T(8,128)(2,1)S(1)} %copy-done.4), kind=kOutput, calls=%fused_computation.12 | convolution fusion | flops 2129494016 | bytes 7561216 | tf_op jit(solution)/shard_map/kmj,pmn->pjkn/dot_general | solution.py:55
  160.4 0.3 slice_negate_fusion
  160.7 0.5 maximum_bitcast_fusion
  161.2 2.8 %pad_maximum_fusion = bf16[3,128,2,4,832]{1,4,0,3,2:T(8,128)(2,1)} fusion(bf16[3,128,1,4,832]{1,4,0,3,2:T(8,128)(2,1)S(1)} %get-tuple-element.12, bf16[3,128,1,4,832]{1,4,0,3,2:T(8,128)(2,1)S(1)} %get-tuple-element.11), kind=kLoop, calls=%fused_computation.4 | loop fusion | flops 2555904 | bytes 10223616 | tf_op jit(solution)/shard_map/stack | solution.py:11
  164.0 11.2 %copy.16 = bf16[3,128,2,4,832]{4,3,2,1,0:T(4,128)(2,1)} copy(bf16[3,128,2,4,832]{1,4,0,3,2:T(8,128)(2,1)} %pad_maximum_fusion) | data formatting | bytes 10223616 | tf_op jit(solution)/shard_map/stack | solution.py:11
  175.2 10.2 %reshape.112 = bf16[768,3328,1]{1,0,2:T(8,128)(2,1)} reshape(bf16[3,128,2,4,832]{4,3,2,1,0:T(4,128)(2,1)} %copy.16) | data formatting | bytes 10223616 | tf_op jit(solution)/shard_map/reshape | solution.py:58
  185.4 12.3 %convolution_convert_fusion = bf16[768,4,384]{2,0,1:T(8,128)(2,1)S(1)} fusion(bf16[768,3328,1]{1,0,2:T(8,128)(2,1)} %reshape.112, bf16[4,3328,384]{2,1,0:T(8,128)(2,1)} %all-gather.7.cloned.1.call-done), kind=kOutput, calls=%fused_computation.14 | convolution fusion | flops 7852916736 | bytes 17694720 | tf_op jit(solution)/shard_map/mk,bkn->mbn/dot_general | solution.py:59
  197.7 0.0 copy-start.1
  197.7 3.3 %copy.17 = bf16[768,4,384]{2,1,0:T(4,128)(2,1)} copy(bf16[768,4,384]{2,0,1:T(8,128)(2,1)S(1)} %convolution_convert_fusion) | data formatting | bytes 4718592 | tf_op jit(solution)/shard_map/convert_element_type | solution.py:60
  200.9 5.9 %reshape.86 = bf16[3,128,2,1536]{3,2,1,0:T(2,128)(2,1)} reshape(bf16[768,4,384]{2,1,0:T(4,128)(2,1)} %copy.17) | data formatting | bytes 4718592 | tf_op jit(solution)/shard_map/reshape | solution.py:60
  206.8 0.0 copy-done.1
  (18 shorter events, 0.2 us)
Async XLA Ops:
  7.2 1.7 copy-start
  7.2 37.9 %copy-start.7 = (bf16[2,2,832,128]{3,2,1,0:T(8,128)(2,1)S(1)}, bf16[2,2,832,128]{3,2,1,0:T(8,128)(2,1)}, u32[]{:S(2)}) copy-start(bf16[2,2,832,128]{3,2,1,0:T(8,128)(2,1)} %param.7) | copy-start | bytes 2555908
  7.2 37.8 %all-gather.5.cloned.1.call-start = ((), (), s32[]{:S(2)}) async-start(), calls=%async_computation | async-start | bytes 1597440 | tf_op jit(solution)/shard_map/all_gather | solution.py:51
  9.7 175.7 %all-gather.7.cloned.1.call-start = ((), (), s32[]{:S(2)}) async-start(), calls=%async_computation.1 | async-start | bytes 11501568 | tf_op jit(solution)/shard_map/all_gather | solution.py:52
  45.1 4.0 %copy-start.9 = (s32[3]{0:T(128)S(1)}, s32[3]{0:T(128)}, u32[]{:S(2)}) copy-start(s32[3]{0:T(128)} %param.11) | copy-start | bytes 40
  45.2 0.8 copy-start.3
  45.2 0.9 copy-start.5
  46.1 3.6 %copy-start.2 = (f32[128]{0:T(128)S(1)}, f32[128]{0:T(128)}, u32[]{:S(2)}) copy-start(f32[128]{0:T(128)} %param.9) | copy-start | bytes 1540
  105.4 2.8 %copy-start.8 = (f32[1536]{0:T(1024)S(1)}, f32[1536]{0:T(1024)}, u32[]{:S(2)}) copy-start(f32[1536]{0:T(1024)} %param.10) | copy-start | bytes 18436
  134.2 19.8 %copy-start.4 = (bf16[2,832,128]{2,1,0:T(8,128)(2,1)S(1)}, bf16[2,832,128]{2,1,0:T(8,128)(2,1)}, u32[]{:S(2)}) copy-start(bf16[2,832,128]{2,1,0:T(8,128)(2,1)} %copy-done.3) | copy-start | bytes 1277956
  134.2 19.8 %copy-start.6 = (bf16[2,832,128]{2,1,0:T(8,128)(2,1)S(1)}, bf16[2,832,128]{2,1,0:T(8,128)(2,1)}, u32[]{:S(2)}) copy-start(bf16[2,832,128]{2,1,0:T(8,128)(2,1)} %copy-done.5) | copy-start | bytes 1277956
  197.7 9.2 %copy-start.1 = (bf16[2,2,832,384]{3,2,1,0:T(8,128)(2,1)S(1)}, bf16[2,2,832,384]{3,2,1,0:T(8,128)(2,1)}, u32[]{:S(2)}) copy-start(bf16[2,2,832,384]{3,2,1,0:T(8,128)(2,1)} %param.8) | copy-start | bytes 7667716
Sparse Core Ops, SparseCore 0:
  10.2 34.8 all-gather.4
  46.9 64.6 all-gather.6

commit v2 on v1

v2 whole, which is shorter than its diff:
```python
import functools

import jax
import jax.numpy as jnp
from jax import lax
from jax.experimental import pallas as pl
from jax.experimental.pallas import tpu as pltpu
from jax.sharding import PartitionSpec as P


def transform_kernel(orbitals, h_ref, v_ref, o_ref):
    real = None
    imag = None
    for s in range(2):
        hr = h_ref[0, s]
        hi = h_ref[0, 2 + s]
        vr = v_ref[0, s * orbitals:(s + 1) * orbitals, :]
        vi = v_ref[0, (2 + s) * orbitals:(3 + s) * orbitals, :]
        rr = jnp.dot(hr, vr, preferred_element_type=jnp.float32)
        ii = jnp.dot(hi, vi, preferred_element_type=jnp.float32)
        ri = jnp.dot(hr, vi, preferred_element_type=jnp.float32)
        ir = jnp.dot(hi, vr, preferred_element_type=jnp.float32)
        real = rr - ii if real is None else real + rr - ii
        imag = ri + ir if imag is None else imag + ri + ir
    o_ref[0, 0] = real.astype(o_ref.dtype)
    o_ref[0, 1] = imag.astype(o_ref.dtype)


def transform(half, v_blocks):
    pn, _, m, n = half.shape
    b, rows, w = v_blocks.shape
    if w % 128 != 0:
        v = v_blocks.reshape(b, 2, 2, n, w)
        hr, hi = half[:, :2], half[:, 2:]
        dims = "pskn,bsnw->pkbw"
        real = jnp.einsum(dims, hr, v[:, 0], preferred_element_type=jnp.float32) - jnp.einsum(
            dims, hi, v[:, 1], preferred_element_type=jnp.float32)
        imag = jnp.einsum(dims, hr, v[:, 1], preferred_element_type=jnp.float32) + jnp.einsum(
            dims, hi, v[:, 0], preferred_element_type=jnp.float32)
        out = jnp.stack([real, imag], 1).astype(jnp.bfloat16)
        return out.reshape(pn, 2, m, b * w)
    flops = 16 * pn * m * n * w * b
    bytes_accessed = 2 * (half.size * b + v_blocks.size + pn * 2 * m * b * w)
    return pl.pallas_call(
        functools.partial(transform_kernel, n),
        grid=(b, pn),
        in_specs=[
            pl.BlockSpec((1, 4, m, n), lambda i, p: (p, 0, 0, 0)),
            pl.BlockSpec((1, rows, w), lambda i, p: (i, 0, 0)),
        ],
        out_specs=pl.BlockSpec((1, 2, m, w), lambda i, p: (p, 0, 0, i)),
        out_shape=jax.ShapeDtypeStruct((pn, 2, m, b * w), jnp.bfloat16),
        cost_estimate=pl.CostEstimate(flops=flops, bytes_accessed=bytes_accessed, transcendentals=0),
    )(half, v_blocks)


def on_device(cholesky, occ_coef, vir_coef, occ_energy, vir_energy, batch_occ):
    vectors = cholesky.shape[0]
    orbitals = cholesky.shape[1]
    occupied = occ_coef.shape[3]
    a_width = vir_coef.shape[3]
    n_pair = lax.axis_size("pair")
    n_aux = lax.axis_size("aux")
    n_parts = lax.axis_size("parts")
    rows = 4 * orbitals
    virtuals = n_pair * a_width
    b_width = virtuals // n_aux
    per_b = b_width // a_width
    batch = batch_occ.shape[0]

    occ_left = jnp.concatenate([occ_coef[0], -occ_coef[1]], 0)
    v_local = vir_coef.reshape(rows, a_width)

    occ_sel = jnp.take(occ_left, batch_occ, axis=2)
    half_sel = jnp.einsum(
        "kmi,pmn->pikn", occ_sel, cholesky, preferred_element_type=jnp.float32
    ).astype(jnp.bfloat16)
    half_sel = half_sel.reshape(vectors * batch * 4, orbitals)
    gathered = lax.all_gather(half_sel, ("aux", "pair"), axis=0)
    count = gathered.shape[0] * vectors
    half_rows = gathered.reshape(count * batch, 4, orbitals).transpose(1, 0, 2)
    sel_own = transform(half_rows[None], v_local[None])
    sel_own = sel_own.reshape(2, count, batch, a_width)

    n_q = n_parts * n_aux
    rows_q = rows // n_q
    q = lax.axis_index("parts") * n_aux + lax.axis_index("aux")
    piece = lax.dynamic_slice_in_dim(v_local, q * rows_q, rows_q, 0)
    stage1 = lax.all_gather(piece, "pair", axis=0)
    stage2 = lax.all_gather(stage1, ("parts", "aux"), axis=1)
    v_full = stage2.reshape(n_pair, rows, a_width)

    half = jnp.einsum(
        "kmj,pmn->pkjn", occ_left, cholesky, preferred_element_type=jnp.float32
    ).astype(jnp.bfloat16)
    full = transform(half, v_full)
    pair_vectors = full.transpose(0, 2, 1, 3)

    sel_all = lax.all_gather(sel_own, "pair", axis=0)
    sel_b = lax.dynamic_slice_in_dim(sel_all, lax.axis_index("aux") * per_b, per_b, 0)
    sel_b = sel_b.transpose(1, 2, 3, 0, 4).reshape(2 * count, batch, b_width)
    left = sel_b.reshape(2 * count * batch, b_width)
    real_right = jnp.concatenate([sel_own[0], -sel_own[1]], 0)
    imag_right = jnp.concatenate([sel_own[1], sel_own[0]], 0)
    right = jnp.stack([real_right, imag_right], 2)
    eye = jnp.arange(batch)[:, None] == jnp.arange(batch)[None, :]
    first = jnp.where(eye[None, :, None, :, None, None], right[:, None, :, None, :, :], 0)
    second = jnp.where(eye[None, :, :, None, None, None], right[:, None, None, :, :, :], 0)
    stacked = (first - second).reshape(2 * count * batch, batch * batch * 2 * a_width)
    paired = lax.dot_general(
        left, stacked, (((0,), (0,)), ((), ())), preferred_element_type=jnp.float32
    ).reshape(b_width, batch, batch, 2, a_width)

    a_start = lax.axis_index("pair") * a_width
    b_start = lax.axis_index("aux") * b_width
    occ_e = jnp.take(occ_energy, batch_occ)
    vir_first = lax.dynamic_slice_in_dim(vir_energy, a_start, a_width)
    vir_second = lax.dynamic_slice_in_dim(vir_energy, b_start, b_width)
    denominator = (
        (occ_e[:, None] + occ_e[None, :])[None, :, :, None, None]
        - vir_first[None, None, None, None, :]
        - vir_second[:, None, None, None, None]
    )
    amplitudes = (paired / denominator).transpose(0, 3, 1, 2, 4)
    return (pair_vectors, amplitudes)


def solution(mesh):
    return jax.shard_map(
        on_device,
        mesh=mesh,
        in_specs=(
            P(("parts", "aux", "pair"), None, None),
            P(),
            P(None, None, None, "pair"),
            P(),
            P(),
            P(),
        ),
        out_specs=(
            P(("parts", "aux", "pair"), None, None, None),
            P(("parts", "aux"), None, None, None, "pair"),
        ),
        check_vma=False,
    )
```

time: 215 us -> 207 us (0.963)
  the two profiles are of different devices: /device:TPU:0 before, /device:TPU:29 now
where the time goes in v2:
time: 207 us; the launch traced here: 203 us
  blocking collectives  60.5 us (29%)
  local copies, waits for them, and re-layouts  51.4 us (25%)
  waiting for transfers between devices  32.5 us (16%)
  Pallas kernels  24.4 us (12%)
  between operations  14.3 us (7%)
  matrix products  11.4 us (6%)
  other arithmetic  8.95 us (4%)
    all_gather x1, blocking collectives, on_device(): gathered = lax.all_gather(half_sel, ('aux', 'pair'), axis=0)  41.8 us
    all_gather x1, waiting for transfers between devices, on_device(): stage1 = lax.all_gather(piece, 'pair', axis=0)  32.5 us
    pallas_call x2, Pallas kernels, transform(): pl.pallas_call(functools.partial(transform_kernel, n), grid=(b, pn), in_s...  24.4 us
    unnamed x16, local copies, waits for them, and re-layouts  20.8 us
    all_gather x1, blocking collectives, on_device(): sel_all = lax.all_gather(sel_own, 'pair', axis=0)  18.7 us
    sub x1, local copies, waits for them, and re-layouts, on_device(): first - second  9.56 us
    dot_general x1, local copies, waits for them, and re-layouts, on_device(): lax.dot_general(left, stacked, (((0,), (0,)), ((), ())), preferred_elemen...  8.45 us
    sub x1, other arithmetic, on_device(): first - second  6.12 us
  transfers between devices with their start and end apart: 2, of which 1 were waited for; matrix products, arithmetic and copies ran while one was open for 31% of the time, Pallas kernels for 2%

profile of v2, /device:TPU:29, one launch (start us, length us, event | category | flops | bytes accessed | tf_op | source)
XLA Modules:
  0.0 203.5 jit_solution(1392948955267764010)
XLA Ops:
  7.2 0.0 copy-start
  7.2 0.0 copy-start.6
  7.2 0.0 all-gather.5.cloned.1.call-start
  7.2 1.7 constant_dynamic-slice_fusion.1
  9.0 0.0 all-gather.5.cloned.1.call-update
  9.0 0.0 all-gather.7.cloned.1.call-start
  9.0 32.5 %all-gather.5.cloned.1.call-done = bf16[1664,384]{1,0:T(8,128)(2,1)} async-done(((bf16[416,384]{1,0:T(8,128)(2,1)}), bf16[1664,384]{1,0:T(8,128)(2,1)}) %all-gather.5.cloned.1.call-update) | async-done | bytes 1277968 | tf_op jit(solution)/shard_map/all_gather | solution.py:89
  41.5 0.0 all-gather.7.cloned.1.call-update
  41.6 1.2 slice_bitcast_fusion
  42.8 0.0 copy-start.3
  42.8 0.7 copy-done.3
  43.5 0.1 pad_maximum_fusion
  43.6 1.2 copy.42
  44.8 0.0 copy-done.6
  44.9 0.6 gather_fusion.1
  45.5 0.6 gather_fusion
  46.1 3.0 %fusion.15 = bf16[3,3,4,832]{3,2,0,1:T(4,128)(2,1)S(1)} fusion(bf16[3,832,832]{2,1,0:T(8,128)(2,1)} %param.6, bf16[3,4,832]{2,1,0:T(4,128)(2,1)S(1)} %gather_fusion, pred[3]{0:T(512)(128)(4,1)S(1)} %get-tuple-element.11), kind=kOutput, calls=%fused_computation.15 | convolution fusion | flops 49880064 | bytes 4233219 | tf_op jit(solution)/shard_map/kmi,pmn->pikn/dot_general | solution.py:75
  49.2 41.8 %all_gather.22 = bf16[16,36,832]{2,1,0:T(8,128)(2,1)S(1)} all-gather(bf16[1,36,832]{2,1,0:T(8,128)(2,1)S(1)} %all_gather_reshape.6), channel_id=1, replica_groups=mesh['parts'=2,'aux'=4,'pair'=4] {'aux','pair'}, dimensions={0}, use_global_device_ids=true | all-gather | bytes 1018368 | tf_op jit(solution)/shard_map/all_gather | solution.py:79
  91.0 0.5 reshape.121
  91.5 1.1 copy.63
  92.6 4.1 %shard_map.78 = bf16[1,2,144,384]{3,2,1,0:T(8,128)(2,1)} custom-call(bf16[1,4,144,832]{3,2,1,0:T(8,128)(2,1)} %bitcast.58, bf16[1,3328,384]{2,1,0:T(8,128)(2,1)} %bitcast.60), custom_call_target="tpu_custom_call" | custom-call | flops 736100352 | bytes 3735552 | tf_op jit(solution)/shard_map/pallas_call | solution.py:44
  96.7 1.1 copy.45
  97.8 1.0 fusion.25
  98.8 0.1 squeeze.14
  98.9 0.1 neg.11
  98.9 0.1 squeeze.13
  99.0 0.4 maximum_bitcast_fusion
  99.4 0.4 pad_maximum_fusion.1
  99.8 0.6 copy.48
  100.5 18.7 %all_gather.23 = bf16[4,2,48,3,384]{4,2,3,1,0:T(8,128)(2,1)S(1)} all-gather(bf16[1,2,48,3,384]{4,2,3,1,0:T(8,128)(2,1)S(1)} %copy.46), channel_id=1, replica_groups=mesh['parts'=2,'aux'=4,'pair'=4] {'pair'}, dimensions={0}, use_global_device_ids=true | all-gather | bytes 1105920 | tf_op jit(solution)/shard_map/all_gather | solution.py:99
  119.2 0.1 copy.47
  119.3 0.9 reshape.147
  120.2 5.3 %fusion.9 = bf16[4,128,3,832]{1,3,2,0:T(8,128)(2,1)S(1)} fusion(bf16[3,832,832]{2,1,0:T(8,128)(2,1)} %param.6, bf16[2,832,128]{2,1,0:T(8,128)(2,1)} %copy-done.3, bf16[2,832,128]{2,1,0:T(8,128)(2,1)S(1)} %get-tuple-element.12), kind=kOutput, calls=%fused_computation.13 | convolution fusion | flops 2129494016 | bytes 7561216 | tf_op jit(solution)/shard_map/kmj,pmn->pkjn/dot_general | solution.py:93
  125.5 2.9 %copy.41 = bf16[4,128,3,832]{3,1,0,2:T(8,128)(2,1)} copy(bf16[4,128,3,832]{1,3,2,0:T(8,128)(2,1)S(1)} %fusion.9) | data formatting | bytes 5111808 | tf_op jit(solution)/shard_map/convert_element_type | solution.py:95
  128.4 6.1 %fusion.4 = bf16[96,3,3,3,2,384]{5,4,3,2,1,0:T(2,128)(2,1)} fusion(pred[3,3]{1,0:T(4,128)(4,1)S(1)} %iota_compare_fusion, bf16[96,3,2,384]{3,2,1,0:T(2,128)(2,1)S(1)} %copy.48), kind=kLoop, calls=%fused_computation.9 | loop fusion | flops 5971968 | bytes 4423689 | tf_op jit(solution)/shard_map/sub | solution.py:109
  134.5 9.6 %sub.44 = bf16[288,6912]{1,0:T(8,128)(2,1)} reshape(bf16[96,3,3,3,2,384]{5,4,3,2,1,0:T(2,128)(2,1)} %fusion.4) | data formatting | bytes 7962624 | tf_op jit(solution)/shard_map/sub | solution.py:109
  144.1 8.5 %dot_general.16 = bf16[3,3,2,384,288]{3,2,1,0,4:T(2,128)(2,1)} reshape(bf16[6912,288]{0,1:T(8,128)(2,1)} %bitcast.57) | data formatting | bytes 7962624 | tf_op jit(solution)/shard_map/dot_general | solution.py:110
  152.6 0.1 fusion.26
  152.6 0.1 broadcast_add_fusion
  152.7 0.1 broadcast_subtract_fusion.1
  152.8 0.5 broadcast_subtract_fusion
  153.3 0.2 copy-done.4
  153.5 1.3 copy-done.2
  154.8 3.0 %divide_bitcast_fusion = f32[384,2,3,3,384]{4,0,1,3,2:T(8,128)S(1)} fusion(f32[384,3,3,384]{3,0,2,1:T(8,128)S(1)} %broadcast_subtract_fusion, bf16[3,3,2,384,288]{3,2,1,0,4:T(2,128)(2,1)S(1)} %copy-done.2, bf16[288,384,1,1,1]{1,0,2,3,4:T(8,128)(2,1)S(1)} %copy-done.4), kind=kOutput, calls=%fused_computation.2 | convolution fusion | flops 1531478016 | bytes 20127744 | tf_op jit(solution)/shard_map/dot_general | solution.py:110
  157.9 13.0 %copy.52 = f32[384,2,3,3,384]{4,1,3,2,0:T(2,128)} copy(f32[384,2,3,3,384]{4,0,1,3,2:T(8,128)S(1)} %divide_bitcast_fusion) | data formatting | bytes 21233664
  170.9 20.3 %shard_map.77 = bf16[3,2,128,1536]{3,2,1,0:T(8,128)(2,1)} custom-call(bf16[3,4,128,832]{3,2,1,0:T(8,128)(2,1)} %bitcast.61, bf16[4,3328,384]{2,1,0:T(8,128)(2,1)} %all-gather.7.cloned.1.call-done.v_ref), custom_call_target="tpu_custom_call" | custom-call | flops 7851737088 | bytes 22806528 | tf_op jit(solution)/shard_map/pallas_call | solution.py:44
  191.2 5.5 %copy.51 = bf16[3,128,2,1536]{3,2,1,0:T(2,128)(2,1)} copy(bf16[3,128,2,1536]{3,1,2,0:T(8,128)(2,1)} %bitcast.62) | data formatting | bytes 4718592
  196.7 0.0 copy-done.1
  (15 shorter events, 0.2 us)
Async XLA Ops:
  7.2 37.7 %copy-start = (f32[128]{0:T(128)S(1)}, f32[128]{0:T(128)}, u32[]{:S(2)}) copy-start(f32[128]{0:T(128)} %param.9) | copy-start | bytes 1540
  7.2 37.6 %copy-start.6 = (s32[3]{0:T(128)S(1)}, s32[3]{0:T(128)}, u32[]{:S(2)}) copy-start(s32[3]{0:T(128)} %param.11) | copy-start | bytes 40
  7.2 34.3 %all-gather.5.cloned.1.call-start = ((), (), s32[]{:S(2)}) async-start(), calls=%async_computation | async-start | bytes 1597440 | tf_op jit(solution)/shard_map/all_gather | solution.py:89
  9.0 161.9 %all-gather.7.cloned.1.call-start = ((), (), s32[]{:S(2)}) async-start(), calls=%async_computation.1 | async-start | bytes 11501568 | tf_op jit(solution)/shard_map/all_gather | solution.py:90
  42.8 0.8 copy-start.3
  144.1 8.5 %copy-start.5 = (f32[1536]{0:T(1024)S(1)}, f32[1536]{0:T(1024)}, u32[]{:S(2)}) copy-start(f32[1536]{0:T(1024)} %param.10) | copy-start | bytes 18436
  152.5 0.9 copy-start.4
  152.5 2.3 %copy-start.2 = (bf16[3,3,2,384,288]{3,2,1,0,4:T(2,128)(2,1)S(1)}, bf16[3,3,2,384,288]{3,2,1,0,4:T(2,128)(2,1)}, u32[]{:S(2)}) copy-start(bf16[3,3,2,384,288]{3,2,1,0,4:T(2,128)(2,1)} %dot_general.16) | copy-start | bytes 11943940
  170.9 25.8 %copy-start.1 = (f32[128]{0:T(128)S(1)}, f32[128]{0:T(128)}, u32[]{:S(2)}) copy-start(f32[128]{0:T(128)} %param.9) | copy-start | bytes 1540
Sparse Core Ops, SparseCore 0:
  10.2 31.3 all-gather.4
  43.4 66.8 all-gather.6

commit v3 on v2

--- a/solution.py
+++ b/solution.py
@@ -9,11 +9,12 @@
 
 
 def transform_kernel(orbitals, h_ref, v_ref, o_ref):
+    pn, _, m, n = h_ref.shape
     real = None
     imag = None
     for s in range(2):
-        hr = h_ref[0, s]
-        hi = h_ref[0, 2 + s]
+        hr = h_ref[:, s].reshape(pn * m, n)
+        hi = h_ref[:, 2 + s].reshape(pn * m, n)
         vr = v_ref[0, s * orbitals:(s + 1) * orbitals, :]
         vi = v_ref[0, (2 + s) * orbitals:(3 + s) * orbitals, :]
         rr = jnp.dot(hr, vr, preferred_element_type=jnp.float32)
@@ -22,8 +23,9 @@
         ir = jnp.dot(hi, vr, preferred_element_type=jnp.float32)
         real = rr - ii if real is None else real + rr - ii
         imag = ri + ir if imag is None else imag + ri + ir
-    o_ref[0, 0] = real.astype(o_ref.dtype)
-    o_ref[0, 1] = imag.astype(o_ref.dtype)
+    w = real.shape[1]
+    o_ref[:, 0] = real.reshape(pn, m, w).astype(o_ref.dtype)
+    o_ref[:, 1] = imag.reshape(pn, m, w).astype(o_ref.dtype)
 
 
 def transform(half, v_blocks):
@@ -40,18 +42,43 @@
         out = jnp.stack([real, imag], 1).astype(jnp.bfloat16)
         return out.reshape(pn, 2, m, b * w)
     flops = 16 * pn * m * n * w * b
-    bytes_accessed = 2 * (half.size * b + v_blocks.size + pn * 2 * m * b * w)
+    bytes_accessed = 2 * (half.size + v_blocks.size + pn * 2 * m * b * w)
     return pl.pallas_call(
         functools.partial(transform_kernel, n),
-        grid=(b, pn),
+        grid=(b,),
         in_specs=[
-            pl.BlockSpec((1, 4, m, n), lambda i, p: (p, 0, 0, 0)),
-            pl.BlockSpec((1, rows, w), lambda i, p: (i, 0, 0)),
+            pl.BlockSpec((pn, 4, m, n), lambda i: (0, 0, 0, 0)),
+            pl.BlockSpec((1, rows, w), lambda i: (i, 0, 0)),
         ],
-        out_specs=pl.BlockSpec((1, 2, m, w), lambda i, p: (p, 0, 0, i)),
+        out_specs=pl.BlockSpec((pn, 2, m, w), lambda i: (0, 0, 0, i)),
         out_shape=jax.ShapeDtypeStruct((pn, 2, m, b * w), jnp.bfloat16),
         cost_estimate=pl.CostEstimate(flops=flops, bytes_accessed=bytes_accessed, transcendentals=0),
     )(half, v_blocks)
+
+
+def pair_terms(batch_rows, column_rows):
+    left = jnp.concatenate([batch_rows[:, :, 0, :], batch_rows[:, :, 1, :]], 0)
+    real_right = jnp.concatenate([column_rows[:, :, 0, :], -column_rows[:, :, 1, :]], 0)
+    imag_right = jnp.concatenate([column_rows[:, :, 1, :], column_rows[:, :, 0, :]], 0)
+    right = jnp.stack([real_right, imag_right], 1)
+    return jnp.einsum("pjb,pcia->bcija", left, right, preferred_element_type=jnp.float32)
+
+
+def gather_group(x, axes, sizes):
+    n = 1
+    for size in sizes:
+        n *= size
+    if n > 16:
+        return lax.all_gather(x, axes, axis=0)
+    me = lax.axis_index(axes[0])
+    for name, size in zip(axes[1:], sizes[1:]):
+        me = me * size + lax.axis_index(name)
+    blocks = [x]
+    for shift in range(1, n):
+        perm = [(i, (i + shift) % n) for i in range(n)]
+        blocks.append(lax.ppermute(x, axes, perm))
+    stacked = jnp.stack(blocks, 0)
+    return jnp.take(stacked, (me - jnp.arange(n)) % n, axis=0)
 
 
 def on_device(cholesky, occ_coef, vir_coef, occ_energy, vir_energy, batch_occ):
@@ -76,7 +103,7 @@
         "kmi,pmn->pikn", occ_sel, cholesky, preferred_element_type=jnp.float32
     ).astype(jnp.bfloat16)
     half_sel = half_sel.reshape(vectors * batch * 4, orbitals)
-    gathered = lax.all_gather(half_sel, ("aux", "pair"), axis=0)
+    gathered = gather_group(half_sel, ("aux", "pair"), (n_aux, n_pair))
     count = gathered.shape[0] * vectors
     half_rows = gathered.reshape(count * batch, 4, orbitals).transpose(1, 0, 2)
     sel_own = transform(half_rows[None], v_local[None])
@@ -87,29 +114,25 @@
     q = lax.axis_index("parts") * n_aux + lax.axis_index("aux")
     piece = lax.dynamic_slice_in_dim(v_local, q * rows_q, rows_q, 0)
     stage1 = lax.all_gather(piece, "pair", axis=0)
-    stage2 = lax.all_gather(stage1, ("parts", "aux"), axis=1)
-    v_full = stage2.reshape(n_pair, rows, a_width)
-
     half = jnp.einsum(
         "kmj,pmn->pkjn", occ_left, cholesky, preferred_element_type=jnp.float32
     ).astype(jnp.bfloat16)
+    stage1, half = lax.optimization_barrier((stage1, half))
+    stage2 = lax.all_gather(stage1, ("parts", "aux"), axis=1)
+    v_full = stage2.reshape(n_pair, rows, a_width)
     full = transform(half, v_full)
     pair_vectors = full.transpose(0, 2, 1, 3)
 
-    sel_all = lax.all_gather(sel_own, "pair", axis=0)
-    sel_b = lax.dynamic_slice_in_dim(sel_all, lax.axis_index("aux") * per_b, per_b, 0)
-    sel_b = sel_b.transpose(1, 2, 3, 0, 4).reshape(2 * count, batch, b_width)
-    left = sel_b.reshape(2 * count * batch, b_width)
-    real_right = jnp.concatenate([sel_own[0], -sel_own[1]], 0)
-    imag_right = jnp.concatenate([sel_own[1], sel_own[0]], 0)
-    right = jnp.stack([real_right, imag_right], 2)
-    eye = jnp.arange(batch)[:, None] == jnp.arange(batch)[None, :]
-    first = jnp.where(eye[None, :, None, :, None, None], right[:, None, :, None, :, :], 0)
-    second = jnp.where(eye[None, :, :, None, None, None], right[:, None, None, :, :, :], 0)
-    stacked = (first - second).reshape(2 * count * batch, batch * batch * 2 * a_width)
-    paired = lax.dot_general(
-        left, stacked, (((0,), (0,)), ((), ())), preferred_element_type=jnp.float32
-    ).reshape(b_width, batch, batch, 2, a_width)
+    sel_a = sel_own.transpose(1, 2, 0, 3)
+    if n_aux == n_pair:
+        perm = [(a * n_pair + z, z * n_pair + a) for a in range(n_aux) for z in range(n_pair)]
+        sel_b = lax.ppermute(sel_a, ("aux", "pair"), perm)
+    else:
+        sel_all = lax.all_gather(sel_a, "pair", axis=0)
+        sel_b = lax.dynamic_slice_in_dim(sel_all, lax.axis_index("aux") * per_b, per_b, 0)
+        sel_b = sel_b.transpose(1, 2, 3, 0, 4).reshape(count, batch, 2, b_width)
+    coulomb = pair_terms(sel_b, sel_a)
+    paired = coulomb - jnp.swapaxes(coulomb, 2, 3)
 
     a_start = lax.axis_index("pair") * a_width
     b_start = lax.axis_index("aux") * b_width
@@ -117,11 +140,11 @@
     vir_first = lax.dynamic_slice_in_dim(vir_energy, a_start, a_width)
     vir_second = lax.dynamic_slice_in_dim(vir_energy, b_start, b_width)
     denominator = (
-        (occ_e[:, None] + occ_e[None, :])[None, :, :, None, None]
+        (occ_e[:, None] + occ_e[None, :])[None, None, :, :, None]
         - vir_first[None, None, None, None, :]
         - vir_second[:, None, None, None, None]
     )
-    amplitudes = (paired / denominator).transpose(0, 3, 1, 2, 4)
+    amplitudes = paired / denominator
     return (pair_vectors, amplitudes)
 
 

time: 207 us -> 161 us (0.78)
  blocking collectives: 60.5 us -> 0 us
  starting transfers between devices: 0.08 us -> 25.3 us
  local copies, waits for them, and re-layouts: 51.4 us -> 36.2 us
  waiting for transfers between devices: 32.5 us -> 41.5 us
  Pallas kernels: 24.4 us -> 20.5 us
    all_gather x2 -> x0, blocking collectives: 60.5 us -> none  [the longest x1 41.8 us: on_device(): gathered = lax.all_gather(half_sel, ('aux', 'pair'), axis=0)]
    ppermute x0 -> x16, starting transfers between devices: none -> 25.2 us  [the longest x15 23 us: gather_group(): blocks.append(lax.ppermute(x, axes, perm))]
    ppermute x0 -> x16, waiting for transfers between devices: none -> 18.3 us  [the longest x1 11.5 us: on_device(): sel_b = lax.ppermute(sel_a, ('aux', 'pair'), perm)]
    sub x1 -> x0, local copies, waits for them, and re-layouts: 9.56 us -> none  [on_device(): first - second]
    all_gather x1, waiting for transfers between devices: 32.5 us -> 23.1 us  [on_device(): stage1 = lax.all_gather(piece, 'pair', axis=0)]
    dot_general x1 -> x0, local copies, waits for them, and re-layouts: 8.45 us -> none  [on_device(): lax.dot_general(left, stacked, (((0,), (0,)), ((), ())), preferred_elemen...]
    unnamed x16 -> x31, local copies, waits for them, and re-layouts: 20.8 us -> 26.4 us
    div x0 -> x1, other arithmetic: none -> 4.55 us  [on_device(): amplitudes = paired / denominator]
  transfers between devices with their start and end apart: 2 -> 18, of which waited for: 1 -> 6; matrix products, arithmetic and copies ran while one was open for 31% -> 30% of each run, Pallas kernels for 2% -> 3%
where the time goes in v3:
time: 161 us; the launch traced here: 158 us
  waiting for transfers between devices  41.5 us (26%)
  local copies, waits for them, and re-layouts  36.2 us (22%)
  starting transfers between devices  25.3 us (16%)
  Pallas kernels  20.5 us (13%)
  between operations  14.4 us (9%)
  matrix products  11.1 us (7%)
  other arithmetic  9.05 us (6%)
    unnamed x31, local copies, waits for them, and re-layouts  26.4 us
    all_gather x1, waiting for transfers between devices, on_device(): stage1 = lax.all_gather(piece, 'pair', axis=0)  23.1 us
    ppermute x15, starting transfers between devices, gather_group(): blocks.append(lax.ppermute(x, axes, perm))  23 us
    pallas_call x2, Pallas kernels, transform(): pl.pallas_call(functools.partial(transform_kernel, n), grid=(b,), in_spec...  20.5 us
    ppermute x1, waiting for transfers between devices, on_device(): sel_b = lax.ppermute(sel_a, ('aux', 'pair'), perm)  11.5 us
    ppermute x15, waiting for transfers between devices, gather_group(): blocks.append(lax.ppermute(x, axes, perm))  6.89 us
    dot_general x1, matrix products, on_device(): jnp.einsum('kmj,pmn->pkjn', occ_left, cholesky, preferred_element_type=jn...  6.42 us
    div x1, other arithmetic, on_device(): amplitudes = paired / denominator  4.55 us
  transfers between devices with their start and end apart: 18, of which 6 were waited for; matrix products, arithmetic and copies ran while one was open for 30% of the time, Pallas kernels for 3%

profile of v3, /device:TPU:29, one launch (start us, length us, event | category | flops | bytes accessed | tf_op | source)
XLA Modules:
  0.0 158.1 jit_solution(12068321863052093633)
XLA Ops:
  7.2 1.8 %constant_dynamic-slice_fusion = bf16[416,384]{1,0:T(8,128)(2,1)} fusion(bf16[3328,384]{1,0:T(8,128)(2,1)} %bitcast.107, s32[]{:T(128)S(6)} %select_n.67), kind=kLoop, calls=%fused_computation.72 | loop fusion | bytes 638980 | tf_op jit(solution)/shard_map/dynamic_slice | solution.py:115
  9.1 0.1 slice_bitcast_fusion
  9.2 6.4 %fusion.5 = bf16[4,128,3,832]{1,3,2,0:T(8,128)(2,1)S(1)} fusion(bf16[3,832,832]{2,1,0:T(8,128)(2,1)} %param.6, bf16[2,832,128]{2,1,0:T(8,128)(2,1)S(1)} %get-tuple-element.15, bf16[2,832,128]{2,1,0:T(8,128)(2,1)S(1)} %get-tuple-element.14), kind=kOutput, calls=%fused_computation.10 | convolution fusion | flops 2129494016 | bytes 7561216 | tf_op jit(solution)/shard_map/kmj,pmn->pkjn/dot_general | solution.py:117
  15.6 2.7 %copy.27 = bf16[4,128,3,832]{3,1,0,2:T(8,128)(2,1)} copy(bf16[4,128,3,832]{1,3,2,0:T(8,128)(2,1)S(1)} %fusion.5) | data formatting | bytes 5111808 | tf_op jit(solution)/shard_map/convert_element_type | solution.py:119
  18.4 23.1 %all-gather.5.cloned.1.call-done = bf16[1664,384]{1,0:T(8,128)(2,1)} async-done(((bf16[416,384]{1,0:T(8,128)(2,1)}), bf16[1664,384]{1,0:T(8,128)(2,1)}) %all-gather.5.cloned.1.call-update) | async-done | bytes 1277968 | tf_op jit(solution)/shard_map/all_gather | solution.py:116
  41.6 0.1 pad_maximum_fusion
  41.7 1.2 copy.28
  42.9 0.6 gather_fusion
  43.5 0.6 gather_fusion.2
  44.1 3.1 %fusion.11 = bf16[3,3,4,832]{3,2,0,1:T(4,128)(2,1)S(1)} fusion(bf16[3,832,832]{2,1,0:T(8,128)(2,1)} %param.6, bf16[3,4,832]{2,1,0:T(4,128)(2,1)S(1)} %gather_fusion, pred[3]{0:T(512)(128)(4,1)S(1)} %get-tuple-element.13), kind=kOutput, calls=%fused_computation.12 | convolution fusion | flops 49880064 | bytes 4233219 | tf_op jit(solution)/shard_map/kmi,pmn->pikn/dot_general | solution.py:102
  47.3 3.5 %collective-permute-start = (bf16[36,832]{1,0:T(8,128)(2,1)S(1)}, bf16[36,832]{1,0:T(8,128)(2,1)S(1)}, u32[]{:S(2)}, u32[]{:S(2)}) collective-permute-start(bf16[36,832]{1,0:T(8,128)(2,1)S(1)} %reshape.136), channel_id=1, source_target_pairs={{0,1},{1,2},{2,3},{3,4},{4,5},{5,6},{6,7},{7,8},{8,9},{9,10},{10,1... | collective-permute-start | bytes 179720 | tf_op jit(solution)/shard_map/ppermute | solution.py:79
  50.8 0.5 collective-permute-start.1
  51.3 1.1 collective-permute-start.3
  52.4 2.1 %collective-permute-start.4 = (bf16[36,832]{1,0:T(8,128)(2,1)S(1)}, bf16[36,832]{1,0:T(8,128)(2,1)S(1)}, u32[]{:S(2)}, u32[]{:S(2)}) collective-permute-start(bf16[36,832]{1,0:T(8,128)(2,1)S(1)} %reshape.136), channel_id=1, source_target_pairs={{0,5},{1,6},{2,7},{3,8},{4,9},{5,10},{6,11},{7,12},{8,13},{9,14},{... | collective-permute-start | bytes 179720 | tf_op jit(solution)/shard_map/ppermute | solution.py:79
  54.6 0.1 broadcast_in_dim.36
  54.7 0.1 broadcast_in_dim.37
  54.8 0.1 fusion.31
  54.9 0.1 broadcast_add_fusion
  55.0 0.1 broadcast_subtract_fusion.1
  55.1 2.9 %broadcast_subtract_fusion = f32[384,3,3,384]{0,3,1,2:T(8,128)} fusion(f32[384]{0:T(512)S(1)} %get-tuple-element.23, f32[3,3,384]{2,0,1:T(4,128)S(1)} %broadcast_subtract_fusion.1), kind=kLoop, calls=%fused_computation.9 | loop fusion | flops 1327104 | bytes 5323776 | tf_op jit(solution)/shard_map/sub | solution.py:143
  58.0 1.3 collective-permute-start.5
  59.3 0.2 collective-permute-start.6
  59.5 1.3 collective-permute-start.7
  60.8 2.9 %collective-permute-start.8 = (bf16[36,832]{1,0:T(8,128)(2,1)S(1)}, bf16[36,832]{1,0:T(8,128)(2,1)S(1)}, u32[]{:S(2)}, u32[]{:S(2)}) collective-permute-start(bf16[36,832]{1,0:T(8,128)(2,1)S(1)} %reshape.136), channel_id=1, source_target_pairs={{0,9},{1,10},{2,11},{3,12},{4,13},{5,14},{6,15},{7,0},{8,1},{9,2},... | collective-permute-start | bytes 179720 | tf_op jit(solution)/shard_map/ppermute | solution.py:79
  63.6 1.8 %collective-permute-start.9 = (bf16[36,832]{1,0:T(8,128)(2,1)S(1)}, bf16[36,832]{1,0:T(8,128)(2,1)S(1)}, u32[]{:S(2)}, u32[]{:S(2)}) collective-permute-start(bf16[36,832]{1,0:T(8,128)(2,1)S(1)} %reshape.136), channel_id=1, source_target_pairs={{0,10},{1,11},{2,12},{3,13},{4,14},{5,15},{6,0},{7,1},{8,2},{9,3},... | collective-permute-start | bytes 179720 | tf_op jit(solution)/shard_map/ppermute | solution.py:79
  65.5 0.1 collective-permute-start.10
  65.6 0.1 collective-permute-done.6
  65.7 1.4 collective-permute-start.11
  67.1 3.0 %collective-permute-start.12 = (bf16[36,832]{1,0:T(8,128)(2,1)S(1)}, bf16[36,832]{1,0:T(8,128)(2,1)S(1)}, u32[]{:S(2)}, u32[]{:S(2)}) collective-permute-start(bf16[36,832]{1,0:T(8,128)(2,1)S(1)} %reshape.136), channel_id=1, source_target_pairs={{0,13},{1,14},{2,15},{3,0},{4,1},{5,2},{6,3},{7,4},{8,5},{9,6},{10... | collective-permute-start | bytes 179720 | tf_op jit(solution)/shard_map/ppermute | solution.py:79
  70.1 3.9 %collective-permute-start.13 = (bf16[36,832]{1,0:T(8,128)(2,1)S(1)}, bf16[36,832]{1,0:T(8,128)(2,1)S(1)}, u32[]{:S(2)}, u32[]{:S(2)}) collective-permute-start(bf16[36,832]{1,0:T(8,128)(2,1)S(1)} %reshape.136), channel_id=1, source_target_pairs={{0,14},{1,15},{2,0},{3,1},{4,2},{5,3},{6,4},{7,5},{8,6},{9,7},{10,... | collective-permute-start | bytes 179720 | tf_op jit(solution)/shard_map/ppermute | solution.py:79
  74.0 0.1 collective-permute-start.14
  74.1 1.3 collective-permute-done.11
  75.5 3.9 %collective-permute-done.13 = bf16[36,832]{1,0:T(8,128)(2,1)S(1)} collective-permute-done((bf16[36,832]{1,0:T(8,128)(2,1)S(1)}, bf16[36,832]{1,0:T(8,128)(2,1)S(1)}, u32[]{:S(2)}, u32[]{:S(2)}) %collective-permute-start.13) | collective-permute-done | bytes 59936 | tf_op jit(solution)/shard_map/ppermute | solution.py:79
  79.4 1.5 collective-permute-done.14
  80.9 0.7 gather_fusion.1
  81.7 0.5 gather.16
  82.2 1.2 fusion.14.h_ref
  83.3 4.1 %shard_map.78 = bf16[1,2,144,384]{3,2,1,0:T(8,128)(2,1)} custom-call(bf16[1,4,144,832]{3,2,1,0:T(8,128)(2,1)} %fusion.14.h_ref, bf16[1,3328,384]{2,1,0:T(8,128)(2,1)} %bitcast.108), custom_call_target="tpu_custom_call" | custom-call | flops 736100352 | bytes 3735552 | tf_op jit(solution)/shard_map/pallas_call | solution.py:46
  87.5 1.1 copy.32
  88.6 2.2 %collective-permute-start.15 = (bf16[48,3,2,384]{3,0,1,2:T(8,128)(2,1)S(1)}, bf16[48,3,2,384]{3,0,1,2:T(8,128)(2,1)S(1)}, u32[]{:S(2)}, u32[]{:S(2)}) collective-permute-start(bf16[48,3,2,384]{3,0,1,2:T(8,128)(2,1)S(1)} %bitcast.111), channel_id=1, source_target_pairs={{0,0},{1,4},{2,8},{3,12},{4,1},{5,5},{6,9},{7,13},{8,2},{9,6},{10,... | collective-permute-start | bytes 663560 | tf_op jit(solution)/shard_map/ppermute | solution.py:129
  91.0 11.5 %collective-permute-done.15 = bf16[48,3,2,384]{3,0,1,2:T(8,128)(2,1)S(1)} collective-permute-done((bf16[48,3,2,384]{3,0,1,2:T(8,128)(2,1)S(1)}, bf16[48,3,2,384]{3,0,1,2:T(8,128)(2,1)S(1)}, u32[]{:S(2)}, u32[]{:S(2)}) %collective-permute-start.15) | collective-permute-done | bytes 221216 | tf_op jit(solution)/shard_map/ppermute | solution.py:129
  102.5 1.6 %fusion.16 = f32[2,3,384,3,384]{4,2,3,1,0:T(8,128)S(1)} fusion(bf16[96,1,3,384]{3,0,2,1:T(8,128)(2,1)S(1)} %get-tuple-element.21, bf16[96,1,3,384]{3,0,2,1:T(8,128)(2,1)S(1)} %get-tuple-element.20, bf16[48,3,384]{2,0,1:T(8,128)(2,1)S(1)} %get-tuple-element.17, bf16[48,3,384]{2,0,1:T(8,128)(2,1)S(1)} %get-tuple-element.16), kind=kOutput, calls=%fused_computation.18 | convolution fusion | flops 510935040 | bytes 11280384 | tf_op jit(solution)/shard_map/pjb,pcia->bcija/dot_general | solution.py:64
  104.0 0.6 slice-done
  104.7 0.3 slice-done.1
  105.0 4.6 %fusion = f32[384,2,3,3,384]{0,4,2,3,1:T(8,128)} fusion(f32[2,3,384,3,384]{4,2,3,1,0:T(8,128)S(1)} %fusion.16, f32[384,3,3,384]{0,3,1,2:T(8,128)S(1)} %bitcast.106), kind=kLoop, calls=%fused_computation.4 | loop fusion | flops 5308416 | bytes 26542080 | tf_op jit(solution)/shard_map/div | solution.py:147
  109.5 19.7 %copy.36 = f32[384,2,3,3,384]{4,1,3,2,0:T(2,128)} copy(f32[384,2,3,3,384]{0,4,2,3,1:T(8,128)} %fusion) | data formatting | bytes 21233664
  129.3 16.4 %shard_map.77 = bf16[3,2,128,1536]{3,2,1,0:T(8,128)(2,1)} custom-call(bf16[3,4,128,832]{3,2,1,0:T(8,128)(2,1)} %bitcast.109, bf16[4,3328,384]{2,1,0:T(8,128)(2,1)} %all-gather.7.cloned.1.call-done.v_ref), custom_call_target="tpu_custom_call" | custom-call | flops 7851737088 | bytes 15138816 | tf_op jit(solution)/shard_map/pallas_call | solution.py:46
  145.7 5.5 %copy.35 = bf16[3,128,2,1536]{3,2,1,0:T(2,128)(2,1)} copy(bf16[3,128,2,1536]{3,1,2,0:T(8,128)(2,1)} %bitcast.110) | data formatting | bytes 4718592
  (60 shorter events, 0.7 us)
Async XLA Ops:
  7.2 36.3 %copy-start = (f32[128]{0:T(128)S(1)}, f32[128]{0:T(128)}, u32[]{:S(2)}) copy-start(f32[128]{0:T(128)} %param.9) | copy-start | bytes 1540
  7.2 1.9 %copy-start.2 = (bf16[2,2,832,128]{3,2,1,0:T(8,128)(2,1)S(1)}, bf16[2,2,832,128]{3,2,1,0:T(8,128)(2,1)}, u32[]{:S(2)}) copy-start(bf16[2,2,832,128]{3,2,1,0:T(8,128)(2,1)} %param.7) | copy-start | bytes 2555908
  7.2 34.3 %all-gather.5.cloned.1.call-start = ((), (), s32[]{:S(2)}) async-start(), calls=%async_computation | async-start | bytes 1597440 | tf_op jit(solution)/shard_map/all_gather | solution.py:116
  9.1 120.2 %all-gather.7.cloned.1.call-start = ((), (), s32[]{:S(2)}) async-start(), calls=%async_computation.1 | async-start | bytes 11501568 | tf_op jit(solution)/shard_map/all_gather | solution.py:121
  41.6 1.2 copy-start.4
  44.1 10.7 %copy-start.3 = (f32[1536]{0:T(1024)S(1)}, f32[1536]{0:T(1024)}, u32[]{:S(2)}) copy-start(f32[1536]{0:T(1024)} %param.10) | copy-start | bytes 18436
  47.3 10.7 %collective-permute-start = (bf16[36,832]{1,0:T(8,128)(2,1)S(1)}, bf16[36,832]{1,0:T(8,128)(2,1)S(1)}, u32[]{:S(2)}, u32[]{:S(2)}) collective-permute-start(bf16[36,832]{1,0:T(8,128)(2,1)S(1)} %reshape.136), channel_id=1, source_target_pairs={{0,1},{1,2},{2,3},{3,4},{4,5},{5,6},{6,7},{7,8},{8,9},{9,10},{10,1... | collective-permute-start | bytes 179720 | tf_op jit(solution)/shard_map/ppermute | solution.py:79
  50.8 8.5 %collective-permute-start.1 = (bf16[36,832]{1,0:T(8,128)(2,1)S(1)}, bf16[36,832]{1,0:T(8,128)(2,1)S(1)}, u32[]{:S(2)}, u32[]{:S(2)}) collective-permute-start(bf16[36,832]{1,0:T(8,128)(2,1)S(1)} %reshape.136), channel_id=1, source_target_pairs={{0,2},{1,3},{2,4},{3,5},{4,6},{5,7},{6,8},{7,9},{8,10},{9,11},{10,... | collective-permute-start | bytes 179720 | tf_op jit(solution)/shard_map/ppermute | solution.py:79
  51.3 8.2 %collective-permute-start.2 = (bf16[36,832]{1,0:T(8,128)(2,1)S(1)}, bf16[36,832]{1,0:T(8,128)(2,1)S(1)}, u32[]{:S(2)}, u32[]{:S(2)}) collective-permute-start(bf16[36,832]{1,0:T(8,128)(2,1)S(1)} %reshape.136), channel_id=1, source_target_pairs={{0,3},{1,4},{2,5},{3,6},{4,7},{5,8},{6,9},{7,10},{8,11},{9,12},{10... | collective-permute-start | bytes 179720 | tf_op jit(solution)/shard_map/ppermute | solution.py:79
  51.3 9.4 %collective-permute-start.3 = (bf16[36,832]{1,0:T(8,128)(2,1)S(1)}, bf16[36,832]{1,0:T(8,128)(2,1)S(1)}, u32[]{:S(2)}, u32[]{:S(2)}) collective-permute-start(bf16[36,832]{1,0:T(8,128)(2,1)S(1)} %reshape.136), channel_id=1, source_target_pairs={{0,4},{1,5},{2,6},{3,7},{4,8},{5,9},{6,10},{7,11},{8,12},{9,13},{1... | collective-permute-start | bytes 179720 | tf_op jit(solution)/shard_map/ppermute | solution.py:79
  52.4 11.2 %collective-permute-start.4 = (bf16[36,832]{1,0:T(8,128)(2,1)S(1)}, bf16[36,832]{1,0:T(8,128)(2,1)S(1)}, u32[]{:S(2)}, u32[]{:S(2)}) collective-permute-start(bf16[36,832]{1,0:T(8,128)(2,1)S(1)} %reshape.136), channel_id=1, source_target_pairs={{0,5},{1,6},{2,7},{3,8},{4,9},{5,10},{6,11},{7,12},{8,13},{9,14},{... | collective-permute-start | bytes 179720 | tf_op jit(solution)/shard_map/ppermute | solution.py:79
  58.0 7.5 %collective-permute-start.5 = (bf16[36,832]{1,0:T(8,128)(2,1)S(1)}, bf16[36,832]{1,0:T(8,128)(2,1)S(1)}, u32[]{:S(2)}, u32[]{:S(2)}) collective-permute-start(bf16[36,832]{1,0:T(8,128)(2,1)S(1)} %reshape.136), channel_id=1, source_target_pairs={{0,6},{1,7},{2,8},{3,9},{4,10},{5,11},{6,12},{7,13},{8,14},{9,15},... | collective-permute-start | bytes 179720 | tf_op jit(solution)/shard_map/ppermute | solution.py:79
  59.3 6.4 %collective-permute-start.6 = (bf16[36,832]{1,0:T(8,128)(2,1)S(1)}, bf16[36,832]{1,0:T(8,128)(2,1)S(1)}, u32[]{:S(2)}, u32[]{:S(2)}) collective-permute-start(bf16[36,832]{1,0:T(8,128)(2,1)S(1)} %reshape.136), channel_id=1, source_target_pairs={{0,7},{1,8},{2,9},{3,10},{4,11},{5,12},{6,13},{7,14},{8,15},{9,0},... | collective-permute-start | bytes 179720 | tf_op jit(solution)/shard_map/ppermute | solution.py:79
  59.5 7.6 %collective-permute-start.7 = (bf16[36,832]{1,0:T(8,128)(2,1)S(1)}, bf16[36,832]{1,0:T(8,128)(2,1)S(1)}, u32[]{:S(2)}, u32[]{:S(2)}) collective-permute-start(bf16[36,832]{1,0:T(8,128)(2,1)S(1)} %reshape.136), channel_id=1, source_target_pairs={{0,8},{1,9},{2,10},{3,11},{4,12},{5,13},{6,14},{7,15},{8,0},{9,1},... | collective-permute-start | bytes 179720 | tf_op jit(solution)/shard_map/ppermute | solution.py:79
  60.8 9.3 %collective-permute-start.8 = (bf16[36,832]{1,0:T(8,128)(2,1)S(1)}, bf16[36,832]{1,0:T(8,128)(2,1)S(1)}, u32[]{:S(2)}, u32[]{:S(2)}) collective-permute-start(bf16[36,832]{1,0:T(8,128)(2,1)S(1)} %reshape.136), channel_id=1, source_target_pairs={{0,9},{1,10},{2,11},{3,12},{4,13},{5,14},{6,15},{7,0},{8,1},{9,2},... | collective-permute-start | bytes 179720 | tf_op jit(solution)/shard_map/ppermute | solution.py:79
  63.6 10.4 %collective-permute-start.9 = (bf16[36,832]{1,0:T(8,128)(2,1)S(1)}, bf16[36,832]{1,0:T(8,128)(2,1)S(1)}, u32[]{:S(2)}, u32[]{:S(2)}) collective-permute-start(bf16[36,832]{1,0:T(8,128)(2,1)S(1)} %reshape.136), channel_id=1, source_target_pairs={{0,10},{1,11},{2,12},{3,13},{4,14},{5,15},{6,0},{7,1},{8,2},{9,3},... | collective-permute-start | bytes 179720 | tf_op jit(solution)/shard_map/ppermute | solution.py:79
  65.5 8.6 %collective-permute-start.10 = (bf16[36,832]{1,0:T(8,128)(2,1)S(1)}, bf16[36,832]{1,0:T(8,128)(2,1)S(1)}, u32[]{:S(2)}, u32[]{:S(2)}) collective-permute-start(bf16[36,832]{1,0:T(8,128)(2,1)S(1)} %reshape.136), channel_id=1, source_target_pairs={{0,11},{1,12},{2,13},{3,14},{4,15},{5,0},{6,1},{7,2},{8,3},{9,4},{... | collective-permute-start | bytes 179720 | tf_op jit(solution)/shard_map/ppermute | solution.py:79
  65.7 9.8 %collective-permute-start.11 = (bf16[36,832]{1,0:T(8,128)(2,1)S(1)}, bf16[36,832]{1,0:T(8,128)(2,1)S(1)}, u32[]{:S(2)}, u32[]{:S(2)}) collective-permute-start(bf16[36,832]{1,0:T(8,128)(2,1)S(1)} %reshape.136), channel_id=1, source_target_pairs={{0,12},{1,13},{2,14},{3,15},{4,0},{5,1},{6,2},{7,3},{8,4},{9,5},{1... | collective-permute-start | bytes 179720 | tf_op jit(solution)/shard_map/ppermute | solution.py:79
  67.1 8.4 %collective-permute-start.12 = (bf16[36,832]{1,0:T(8,128)(2,1)S(1)}, bf16[36,832]{1,0:T(8,128)(2,1)S(1)}, u32[]{:S(2)}, u32[]{:S(2)}) collective-permute-start(bf16[36,832]{1,0:T(8,128)(2,1)S(1)} %reshape.136), channel_id=1, source_target_pairs={{0,13},{1,14},{2,15},{3,0},{4,1},{5,2},{6,3},{7,4},{8,5},{9,6},{10... | collective-permute-start | bytes 179720 | tf_op jit(solution)/shard_map/ppermute | solution.py:79
  70.1 9.4 %collective-permute-start.13 = (bf16[36,832]{1,0:T(8,128)(2,1)S(1)}, bf16[36,832]{1,0:T(8,128)(2,1)S(1)}, u32[]{:S(2)}, u32[]{:S(2)}) collective-permute-start(bf16[36,832]{1,0:T(8,128)(2,1)S(1)} %reshape.136), channel_id=1, source_target_pairs={{0,14},{1,15},{2,0},{3,1},{4,2},{5,3},{6,4},{7,5},{8,6},{9,7},{10,... | collective-permute-start | bytes 179720 | tf_op jit(solution)/shard_map/ppermute | solution.py:79
  74.0 6.9 %collective-permute-start.14 = (bf16[36,832]{1,0:T(8,128)(2,1)S(1)}, bf16[36,832]{1,0:T(8,128)(2,1)S(1)}, u32[]{:S(2)}, u32[]{:S(2)}) collective-permute-start(bf16[36,832]{1,0:T(8,128)(2,1)S(1)} %reshape.136), channel_id=1, source_target_pairs={{0,15},{1,0},{2,1},{3,2},{4,3},{5,4},{6,5},{7,6},{8,7},{9,8},{10,9... | collective-permute-start | bytes 179720 | tf_op jit(solution)/shard_map/ppermute | solution.py:79
  88.6 13.8 %collective-permute-start.15 = (bf16[48,3,2,384]{3,0,1,2:T(8,128)(2,1)S(1)}, bf16[48,3,2,384]{3,0,1,2:T(8,128)(2,1)S(1)}, u32[]{:S(2)}, u32[]{:S(2)}) collective-permute-start(bf16[48,3,2,384]{3,0,1,2:T(8,128)(2,1)S(1)} %bitcast.111), channel_id=1, source_target_pairs={{0,0},{1,4},{2,8},{3,12},{4,1},{5,5},{6,9},{7,13},{8,2},{9,6},{10,... | collective-permute-start | bytes 663560 | tf_op jit(solution)/shard_map/ppermute | solution.py:129
  102.4 2.2 %slice-start = ((s8[5308416]{0:T(1024)(128)(4,1)}), s8[4194304]{0:T(1024)(128)(4,1)S(1)}, s32[]{:S(2)}) async-start(s8[5308416]{0:T(1024)(128)(4,1)} %bitcast.105), calls=%async_computation.2 | async-start | bytes 8388608
  102.4 2.5 %slice-start.1 = ((s8[5308416]{0:T(1024)(128)(4,1)}), s8[1114112]{0:T(1024)(128)(4,1)S(1)}, s32[]{:S(2)}) async-start(s8[5308416]{0:T(1024)(128)(4,1)} %bitcast.105), calls=%async_computation.3 | async-start | bytes 2228224
  145.7 5.5 %copy-start.1 = (f32[128]{0:T(128)S(1)}, f32[128]{0:T(128)}, u32[]{:S(2)}) copy-start(f32[128]{0:T(128)} %param.9) | copy-start | bytes 1540
Sparse Core Ops, SparseCore 0:
  10.2 31.3 all-gather.4
  43.4 78.4 all-gather.6

commit v4 on v3

--- a/solution.py
+++ b/solution.py
@@ -102,26 +102,40 @@
     half_sel = jnp.einsum(
         "kmi,pmn->pikn", occ_sel, cholesky, preferred_element_type=jnp.float32
     ).astype(jnp.bfloat16)
-    half_sel = half_sel.reshape(vectors * batch * 4, orbitals)
-    gathered = gather_group(half_sel, ("aux", "pair"), (n_aux, n_pair))
-    count = gathered.shape[0] * vectors
+    sel_size = half_sel.size
+    sel_rows = -(-sel_size // a_width)
+    sel_flat = jnp.pad(half_sel.reshape(-1), (0, sel_rows * a_width - sel_size))
+
+    n_q = n_parts * n_aux
+    rows_q = rows // n_q
+    me_pair = lax.axis_index("pair")
+    q = lax.axis_index("parts") * n_aux + lax.axis_index("aux")
+    piece = lax.dynamic_slice_in_dim(v_local, q * rows_q, rows_q, 0)
+    carried = jnp.concatenate([piece, sel_flat.reshape(sel_rows, a_width)], 0)
+    stage1 = lax.all_gather(carried, "pair", axis=0)
+
+    half = jnp.einsum(
+        "kmj,pmn->pkjn", occ_left, cholesky, preferred_element_type=jnp.float32
+    ).astype(jnp.bfloat16)
+    own = transform(half, v_local[None]).transpose(0, 2, 1, 3)
+    stage1, half, own = lax.optimization_barrier((stage1, half, own))
+    pair_vectors = jnp.zeros((vectors, occupied, 2, virtuals), jnp.bfloat16)
+    pair_vectors = lax.dynamic_update_slice_in_dim(pair_vectors, own, me_pair * a_width, 3)
+
+    sel_pair = stage1[:, rows_q:].reshape(n_pair, -1)[:, :sel_size]
+    gathered = gather_group(sel_pair, ("aux",), (n_aux,))
+    count = n_aux * n_pair * vectors
     half_rows = gathered.reshape(count * batch, 4, orbitals).transpose(1, 0, 2)
     sel_own = transform(half_rows[None], v_local[None])
     sel_own = sel_own.reshape(2, count, batch, a_width)
 
-    n_q = n_parts * n_aux
-    rows_q = rows // n_q
-    q = lax.axis_index("parts") * n_aux + lax.axis_index("aux")
-    piece = lax.dynamic_slice_in_dim(v_local, q * rows_q, rows_q, 0)
-    stage1 = lax.all_gather(piece, "pair", axis=0)
-    half = jnp.einsum(
-        "kmj,pmn->pkjn", occ_left, cholesky, preferred_element_type=jnp.float32
-    ).astype(jnp.bfloat16)
-    stage1, half = lax.optimization_barrier((stage1, half))
-    stage2 = lax.all_gather(stage1, ("parts", "aux"), axis=1)
-    v_full = stage2.reshape(n_pair, rows, a_width)
-    full = transform(half, v_full)
-    pair_vectors = full.transpose(0, 2, 1, 3)
+    pieces = stage1[:, :rows_q]
+    for step in range(1, n_pair):
+        block = (me_pair + step) % n_pair
+        part = lax.dynamic_index_in_dim(pieces, block, 0, keepdims=False)
+        v_block = lax.all_gather(part, ("parts", "aux"), axis=0, tiled=True)
+        done = transform(half, v_block[None]).transpose(0, 2, 1, 3)
+        pair_vectors = lax.dynamic_update_slice_in_dim(pair_vectors, done, block * a_width, 3)
 
     sel_a = sel_own.transpose(1, 2, 0, 3)
     if n_aux == n_pair:

time: 161 us -> 172 us (1.068)
  starting transfers between devices: 25.3 us -> 6.74 us
  waiting for transfers between devices: 41.5 us -> 52.2 us
  Pallas kernels: 20.5 us -> 30.8 us
  local copies, waits for them, and re-layouts: 36.2 us -> 42.1 us
  other arithmetic: 9.05 us -> 12.4 us
    ppermute x15 -> x3, starting transfers between devices: 23 us -> 3.27 us  [gather_group(): blocks.append(lax.ppermute(x, axes, perm))]
    pallas_call x2 -> x5, Pallas kernels: 20.5 us -> 30.8 us  [transform(): pl.pallas_call(functools.partial(transform_kernel, n), grid=(b,), in_spec...]
    all_gather x2 -> x4, waiting for transfers between devices: 23.1 us -> 29.4 us  [the longest x1 19.5 us: on_device(): stage1 = lax.all_gather(carried, 'pair', axis=0)]
    dynamic_update_slice x0 -> x4, local copies, waits for them, and re-layouts: none -> 5.1 us  [the longest x3 4.36 us: on_device(): lax.dynamic_update_slice_in_dim(pair_vectors, done, block * a_width, 3)]
    unnamed x31 -> x24, local copies, waits for them, and re-layouts: 26.4 us -> 22.1 us
    ppermute x15 -> x3, waiting for transfers between devices: 6.89 us -> 10.5 us  [gather_group(): blocks.append(lax.ppermute(x, axes, perm))]
    select_n x0 -> x2, local copies, waits for them, and re-layouts: none -> 2.26 us  [gather_group(): return jnp.take(stacked, (me - jnp.arange(n)) % n, axis=0)]
  transfers between devices with their start and end apart: 18 -> 8, of which waited for: 6 -> 5; matrix products, arithmetic and copies ran while one was open for 30% -> 29% of each run, Pallas kernels for 3% -> 14%
where the time goes in v4:
time: 172 us; the launch traced here: 169 us
  waiting for transfers between devices  52.2 us (30%)
  local copies, waits for them, and re-layouts  42.1 us (24%)
  Pallas kernels  30.8 us (18%)
  between operations  14.1 us (8%)
  other arithmetic  12.4 us (7%)
  matrix products  11.1 us (6%)
  starting transfers between devices  6.74 us (4%)
    pallas_call x5, Pallas kernels, transform(): pl.pallas_call(functools.partial(transform_kernel, n), grid=(b,), in_spec...  30.8 us
    unnamed x24, local copies, waits for them, and re-layouts  22.1 us
    all_gather x1, waiting for transfers between devices, on_device(): stage1 = lax.all_gather(carried, 'pair', axis=0)  19.5 us
    ppermute x1, waiting for transfers between devices, on_device(): sel_b = lax.ppermute(sel_a, ('aux', 'pair'), perm)  11.5 us
    ppermute x3, waiting for transfers between devices, gather_group(): blocks.append(lax.ppermute(x, axes, perm))  10.5 us
    all_gather x3, waiting for transfers between devices, on_device(): v_block = lax.all_gather(part, ('parts', 'aux'), axis=0, tiled=True)  9.91 us
    dot_general x1, matrix products, on_device(): jnp.einsum('kmj,pmn->pkjn', occ_left, cholesky, preferred_element_type=jn...  6.42 us
    div x1, other arithmetic, on_device(): amplitudes = paired / denominator  4.5 us
  transfers between devices with their start and end apart: 8, of which 5 were waited for; matrix products, arithmetic and copies ran while one was open for 29% of the time, Pallas kernels for 14%

profile of v4, /device:TPU:29, one launch (start us, length us, event | category | flops | bytes accessed | tf_op | source)
XLA Modules:
  0.0 169.4 jit_solution(2437506043983278761)
XLA Ops:
  7.2 0.7 compare_select_fusion.2
  7.9 0.6 gather_fusion.2
  8.5 0.7 broadcast_select_fusion.1
  9.2 1.2 slice_bitcast_fusion
  10.5 1.2 copy.57
  11.7 0.6 gather_fusion
  12.3 3.0 %fusion.11 = bf16[3,3,4,832]{3,2,0,1:T(4,128)(2,1)S(1)} fusion(bf16[3,832,832]{2,1,0:T(8,128)(2,1)} %param.6, bf16[3,4,832]{2,1,0:T(4,128)(2,1)S(1)} %gather_fusion, pred[3]{0:T(512)(128)(4,1)S(1)} %get-tuple-element.19), kind=kOutput, calls=%fused_computation.12 | convolution fusion | flops 49880064 | bytes 4233219 | tf_op jit(solution)/shard_map/kmi,pmn->pikn/dot_general | solution.py:102
  15.4 0.1 reshape.139
  15.5 1.0 constant_dynamic-slice_fusion.3
  16.5 0.8 maximum_bitcast_fusion.2
  17.4 6.4 %fusion.5 = bf16[4,128,3,832]{1,3,2,0:T(8,128)(2,1)S(1)} fusion(bf16[3,832,832]{2,1,0:T(8,128)(2,1)} %param.6, bf16[2,832,128]{2,1,0:T(8,128)(2,1)S(1)} %get-tuple-element.26, bf16[2,832,128]{2,1,0:T(8,128)(2,1)S(1)} %get-tuple-element.25), kind=kOutput, calls=%fused_computation.10 | convolution fusion | flops 2129494016 | bytes 7561216 | tf_op jit(solution)/shard_map/kmj,pmn->pkjn/dot_general | solution.py:117
  23.9 2.8 %copy.60 = bf16[4,128,3,832]{3,1,0,2:T(8,128)(2,1)} copy(bf16[4,128,3,832]{1,3,2,0:T(8,128)(2,1)S(1)} %fusion.5) | data formatting | bytes 5111808 | tf_op jit(solution)/shard_map/convert_element_type | solution.py:119
  26.6 6.7 %shard_map.77 = bf16[3,2,128,384]{3,2,1,0:T(8,128)(2,1)} custom-call(bf16[3,4,128,832]{3,2,1,0:T(8,128)(2,1)} %bitcast.92, bf16[1,3328,384]{2,1,0:T(8,128)(2,1)} %bitcast.90), custom_call_target="tpu_custom_call" | custom-call | flops 1962934272 | bytes 5701632 | tf_op jit(solution)/shard_map/pallas_call | solution.py:46
  33.3 19.5 %all-gather.16.cloned.1.call-done = bf16[4,494,384]{2,1,0:T(8,128)(2,1)} async-done(((bf16[1,494,384]{2,1,0:T(8,128)(2,1)}), bf16[4,494,384]{2,1,0:T(8,128)(2,1)}) %all-gather.16.cloned.1.call-update) | async-done | bytes 1517584 | tf_op jit(solution)/shard_map/all_gather | solution.py:115
  52.8 1.3 slice-done.2
  54.1 1.0 constant_dynamic-slice_fusion
  55.2 0.7 all-gather.10.cloned.1.call-update
  56.3 2.9 %broadcast_subtract_fusion = f32[384,3,3,384]{0,3,1,2:T(8,128)} fusion(f32[384]{0:T(512)S(1)} %get-tuple-element.34, f32[3,3,384]{2,0,1:T(4,128)S(1)} %broadcast_subtract_fusion.1), kind=kLoop, calls=%fused_computation.9 | loop fusion | flops 1327104 | bytes 5323776 | tf_op jit(solution)/shard_map/sub | solution.py:157
  59.2 0.1 copy.76
  59.3 0.6 collective-permute-start.2
  59.9 1.2 collective-permute-start.1
  61.1 1.5 collective-permute-start
  62.7 1.2 broadcast_in_dim.44
  64.0 0.7 copy_dynamic-update-slice_fusion.3
  64.7 4.4 %collective-permute-done.2 = bf16[4,29952]{1,0:T(4,128)(2,1)S(1)} collective-permute-done((bf16[4,29952]{1,0:T(4,128)(2,1)S(1)}, bf16[4,29952]{1,0:T(4,128)(2,1)S(1)}, u32[]{:S(2)}, u32[]{:S(2)}) %collective-permute-start.2) | collective-permute-done | bytes 239648 | tf_op jit(solution)/shard_map/ppermute | solution.py:79
  69.1 6.1 %collective-permute-done = bf16[4,29952]{1,0:T(4,128)(2,1)S(1)} collective-permute-done((bf16[4,29952]{1,0:T(4,128)(2,1)S(1)}, bf16[4,29952]{1,0:T(4,128)(2,1)S(1)}, u32[]{:S(2)}, u32[]{:S(2)}) %collective-permute-start) | collective-permute-done | bytes 239648 | tf_op jit(solution)/shard_map/ppermute | solution.py:79
  75.2 0.9 pad_maximum_fusion
  76.1 1.4 gather_fusion.1
  77.5 0.5 broadcast_select_fusion
  78.0 1.2 select_n.122
  79.1 1.1 copy.84
  80.2 4.1 %shard_map.81 = bf16[1,2,144,384]{3,2,1,0:T(8,128)(2,1)} custom-call(bf16[1,4,144,832]{3,2,1,0:T(8,128)(2,1)} %bitcast.88, bf16[1,3328,384]{2,1,0:T(8,128)(2,1)} %bitcast.91), custom_call_target="tpu_custom_call" | custom-call | flops 736100352 | bytes 3735552 | tf_op jit(solution)/shard_map/pallas_call | solution.py:46
  84.4 1.1 copy.66
  85.5 3.3 %collective-permute-start.3 = (bf16[48,3,2,384]{3,0,1,2:T(8,128)(2,1)S(1)}, bf16[48,3,2,384]{3,0,1,2:T(8,128)(2,1)S(1)}, u32[]{:S(2)}, u32[]{:S(2)}) collective-permute-start(bf16[48,3,2,384]{3,0,1,2:T(8,128)(2,1)S(1)} %bitcast.96), channel_id=1, source_target_pairs={{0,0},{1,4},{2,8},{3,12},{4,1},{5,5},{6,9},{7,13},{8,2},{9,6},{10,... | collective-permute-start | bytes 663560 | tf_op jit(solution)/shard_map/ppermute | solution.py:143
  88.9 11.5 %collective-permute-done.3 = bf16[48,3,2,384]{3,0,1,2:T(8,128)(2,1)S(1)} collective-permute-done((bf16[48,3,2,384]{3,0,1,2:T(8,128)(2,1)S(1)}, bf16[48,3,2,384]{3,0,1,2:T(8,128)(2,1)S(1)}, u32[]{:S(2)}, u32[]{:S(2)}) %collective-permute-start.3) | collective-permute-done | bytes 221216 | tf_op jit(solution)/shard_map/ppermute | solution.py:143
  100.5 1.6 fusion.15
  102.1 0.6 slice-done
  102.7 0.3 slice-done.1
  103.0 4.5 %fusion = f32[384,2,3,3,384]{0,4,2,3,1:T(8,128)} fusion(f32[2,3,384,3,384]{4,2,3,1,0:T(8,128)S(1)} %fusion.15, f32[384,3,3,384]{0,3,1,2:T(8,128)S(1)} %bitcast.87), kind=kLoop, calls=%fused_computation.4 | loop fusion | flops 5308416 | bytes 26542080 | tf_op jit(solution)/shard_map/div | solution.py:161
  107.5 19.7 %copy.69 = f32[384,2,3,3,384]{4,1,3,2,0:T(2,128)} copy(f32[384,2,3,3,384]{0,4,2,3,1:T(8,128)} %fusion) | data formatting | bytes 21233664
  127.2 6.6 %shard_map.79 = bf16[3,2,128,384]{3,2,1,0:T(8,128)(2,1)} custom-call(bf16[3,4,128,832]{3,2,1,0:T(8,128)(2,1)} %bitcast.93, bf16[1,3328,384]{2,1,0:T(8,128)(2,1)} %all-gather.12.cloned.1.call-done.v_ref), custom_call_target="tpu_custom_call" | custom-call | flops 1962934272 | bytes 5701632 | tf_op jit(solution)/shard_map/pallas_call | solution.py:46
  133.7 6.8 %shard_map.78 = bf16[3,2,128,384]{3,2,1,0:T(8,128)(2,1)} custom-call(bf16[3,4,128,832]{3,2,1,0:T(8,128)(2,1)} %bitcast.94, bf16[1,3328,384]{2,1,0:T(8,128)(2,1)} %all-gather.10.cloned.1.call-done.v_ref), custom_call_target="tpu_custom_call" | custom-call | flops 1962934272 | bytes 5701632 | tf_op jit(solution)/shard_map/pallas_call | solution.py:46
  140.5 1.8 %copy_dynamic-update-slice_fusion.2 = bf16[3,128,2,1536]{3,2,1,0:T(2,128)(2,1)S(1)} fusion(bf16[3,128,2,1536]{3,2,1,0:T(2,128)(2,1)S(1)} %copy-done.4, s32[]{:T(128)S(6)} %select_n.110, bf16[3,128,2,384]{3,1,2,0:T(8,128)(2,1)} %bitcast.103), kind=kLoop, calls=%fused_computation.20 | loop fusion | bytes 1179652 | tf_op jit(solution)/shard_map/dynamic_update_slice | solution.py:138
  142.4 0.7 copy_dynamic-update-slice_fusion.1
  143.1 9.9 %all-gather.14.cloned.1.call-done.v_ref = bf16[1,3328,384]{2,1,0:T(8,128)(2,1)} async-done(((bf16[1,416,384]{2,1,0:T(8,128)(2,1)}), bf16[1,3328,384]{2,1,0:T(8,128)(2,1)}) %all-gather.14.cloned.1.call-update) | async-done | bytes 2555920 | tf_op jit(solution)/shard_map/all_gather | solution.py:136
  153.0 6.6 %shard_map.80 = bf16[3,2,128,384]{3,2,1,0:T(8,128)(2,1)} custom-call(bf16[3,4,128,832]{3,2,1,0:T(8,128)(2,1)} %bitcast.95, bf16[1,3328,384]{2,1,0:T(8,128)(2,1)} %all-gather.14.cloned.1.call-done.v_ref), custom_call_target="tpu_custom_call" | custom-call | flops 1962934272 | bytes 5701632 | tf_op jit(solution)/shard_map/pallas_call | solution.py:46
  159.6 1.8 %copy_dynamic-update-slice_fusion = bf16[3,128,2,1536]{3,2,1,0:T(2,128)(2,1)S(1)} fusion(bf16[3,128,2,1536]{3,2,1,0:T(2,128)(2,1)S(1)} %copy_dynamic-update-slice_fusion.1, s32[]{:T(128)S(6)} %select_n.116, bf16[3,128,2,384]{3,1,2,0:T(8,128)(2,1)} %bitcast.102), kind=kLoop, calls=%fused_computation.18 | loop fusion | bytes 1179652 | tf_op jit(solution)/shard_map/dynamic_update_slice | solution.py:138
  161.4 1.4 copy-done.5
  (47 shorter events, 0.9 us)
Async XLA Ops:
  7.2 0.7 copy-start
  7.2 45.7 %all-gather.16.cloned.1.call-start = ((), (), s32[]{:S(2)}) async-start(), calls=%async_computation.3 | async-start | bytes 1904640 | tf_op jit(solution)/shard_map/all_gather | solution.py:115
  17.4 109.8 %all-gather.12.cloned.1.call-start = ((), (), s32[]{:S(2)}) async-start(), calls=%async_computation.1 | async-start | bytes 2875392 | tf_op jit(solution)/shard_map/all_gather | solution.py:136
  52.8 1.3 slice-start.2
  52.8 3.2 %copy-start.8 = (f32[1536]{0:T(1024)S(1)}, f32[1536]{0:T(1024)}, u32[]{:S(2)}) copy-start(f32[1536]{0:T(1024)} %param.10) | copy-start | bytes 18436
  55.2 78.6 %all-gather.10.cloned.1.call-start = ((), (), s32[]{:S(2)}) async-start(), calls=%async_computation | async-start | bytes 2875392 | tf_op jit(solution)/shard_map/all_gather | solution.py:136
  55.9 97.1 %all-gather.14.cloned.1.call-start = ((), (), s32[]{:S(2)}) async-start(), calls=%async_computation.2 | async-start | bytes 2875392 | tf_op jit(solution)/shard_map/all_gather | solution.py:136
  56.3 2.9 %copy-start.2 = (bf16[4,494,384]{2,1,0:T(8,128)(2,1)S(1)}, bf16[4,494,384]{2,1,0:T(8,128)(2,1)}, u32[]{:S(2)}) copy-start(bf16[4,494,384]{2,1,0:T(8,128)(2,1)} %all-gather.16.cloned.1.call-done) | copy-start | bytes 4552708
  59.2 4.8 %copy-start.6 = (bf16[3,2,128,384]{3,2,1,0:T(8,128)(2,1)S(1)}, bf16[3,2,128,384]{3,2,1,0:T(8,128)(2,1)}, u32[]{:S(2)}) copy-start(bf16[3,2,128,384]{3,2,1,0:T(8,128)(2,1)} %shard_map.77) | copy-start | bytes 1769476
  59.3 9.8 %collective-permute-start.2 = (bf16[4,29952]{1,0:T(4,128)(2,1)S(1)}, bf16[4,29952]{1,0:T(4,128)(2,1)S(1)}, u32[]{:S(2)}, u32[]{:S(2)}) collective-permute-start(bf16[4,29952]{1,0:T(4,128)(2,1)S(1)} %bitcast.104), channel_id=1, source_target_pairs={{0,12},{4,0},{8,4},{12,8},{1,13},{5,1},{9,5},{13,9},{2,14},{6,2},{... | collective-permute-start | bytes 718856 | tf_op jit(solution)/shard_map/ppermute | solution.py:79
  59.9 9.2 %collective-permute-start.1 = (bf16[4,29952]{1,0:T(4,128)(2,1)S(1)}, bf16[4,29952]{1,0:T(4,128)(2,1)S(1)}, u32[]{:S(2)}, u32[]{:S(2)}) collective-permute-start(bf16[4,29952]{1,0:T(4,128)(2,1)S(1)} %bitcast.105), channel_id=1, source_target_pairs={{0,8},{4,12},{8,0},{12,4},{1,9},{5,13},{9,1},{13,5},{2,10},{6,14},... | collective-permute-start | bytes 718856 | tf_op jit(solution)/shard_map/ppermute | solution.py:79
  61.1 14.1 %collective-permute-start = (bf16[4,29952]{1,0:T(4,128)(2,1)S(1)}, bf16[4,29952]{1,0:T(4,128)(2,1)S(1)}, u32[]{:S(2)}, u32[]{:S(2)}) collective-permute-start(bf16[4,29952]{1,0:T(4,128)(2,1)S(1)} %bitcast.106), channel_id=1, source_target_pairs={{0,4},{4,8},{8,12},{12,0},{1,5},{5,9},{9,13},{13,1},{2,6},{6,10},{... | collective-permute-start | bytes 718856 | tf_op jit(solution)/shard_map/ppermute | solution.py:79
  64.7 10.5 %copy-start.3 = (bf16[3,128,2,1536]{3,2,1,0:T(2,128)(2,1)}, bf16[3,128,2,1536]{3,2,1,0:T(2,128)(2,1)S(1)}, u32[]{:S(2)}) copy-start(bf16[3,128,2,1536]{3,2,1,0:T(2,128)(2,1)S(1)} %copy_dynamic-update-slice_fusion.3) | copy-start | bytes 7077892
  85.5 15.0 %collective-permute-start.3 = (bf16[48,3,2,384]{3,0,1,2:T(8,128)(2,1)S(1)}, bf16[48,3,2,384]{3,0,1,2:T(8,128)(2,1)S(1)}, u32[]{:S(2)}, u32[]{:S(2)}) collective-permute-start(bf16[48,3,2,384]{3,0,1,2:T(8,128)(2,1)S(1)} %bitcast.96), channel_id=1, source_target_pairs={{0,0},{1,4},{2,8},{3,12},{4,1},{5,5},{6,9},{7,13},{8,2},{9,6},{10,... | collective-permute-start | bytes 663560 | tf_op jit(solution)/shard_map/ppermute | solution.py:143
  100.5 2.2 %slice-start = ((s8[5308416]{0:T(1024)(128)(4,1)}), s8[4194304]{0:T(1024)(128)(4,1)S(1)}, s32[]{:S(2)}) async-start(s8[5308416]{0:T(1024)(128)(4,1)} %bitcast.86), calls=%async_computation.4 | async-start | bytes 8388608
  100.5 2.5 %slice-start.1 = ((s8[5308416]{0:T(1024)(128)(4,1)}), s8[1114112]{0:T(1024)(128)(4,1)S(1)}, s32[]{:S(2)}) async-start(s8[5308416]{0:T(1024)(128)(4,1)} %bitcast.86), calls=%async_computation.5 | async-start | bytes 2228224
  133.7 6.8 %copy-start.4 = (bf16[3,128,2,1536]{3,2,1,0:T(2,128)(2,1)S(1)}, bf16[3,128,2,1536]{3,2,1,0:T(2,128)(2,1)}, u32[]{:S(2)}) copy-start(bf16[3,128,2,1536]{3,2,1,0:T(2,128)(2,1)} %copy-done.3) | copy-start | bytes 7077892
  133.7 8.6 %copy-start.7 = (bf16[3,2,128,384]{3,2,1,0:T(8,128)(2,1)S(1)}, bf16[3,2,128,384]{3,2,1,0:T(8,128)(2,1)}, u32[]{:S(2)}) copy-start(bf16[3,2,128,384]{3,2,1,0:T(8,128)(2,1)} %shard_map.79) | copy-start | bytes 1769476
  142.4 20.5 %copy-start.1 = (f32[128]{0:T(128)S(1)}, f32[128]{0:T(128)}, u32[]{:S(2)}) copy-start(f32[128]{0:T(128)} %param.9) | copy-start | bytes 1540
  161.4 1.4 copy-start.5
Sparse Core Ops, SparseCore 0:
  17.5 35.3 all-gather.15
  55.3 34.3 all-gather.11
  91.5 29.8 all-gather.9
  123.2 29.8 all-gather.13

commit v5 on v4

--- a/solution.py
+++ b/solution.py
@@ -130,12 +130,15 @@
     sel_own = sel_own.reshape(2, count, batch, a_width)
 
     pieces = stage1[:, :rows_q]
+    others = (me_pair + jnp.arange(1, n_pair)) % n_pair
+    send = jnp.take(pieces, others, axis=0)
+    plane = gather_group(send, ("parts", "aux"), (n_parts, n_aux))
+    v_others = plane.transpose(1, 0, 2, 3).reshape(n_pair - 1, rows, a_width)
+    done = transform(half, v_others).transpose(0, 2, 1, 3)
     for step in range(1, n_pair):
-        block = (me_pair + step) % n_pair
-        part = lax.dynamic_index_in_dim(pieces, block, 0, keepdims=False)
-        v_block = lax.all_gather(part, ("parts", "aux"), axis=0, tiled=True)
-        done = transform(half, v_block[None]).transpose(0, 2, 1, 3)
-        pair_vectors = lax.dynamic_update_slice_in_dim(pair_vectors, done, block * a_width, 3)
+        block = others[step - 1]
+        cols = done[..., (step - 1) * a_width:step * a_width]
+        pair_vectors = lax.dynamic_update_slice_in_dim(pair_vectors, cols, block * a_width, 3)
 
     sel_a = sel_own.transpose(1, 2, 0, 3)
     if n_aux == n_pair:

time: 172 us -> 243 us (1.41)
  the two profiles are of different devices: /device:TPU:29 before, /device:TPU:3 now
where the time goes in v5:
time: 243 us; the launch traced here: 242 us
  waiting for transfers between devices  86.3 us (36%)
  local copies, waits for them, and re-layouts  66.3 us (27%)
  Pallas kernels  24 us (10%)
  starting transfers between devices  19.2 us (8%)
  other arithmetic  19 us (8%)
  between operations  16.4 us (7%)
  matrix products  11.1 us (5%)
    ppermute x10, waiting for transfers between devices, gather_group(): blocks.append(lax.ppermute(x, axes, perm))  65.4 us
    unnamed x26, local copies, waits for them, and re-layouts  32.4 us
    pallas_call x3, Pallas kernels, transform(): pl.pallas_call(functools.partial(transform_kernel, n), grid=(b,), in_spec...  24 us
    all_gather x1, waiting for transfers between devices, on_device(): stage1 = lax.all_gather(carried, 'pair', axis=0)  15.2 us
    ppermute x10, starting transfers between devices, gather_group(): blocks.append(lax.ppermute(x, axes, perm))  13.9 us
    gather x2, local copies, waits for them, and re-layouts, gather_group(): return jnp.take(stacked, (me - jnp.arange(n)) % n, axis=0)  9.18 us
    dot_general x1, matrix products, on_device(): jnp.einsum('kmj,pmn->pkjn', occ_left, cholesky, preferred_element_type=jn...  6.42 us
    select_n x3, local copies, waits for them, and re-layouts, gather_group(): return jnp.take(stacked, (me - jnp.arange(n)) % n, axis=0)  6.13 us
  transfers between devices with their start and end apart: 12, of which 7 were waited for; matrix products, arithmetic and copies ran while one was open for 25% of the time, Pallas kernels for 4%

profile of v5, /device:TPU:3, one launch (start us, length us, event | category | flops | bytes accessed | tf_op | source)
XLA Modules:
  0.0 242.2 jit_solution(15673926436254276953)
XLA Ops:
  7.2 1.2 slice_bitcast_fusion
  8.5 1.2 copy.46
  12.3 3.0 %fusion.11 = bf16[3,3,4,832]{3,2,0,1:T(4,128)(2,1)S(1)} fusion(bf16[3,832,832]{2,1,0:T(8,128)(2,1)} %param.6, bf16[3,4,832]{2,1,0:T(4,128)(2,1)S(1)} %gather_fusion, pred[3]{0:T(512)(128)(4,1)S(1)} %get-tuple-element.17), kind=kOutput, calls=%fused_computation.15 | convolution fusion | flops 49880064 | bytes 4233219 | tf_op jit(solution)/shard_map/kmi,pmn->pikn/dot_general | solution.py:102
  15.6 1.0 constant_dynamic-slice_fusion
  20.1 6.4 %fusion.5 = bf16[4,128,3,832]{1,3,2,0:T(8,128)(2,1)S(1)} fusion(bf16[3,832,832]{2,1,0:T(8,128)(2,1)} %param.6, bf16[2,832,128]{2,1,0:T(8,128)(2,1)S(1)} %get-tuple-element.24, bf16[2,832,128]{2,1,0:T(8,128)(2,1)S(1)} %get-tuple-element.23), kind=kOutput, calls=%fused_computation.13 | convolution fusion | flops 2129494016 | bytes 7561216 | tf_op jit(solution)/shard_map/kmj,pmn->pkjn/dot_general | solution.py:117
  26.5 2.7 %copy.49 = bf16[4,128,3,832]{3,1,0,2:T(8,128)(2,1)} copy(bf16[4,128,3,832]{1,3,2,0:T(8,128)(2,1)S(1)} %fusion.5) | data formatting | bytes 5111808 | tf_op jit(solution)/shard_map/convert_element_type | solution.py:119
  29.4 6.6 %shard_map.77 = bf16[3,2,128,384]{3,2,1,0:T(8,128)(2,1)} custom-call(bf16[3,4,128,832]{3,2,1,0:T(8,128)(2,1)} %bitcast.119, bf16[1,3328,384]{2,1,0:T(8,128)(2,1)} %bitcast.117), custom_call_target="tpu_custom_call" | custom-call | flops 1962934272 | bytes 5701632 | tf_op jit(solution)/shard_map/pallas_call | solution.py:46
  36.2 2.9 %broadcast_subtract_fusion = f32[384,3,3,384]{0,3,1,2:T(8,128)} fusion(f32[384]{0:T(512)S(1)} %get-tuple-element.32, f32[3,3,384]{2,0,1:T(4,128)S(1)} %broadcast_subtract_fusion.1), kind=kLoop, calls=%fused_computation.12 | loop fusion | flops 1327104 | bytes 5323776 | tf_op jit(solution)/shard_map/sub | solution.py:160
  39.1 15.2 %all-gather.4.cloned.1.call-done = bf16[4,494,384]{2,1,0:T(8,128)(2,1)} async-done(((bf16[1,494,384]{2,1,0:T(8,128)(2,1)}), bf16[4,494,384]{2,1,0:T(8,128)(2,1)}) %all-gather.4.cloned.1.call-update) | async-done | bytes 1517584 | tf_op jit(solution)/shard_map/all_gather | solution.py:115
  54.3 1.4 slice.46
  56.5 1.2 fusion.14
  57.7 1.2 broadcast_select_fusion.1
  58.9 2.5 %collective-permute-start = (bf16[3,416,384]{2,1,0:T(8,128)(2,1)}, bf16[3,416,384]{2,1,0:T(8,128)(2,1)}, u32[]{:S(2)}, u32[]{:S(2)}) collective-permute-start(bf16[3,416,384]{2,1,0:T(8,128)(2,1)} %broadcast_select_fusion.1), channel_id=1, source_target_pairs={{0,4},{4,8},{8,12},{12,16},{16,20},{20,24},{24,28},{28,0},{1,5},{5... | collective-permute-start | bytes 2875400 | tf_op jit(solution)/shard_map/ppermute | solution.py:79
  61.4 1.2 collective-permute-start.1
  62.6 1.0 fusion.38
  64.1 1.9 collective-permute-start.7
  66.1 1.2 broadcast_in_dim.59
  68.1 20.9 %collective-permute-done.9 = bf16[4,29952]{1,0:T(4,128)(2,1)S(1)} collective-permute-done((bf16[4,29952]{1,0:T(4,128)(2,1)S(1)}, bf16[4,29952]{1,0:T(4,128)(2,1)S(1)}, u32[]{:S(2)}, u32[]{:S(2)}) %collective-permute-start.9) | collective-permute-done | bytes 239648 | tf_op jit(solution)/shard_map/ppermute | solution.py:79
  89.1 19.8 %collective-permute-done.8 = bf16[4,29952]{1,0:T(4,128)(2,1)S(1)} collective-permute-done((bf16[4,29952]{1,0:T(4,128)(2,1)S(1)}, bf16[4,29952]{1,0:T(4,128)(2,1)S(1)}, u32[]{:S(2)}, u32[]{:S(2)}) %collective-permute-start.8) | collective-permute-done | bytes 239648 | tf_op jit(solution)/shard_map/ppermute | solution.py:79
  108.9 1.2 collective-permute-start.3
  110.1 2.9 %collective-permute-done.7 = bf16[4,29952]{1,0:T(4,128)(2,1)S(1)} collective-permute-done((bf16[4,29952]{1,0:T(4,128)(2,1)S(1)}, bf16[4,29952]{1,0:T(4,128)(2,1)S(1)}, u32[]{:S(2)}, u32[]{:S(2)}) %collective-permute-start.7) | collective-permute-done | bytes 239648 | tf_op jit(solution)/shard_map/ppermute | solution.py:79
  113.0 0.9 pad_maximum_fusion
  113.8 1.4 gather_fusion.3
  115.7 1.2 select_n.190
  116.9 1.1 copy.74
  118.0 4.1 %shard_map.79 = bf16[1,2,144,384]{3,2,1,0:T(8,128)(2,1)} custom-call(bf16[1,4,144,832]{3,2,1,0:T(8,128)(2,1)} %bitcast.115, bf16[1,3328,384]{2,1,0:T(8,128)(2,1)} %bitcast.118), custom_call_target="tpu_custom_call" | custom-call | flops 736100352 | bytes 3735552 | tf_op jit(solution)/shard_map/pallas_call | solution.py:46
  122.1 1.3 copy.56
  123.4 5.2 %collective-permute-start.10 = (bf16[48,3,2,384]{3,0,1,2:T(8,128)(2,1)S(1)}, bf16[48,3,2,384]{3,0,1,2:T(8,128)(2,1)S(1)}, u32[]{:S(2)}, u32[]{:S(2)}) collective-permute-start(bf16[48,3,2,384]{3,0,1,2:T(8,128)(2,1)S(1)} %bitcast.123), channel_id=1, source_target_pairs={{0,0},{1,4},{2,8},{3,12},{4,1},{5,5},{6,9},{7,13},{8,2},{9,6},{10,... | collective-permute-start | bytes 663560 | tf_op jit(solution)/shard_map/ppermute | solution.py:146
  128.7 5.7 %collective-permute-done.10 = bf16[48,3,2,384]{3,0,1,2:T(8,128)(2,1)S(1)} collective-permute-done((bf16[48,3,2,384]{3,0,1,2:T(8,128)(2,1)S(1)}, bf16[48,3,2,384]{3,0,1,2:T(8,128)(2,1)S(1)}, u32[]{:S(2)}, u32[]{:S(2)}) %collective-permute-start.10) | collective-permute-done | bytes 221216 | tf_op jit(solution)/shard_map/ppermute | solution.py:146
  134.5 1.6 fusion.16
  136.1 4.5 %fusion = f32[384,2,3,3,384]{0,4,2,3,1:T(8,128)} fusion(f32[2,3,384,3,384]{4,2,3,1,0:T(8,128)S(1)} %fusion.16, f32[384,3,3,384]{0,3,1,2:T(8,128)S(1)} %bitcast.113), kind=kLoop, calls=%fused_computation.6 | loop fusion | flops 5308416 | bytes 26542080 | tf_op jit(solution)/shard_map/div | solution.py:164
  140.6 19.7 %copy.59 = f32[384,2,3,3,384]{4,1,3,2,0:T(2,128)} copy(f32[384,2,3,3,384]{0,4,2,3,1:T(8,128)} %fusion) | data formatting | bytes 21233664
  160.3 6.7 %collective-permute-start.5 = (bf16[3,416,384]{2,1,0:T(8,128)(2,1)}, bf16[3,416,384]{2,1,0:T(8,128)(2,1)S(1)}, u32[]{:S(2)}, u32[]{:S(2)}) collective-permute-start(bf16[3,416,384]{2,1,0:T(8,128)(2,1)} %broadcast_select_fusion.1), channel_id=1, source_target_pairs={{0,24},{4,28},{8,0},{12,4},{16,8},{20,12},{24,16},{28,20},{1,25},{... | collective-permute-start | bytes 2875400 | tf_op jit(solution)/shard_map/ppermute | solution.py:79
  167.0 2.3 bitcast_dynamic-update-slice_fusion.6
  169.3 2.3 bitcast_dynamic-update-slice_fusion.5
  171.6 2.3 bitcast_dynamic-update-slice_fusion.4
  173.8 2.3 bitcast_dynamic-update-slice_fusion.3
  176.1 1.0 bitcast_dynamic-update-slice_fusion.2
  177.1 12.3 %collective-permute-done.5 = bf16[3,416,384]{2,1,0:T(8,128)(2,1)S(1)} collective-permute-done((bf16[3,416,384]{2,1,0:T(8,128)(2,1)}, bf16[3,416,384]{2,1,0:T(8,128)(2,1)S(1)}, u32[]{:S(2)}, u32[]{:S(2)}) %collective-permute-start.5) | collective-permute-done | bytes 958496 | tf_op jit(solution)/shard_map/ppermute | solution.py:79
  189.4 1.0 bitcast_dynamic-update-slice_fusion.1
  190.4 9.5 %collective-permute-done.6 = bf16[3,416,384]{2,1,0:T(8,128)(2,1)S(1)} collective-permute-done((bf16[3,416,384]{2,1,0:T(8,128)(2,1)}, bf16[3,416,384]{2,1,0:T(8,128)(2,1)S(1)}, u32[]{:S(2)}, u32[]{:S(2)}) %collective-permute-start.6) | collective-permute-done | bytes 958496 | tf_op jit(solution)/shard_map/ppermute | solution.py:79
  199.9 1.1 bitcast_dynamic-update-slice_fusion
  201.0 7.8 %gather_fusion.2 = bf16[8,3,416,384]{3,2,1,0:T(8,128)(2,1)} fusion(bf16[8,3,416,384]{3,2,1,0:T(8,128)(2,1)} %bitcast_dynamic-update-slice_fusion, s32[1024]{0:T(1024)S(1)} %pad_clamp_fusion.1), kind=kCustom, calls=%fused_computation.2 | custom fusion | bytes 15335456 | tf_op jit(solution)/shard_map/jit(_take)/gather | solution.py:81
  208.8 4.1 %select_bitcast_fusion = bf16[3,8,416,384]{3,2,0,1:T(8,128)(2,1)S(1)} fusion(bf16[8,3,416,384]{3,2,1,0:T(8,128)(2,1)} %gather_fusion.2, pred[8]{0:T(512)(128)(4,1)S(1)} %compare_and_fusion.2), kind=kLoop, calls=%fused_computation.7 | loop fusion | flops 3833856 | bytes 15335432 | tf_op jit(solution)/shard_map/jit(_take)/select_n | solution.py:81
  212.9 3.9 %copy.51 = bf16[3,8,416,384]{3,2,1,0:T(8,128)(2,1)} copy(bf16[3,8,416,384]{3,2,0,1:T(8,128)(2,1)S(1)} %select_bitcast_fusion) | data formatting | bytes 15335424 | tf_op jit(solution)/shard_map/jit(_take)/select_n | solution.py:81
  216.8 13.3 %shard_map.78 = bf16[3,2,128,1152]{3,2,1,0:T(8,128)(2,1)} custom-call(bf16[3,4,128,832]{3,2,1,0:T(8,128)(2,1)} %bitcast.120, bf16[3,3328,384]{2,1,0:T(8,128)(2,1)} %bitcast.114), custom_call_target="tpu_custom_call" | custom-call | flops 5888802816 | bytes 11993088 | tf_op jit(solution)/shard_map/pallas_call | solution.py:46
  230.1 1.6 fusion.37
  234.0 1.4 copy-done.4
  (65 shorter events, 9.7 us)
Async XLA Ops:
  7.2 3.8 %copy-start = (f32[128]{0:T(128)S(1)}, f32[128]{0:T(128)}, u32[]{:S(2)}) copy-start(f32[128]{0:T(128)} %param.9) | copy-start | bytes 1540
  7.2 47.1 %all-gather.4.cloned.1.call-start = ((), (), s32[]{:S(2)}) async-start(), calls=%async_computation | async-start | bytes 1904640 | tf_op jit(solution)/shard_map/all_gather | solution.py:115
  20.1 9.3 %copy-start.6 = (f32[1536]{0:T(1024)S(1)}, f32[1536]{0:T(1024)}, u32[]{:S(2)}) copy-start(f32[1536]{0:T(1024)} %param.10) | copy-start | bytes 18436
  36.2 31.2 %copy-start.5 = (bf16[3,2,128,384]{3,2,1,0:T(8,128)(2,1)S(1)}, bf16[3,2,128,384]{3,2,1,0:T(8,128)(2,1)}, u32[]{:S(2)}) copy-start(bf16[3,2,128,384]{3,2,1,0:T(8,128)(2,1)} %shard_map.77) | copy-start | bytes 1769476
  58.9 101.5 %collective-permute-start = (bf16[3,416,384]{2,1,0:T(8,128)(2,1)}, bf16[3,416,384]{2,1,0:T(8,128)(2,1)}, u32[]{:S(2)}, u32[]{:S(2)}) collective-permute-start(bf16[3,416,384]{2,1,0:T(8,128)(2,1)} %broadcast_select_fusion.1), channel_id=1, source_target_pairs={{0,4},{4,8},{8,12},{12,16},{16,20},{20,24},{24,28},{28,0},{1,5},{5... | collective-permute-start | bytes 2875400 | tf_op jit(solution)/shard_map/ppermute | solution.py:79
  61.4 107.9 %collective-permute-start.1 = (bf16[3,416,384]{2,1,0:T(8,128)(2,1)}, bf16[3,416,384]{2,1,0:T(8,128)(2,1)}, u32[]{:S(2)}, u32[]{:S(2)}) collective-permute-start(bf16[3,416,384]{2,1,0:T(8,128)(2,1)} %broadcast_select_fusion.1), channel_id=1, source_target_pairs={{0,8},{4,12},{8,16},{12,20},{16,24},{20,28},{24,0},{28,4},{1,9},{5... | collective-permute-start | bytes 2875400 | tf_op jit(solution)/shard_map/ppermute | solution.py:79
  63.7 25.4 %collective-permute-start.9 = (bf16[4,29952]{1,0:T(4,128)(2,1)S(1)}, bf16[4,29952]{1,0:T(4,128)(2,1)S(1)}, u32[]{:S(2)}, u32[]{:S(2)}) collective-permute-start(bf16[4,29952]{1,0:T(4,128)(2,1)S(1)} %bitcast.127), channel_id=1, source_target_pairs={{0,12},{4,0},{8,4},{12,8},{1,13},{5,1},{9,5},{13,9},{2,14},{6,2},{... | collective-permute-start | bytes 718856 | tf_op jit(solution)/shard_map/ppermute | solution.py:79
  63.7 45.2 %collective-permute-start.8 = (bf16[4,29952]{1,0:T(4,128)(2,1)S(1)}, bf16[4,29952]{1,0:T(4,128)(2,1)S(1)}, u32[]{:S(2)}, u32[]{:S(2)}) collective-permute-start(bf16[4,29952]{1,0:T(4,128)(2,1)S(1)} %bitcast.128), channel_id=1, source_target_pairs={{0,8},{4,12},{8,0},{12,4},{1,9},{5,13},{9,1},{13,5},{2,10},{6,14},... | collective-permute-start | bytes 718856 | tf_op jit(solution)/shard_map/ppermute | solution.py:79
  64.1 48.9 %collective-permute-start.7 = (bf16[4,29952]{1,0:T(4,128)(2,1)S(1)}, bf16[4,29952]{1,0:T(4,128)(2,1)S(1)}, u32[]{:S(2)}, u32[]{:S(2)}) collective-permute-start(bf16[4,29952]{1,0:T(4,128)(2,1)S(1)} %bitcast.129), channel_id=1, source_target_pairs={{0,4},{4,8},{8,12},{12,0},{1,5},{5,9},{9,13},{13,1},{2,6},{6,10},{... | collective-permute-start | bytes 718856 | tf_op jit(solution)/shard_map/ppermute | solution.py:79
  68.1 44.8 %copy-start.2 = (bf16[3,128,2,1536]{3,2,1,0:T(2,128)(2,1)}, bf16[3,128,2,1536]{3,2,1,0:T(2,128)(2,1)S(1)}, u32[]{:S(2)}) copy-start(bf16[3,128,2,1536]{3,2,1,0:T(2,128)(2,1)S(1)} %copy_dynamic-update-slice_fusion.3) | copy-start | bytes 7077892
  89.1 82.5 %collective-permute-start.2 = (bf16[3,416,384]{2,1,0:T(8,128)(2,1)}, bf16[3,416,384]{2,1,0:T(8,128)(2,1)}, u32[]{:S(2)}, u32[]{:S(2)}) collective-permute-start(bf16[3,416,384]{2,1,0:T(8,128)(2,1)} %broadcast_select_fusion.1), channel_id=1, source_target_pairs={{0,12},{4,16},{8,20},{12,24},{16,28},{20,0},{24,4},{28,8},{1,13},{... | collective-permute-start | bytes 2875400 | tf_op jit(solution)/shard_map/ppermute | solution.py:79
  108.9 64.9 %collective-permute-start.3 = (bf16[3,416,384]{2,1,0:T(8,128)(2,1)}, bf16[3,416,384]{2,1,0:T(8,128)(2,1)}, u32[]{:S(2)}, u32[]{:S(2)}) collective-permute-start(bf16[3,416,384]{2,1,0:T(8,128)(2,1)} %broadcast_select_fusion.1), channel_id=1, source_target_pairs={{0,16},{4,20},{8,24},{12,28},{16,0},{20,4},{24,8},{28,12},{1,17},{... | collective-permute-start | bytes 2875400 | tf_op jit(solution)/shard_map/ppermute | solution.py:79
  122.1 14.0 %slice-start = ((s8[5308416]{0:T(1024)(128)(4,1)}), s8[4194304]{0:T(1024)(128)(4,1)S(1)}, s32[]{:S(2)}) async-start(s8[5308416]{0:T(1024)(128)(4,1)} %bitcast.112), calls=%async_computation.1 | async-start | bytes 8388608
  123.4 11.0 %collective-permute-start.10 = (bf16[48,3,2,384]{3,0,1,2:T(8,128)(2,1)S(1)}, bf16[48,3,2,384]{3,0,1,2:T(8,128)(2,1)S(1)}, u32[]{:S(2)}, u32[]{:S(2)}) collective-permute-start(bf16[48,3,2,384]{3,0,1,2:T(8,128)(2,1)S(1)} %bitcast.123), channel_id=1, source_target_pairs={{0,0},{1,4},{2,8},{3,12},{4,1},{5,5},{6,9},{7,13},{8,2},{9,6},{10,... | collective-permute-start | bytes 663560 | tf_op jit(solution)/shard_map/ppermute | solution.py:146
  134.4 41.7 %collective-permute-start.4 = (bf16[3,416,384]{2,1,0:T(8,128)(2,1)}, bf16[3,416,384]{2,1,0:T(8,128)(2,1)S(1)}, u32[]{:S(2)}, u32[]{:S(2)}) collective-permute-start(bf16[3,416,384]{2,1,0:T(8,128)(2,1)} %broadcast_select_fusion.1), channel_id=1, source_target_pairs={{0,20},{4,24},{8,28},{12,0},{16,4},{20,8},{24,12},{28,16},{1,21},{... | collective-permute-start | bytes 2875400 | tf_op jit(solution)/shard_map/ppermute | solution.py:79
  134.4 1.6 slice-start.1
  160.3 29.1 %collective-permute-start.5 = (bf16[3,416,384]{2,1,0:T(8,128)(2,1)}, bf16[3,416,384]{2,1,0:T(8,128)(2,1)S(1)}, u32[]{:S(2)}, u32[]{:S(2)}) collective-permute-start(bf16[3,416,384]{2,1,0:T(8,128)(2,1)} %broadcast_select_fusion.1), channel_id=1, source_target_pairs={{0,24},{4,28},{8,0},{12,4},{16,8},{20,12},{24,16},{28,20},{1,25},{... | collective-permute-start | bytes 2875400 | tf_op jit(solution)/shard_map/ppermute | solution.py:79
  169.3 30.6 %collective-permute-start.6 = (bf16[3,416,384]{2,1,0:T(8,128)(2,1)}, bf16[3,416,384]{2,1,0:T(8,128)(2,1)S(1)}, u32[]{:S(2)}, u32[]{:S(2)}) collective-permute-start(bf16[3,416,384]{2,1,0:T(8,128)(2,1)} %broadcast_select_fusion.1), channel_id=1, source_target_pairs={{0,28},{4,0},{8,4},{12,8},{16,12},{20,16},{24,20},{28,24},{1,29},{... | collective-permute-start | bytes 2875400 | tf_op jit(solution)/shard_map/ppermute | solution.py:79
  216.8 14.9 %copy-start.3 = (bf16[3,128,2,1536]{3,2,1,0:T(2,128)(2,1)S(1)}, bf16[3,128,2,1536]{3,2,1,0:T(2,128)(2,1)}, u32[]{:S(2)}) copy-start(bf16[3,128,2,1536]{3,2,1,0:T(2,128)(2,1)} %copy-done.2) | copy-start | bytes 7077892
  216.8 18.6 %copy-start.1 = (f32[128]{0:T(128)S(1)}, f32[128]{0:T(128)}, u32[]{:S(2)}) copy-start(f32[128]{0:T(128)} %param.9) | copy-start | bytes 1540
  234.0 1.4 copy-start.4
Sparse Core Ops, SparseCore 0:
  17.5 36.7 all-gather.3

commit v6 on v5

--- a/solution.py
+++ b/solution.py
@@ -112,7 +112,7 @@
     q = lax.axis_index("parts") * n_aux + lax.axis_index("aux")
     piece = lax.dynamic_slice_in_dim(v_local, q * rows_q, rows_q, 0)
     carried = jnp.concatenate([piece, sel_flat.reshape(sel_rows, a_width)], 0)
-    stage1 = lax.all_gather(carried, "pair", axis=0)
+    stage1 = gather_group(carried, ("pair",), (n_pair,))
 
     half = jnp.einsum(
         "kmj,pmn->pkjn", occ_left, cholesky, preferred_element_type=jnp.float32
@@ -132,7 +132,7 @@
     pieces = stage1[:, :rows_q]
     others = (me_pair + jnp.arange(1, n_pair)) % n_pair
     send = jnp.take(pieces, others, axis=0)
-    plane = gather_group(send, ("parts", "aux"), (n_parts, n_aux))
+    plane = lax.all_gather(send, ("parts", "aux"), axis=0)
     v_others = plane.transpose(1, 0, 2, 3).reshape(n_pair - 1, rows, a_width)
     done = transform(half, v_others).transpose(0, 2, 1, 3)
     for step in range(1, n_pair):

time: 243 us -> 158 us (0.65)
  the two profiles are of different devices: /device:TPU:3 before, /device:TPU:6 now
where the time goes in v6:
time: 158 us; the launch traced here: 157 us
  local copies, waits for them, and re-layouts  49.5 us (31%)
  Pallas kernels  23.8 us (15%)
  starting transfers between devices  22.6 us (14%)
  waiting for transfers between devices  16.9 us (11%)
  other arithmetic  16.8 us (11%)
  between operations  16.4 us (10%)
  matrix products  11.1 us (7%)
    pallas_call x3, Pallas kernels, transform(): pl.pallas_call(functools.partial(transform_kernel, n), grid=(b,), in_spec...  23.8 us
    unnamed x22, local copies, waits for them, and re-layouts  21.7 us
    ppermute x1, starting transfers between devices, on_device(): sel_b = lax.ppermute(sel_a, ('aux', 'pair'), perm)  15.3 us
    ppermute x6, waiting for transfers between devices, gather_group(): blocks.append(lax.ppermute(x, axes, perm))  11.1 us
    ppermute x6, starting transfers between devices, gather_group(): blocks.append(lax.ppermute(x, axes, perm))  7.24 us
    transpose x1, local copies, waits for them, and re-layouts, on_device(): v_others = plane.transpose(1, 0, 2, 3).reshape(n_pair - 1, rows, a_width)  7.15 us
    dot_general x1, matrix products, on_device(): jnp.einsum('kmj,pmn->pkjn', occ_left, cholesky, preferred_element_type=jn...  6.42 us
    ppermute x1, waiting for transfers between devices, on_device(): sel_b = lax.ppermute(sel_a, ('aux', 'pair'), perm)  5.8 us
  transfers between devices with their start and end apart: 8, of which 6 were waited for; matrix products, arithmetic and copies ran while one was open for 30% of the time, Pallas kernels for 7%

profile of v6, /device:TPU:6, one launch (start us, length us, event | category | flops | bytes accessed | tf_op | source)
XLA Modules:
  0.0 157.1 jit_solution(18157398009536448397)
XLA Ops:
  7.2 0.7 compare_select_fusion.5
  7.9 0.6 gather_fusion.4
  8.5 0.7 broadcast_select_fusion.2
  9.2 1.2 slice_bitcast_fusion
  10.5 1.2 copy.46
  11.7 0.6 gather_fusion
  12.3 3.0 %fusion.11 = bf16[3,3,4,832]{3,2,0,1:T(4,128)(2,1)S(1)} fusion(bf16[3,832,832]{2,1,0:T(8,128)(2,1)} %param.6, bf16[3,4,832]{2,1,0:T(4,128)(2,1)S(1)} %gather_fusion, pred[3]{0:T(512)(128)(4,1)S(1)} %get-tuple-element.17), kind=kOutput, calls=%fused_computation.16 | convolution fusion | flops 49880064 | bytes 4233219 | tf_op jit(solution)/shard_map/kmi,pmn->pikn/dot_general | solution.py:102
  15.5 1.0 constant_dynamic-slice_fusion
  16.5 0.9 fusion.36
  17.5 2.6 %collective-permute-start.1 = (bf16[494,384]{1,0:T(8,128)(2,1)}, bf16[494,384]{1,0:T(8,128)(2,1)}, u32[]{:S(2)}, u32[]{:S(2)}) collective-permute-start(bf16[494,384]{1,0:T(8,128)(2,1)} %get-tuple-element.26), channel_id=1, source_target_pairs={{0,2},{1,3},{2,0},{3,1},{4,6},{5,7},{6,4},{7,5},{8,10},{9,11},{10,... | collective-permute-start | bytes 1138184 | tf_op jit(solution)/shard_map/ppermute | solution.py:79
  20.1 1.6 %collective-permute-start = (bf16[494,384]{1,0:T(8,128)(2,1)}, bf16[494,384]{1,0:T(8,128)(2,1)}, u32[]{:S(2)}, u32[]{:S(2)}) collective-permute-start(bf16[494,384]{1,0:T(8,128)(2,1)} %get-tuple-element.26), channel_id=1, source_target_pairs={{0,1},{1,2},{2,3},{3,0},{4,5},{5,6},{6,7},{7,4},{8,9},{9,10},{10,1... | collective-permute-start | bytes 1138184 | tf_op jit(solution)/shard_map/ppermute | solution.py:79
  21.6 2.2 %collective-permute-start.2 = (bf16[494,384]{1,0:T(8,128)(2,1)}, bf16[494,384]{1,0:T(8,128)(2,1)}, u32[]{:S(2)}, u32[]{:S(2)}) collective-permute-start(bf16[494,384]{1,0:T(8,128)(2,1)} %get-tuple-element.26), channel_id=1, source_target_pairs={{0,3},{1,0},{2,1},{3,2},{4,7},{5,4},{6,5},{7,6},{8,11},{9,8},{10,9... | collective-permute-start | bytes 1138184 | tf_op jit(solution)/shard_map/ppermute | solution.py:79
  24.0 6.4 %fusion.5 = bf16[4,128,3,832]{1,3,2,0:T(8,128)(2,1)S(1)} fusion(bf16[3,832,832]{2,1,0:T(8,128)(2,1)} %param.6, bf16[2,832,128]{2,1,0:T(8,128)(2,1)S(1)} %get-tuple-element.24, bf16[2,832,128]{2,1,0:T(8,128)(2,1)S(1)} %get-tuple-element.23), kind=kOutput, calls=%fused_computation.12 | convolution fusion | flops 2129494016 | bytes 7561216 | tf_op jit(solution)/shard_map/kmj,pmn->pkjn/dot_general | solution.py:117
  30.4 0.7 fusion.40
  31.2 2.7 %copy.49 = bf16[4,128,3,832]{3,1,0,2:T(8,128)(2,1)} copy(bf16[4,128,3,832]{1,3,2,0:T(8,128)(2,1)S(1)} %fusion.5) | data formatting | bytes 5111808 | tf_op jit(solution)/shard_map/convert_element_type | solution.py:119
  34.0 6.6 %shard_map.77 = bf16[3,2,128,384]{3,2,1,0:T(8,128)(2,1)} custom-call(bf16[3,4,128,832]{3,2,1,0:T(8,128)(2,1)} %bitcast.106, bf16[1,3328,384]{2,1,0:T(8,128)(2,1)} %bitcast.104), custom_call_target="tpu_custom_call" | custom-call | flops 1962934272 | bytes 5701632 | tf_op jit(solution)/shard_map/pallas_call | solution.py:46
  42.7 2.9 %broadcast_subtract_fusion = f32[384,3,3,384]{0,3,1,2:T(8,128)} fusion(f32[384]{0:T(512)S(1)} %get-tuple-element.34, f32[3,3,384]{2,0,1:T(4,128)S(1)} %broadcast_subtract_fusion.1), kind=kLoop, calls=%fused_computation.11 | loop fusion | flops 1327104 | bytes 5323776 | tf_op jit(solution)/shard_map/sub | solution.py:160
  45.6 1.2 collective-permute-done.1
  47.2 1.5 pad_maximum_fusion
  48.7 0.9 gather_fusion.1
  49.9 1.7 %gather_fusion.2 = bf16[3,416,384]{2,1,0:T(8,128)(2,1)} fusion(bf16[4,416,384]{2,1,0:T(8,128)(2,1)S(1)} %slice.46, s32[1024]{0:T(1024)S(1)} %pad_clamp_fusion.1), kind=kCustom, calls=%fused_computation.2 | custom fusion | bytes 1916940 | tf_op jit(solution)/shard_map/jit(_take)/gather | solution.py:134
  51.6 2.4 %bitcast_select_fusion = bf16[1,3,416,384]{3,2,1,0:T(8,128)(2,1)} fusion(bf16[3,416,384]{2,1,0:T(8,128)(2,1)} %gather_fusion.2, pred[3]{0:T(512)(128)(4,1)S(1)} %compare_and_fusion.1), kind=kLoop, calls=%fused_computation.19 | loop fusion | flops 479232 | bytes 1916931 | tf_op jit(solution)/shard_map/jit(_take)/select_n | solution.py:134
  54.2 0.6 collective-permute-start.4
  55.1 1.2 broadcast_in_dim.55
  56.3 0.7 copy_dynamic-update-slice_fusion.3
  57.1 3.3 %collective-permute-done.5 = bf16[4,29952]{1,0:T(4,128)(2,1)S(1)} collective-permute-done((bf16[4,29952]{1,0:T(4,128)(2,1)S(1)}, bf16[4,29952]{1,0:T(4,128)(2,1)S(1)}, u32[]{:S(2)}, u32[]{:S(2)}) %collective-permute-start.5) | collective-permute-done | bytes 239648 | tf_op jit(solution)/shard_map/ppermute | solution.py:79
  60.4 5.2 %collective-permute-done.4 = bf16[4,29952]{1,0:T(4,128)(2,1)S(1)} collective-permute-done((bf16[4,29952]{1,0:T(4,128)(2,1)S(1)}, bf16[4,29952]{1,0:T(4,128)(2,1)S(1)}, u32[]{:S(2)}, u32[]{:S(2)}) %collective-permute-start.4) | collective-permute-done | bytes 239648 | tf_op jit(solution)/shard_map/ppermute | solution.py:79
  65.5 1.0 collective-permute-done.3
  66.6 0.9 pad_maximum_fusion.1
  67.4 1.4 gather_fusion.3
  68.8 0.5 broadcast_select_fusion.1
  69.3 1.2 select_n.179
  70.5 1.1 copy.74
  71.6 4.1 %shard_map.79 = bf16[1,2,144,384]{3,2,1,0:T(8,128)(2,1)} custom-call(bf16[1,4,144,832]{3,2,1,0:T(8,128)(2,1)} %bitcast.102, bf16[1,3328,384]{2,1,0:T(8,128)(2,1)} %bitcast.105), custom_call_target="tpu_custom_call" | custom-call | flops 736100352 | bytes 3735552 | tf_op jit(solution)/shard_map/pallas_call | solution.py:46
  75.7 1.1 copy.56
  76.9 15.3 %collective-permute-start.6 = (bf16[48,3,2,384]{3,0,1,2:T(8,128)(2,1)S(1)}, bf16[48,3,2,384]{3,0,1,2:T(8,128)(2,1)S(1)}, u32[]{:S(2)}, u32[]{:S(2)}) collective-permute-start(bf16[48,3,2,384]{3,0,1,2:T(8,128)(2,1)S(1)} %bitcast.109), channel_id=1, source_target_pairs={{0,0},{1,4},{2,8},{3,12},{4,1},{5,5},{6,9},{7,13},{8,2},{9,6},{10,... | collective-permute-start | bytes 663560 | tf_op jit(solution)/shard_map/ppermute | solution.py:146
  92.3 5.8 %collective-permute-done.6 = bf16[48,3,2,384]{3,0,1,2:T(8,128)(2,1)S(1)} collective-permute-done((bf16[48,3,2,384]{3,0,1,2:T(8,128)(2,1)S(1)}, bf16[48,3,2,384]{3,0,1,2:T(8,128)(2,1)S(1)}, u32[]{:S(2)}, u32[]{:S(2)}) %collective-permute-start.6) | collective-permute-done | bytes 221216 | tf_op jit(solution)/shard_map/ppermute | solution.py:146
  98.1 1.6 %fusion.15 = f32[2,3,384,3,384]{4,2,3,1,0:T(8,128)S(1)} fusion(bf16[96,1,3,384]{3,0,2,1:T(8,128)(2,1)S(1)} %get-tuple-element.32, bf16[96,1,3,384]{3,0,2,1:T(8,128)(2,1)S(1)} %get-tuple-element.31, bf16[48,3,384]{2,0,1:T(8,128)(2,1)S(1)} %get-tuple-element.28, bf16[48,3,384]{2,0,1:T(8,128)(2,1)S(1)} %get-tuple-element.27), kind=kOutput, calls=%fused_computation.28 | convolution fusion | flops 510935040 | bytes 11280384 | tf_op jit(solution)/shard_map/pjb,pcia->bcija/dot_general | solution.py:64
  99.7 4.6 %fusion = f32[384,2,3,3,384]{0,4,2,3,1:T(8,128)} fusion(f32[2,3,384,3,384]{4,2,3,1,0:T(8,128)S(1)} %fusion.15, f32[384,3,3,384]{0,3,1,2:T(8,128)S(1)} %bitcast.99), kind=kLoop, calls=%fused_computation.6 | loop fusion | flops 5308416 | bytes 26542080 | tf_op jit(solution)/shard_map/div | solution.py:164
  104.3 19.8 %copy.59 = f32[384,2,3,3,384]{4,1,3,2,0:T(2,128)} copy(f32[384,2,3,3,384]{0,4,2,3,1:T(8,128)} %fusion) | data formatting | bytes 21233664
  124.1 7.2 %copy.51 = bf16[3,8,416,384]{3,2,1,0:T(8,128)(2,1)} copy(bf16[3,8,416,384]{3,2,0,1:T(8,128)(2,1)} %bitcast.100) | data formatting | bytes 15335424 | tf_op jit(solution)/shard_map/transpose | solution.py:136
  131.2 13.1 %shard_map.78 = bf16[3,2,128,1152]{3,2,1,0:T(8,128)(2,1)} custom-call(bf16[3,4,128,832]{3,2,1,0:T(8,128)(2,1)} %bitcast.107, bf16[3,3328,384]{2,1,0:T(8,128)(2,1)} %bitcast.101), custom_call_target="tpu_custom_call" | custom-call | flops 5888802816 | bytes 11993088 | tf_op jit(solution)/shard_map/pallas_call | solution.py:46
  144.3 1.8 %fusion.37 = (bf16[3,128,2,384]{3,1,2,0:T(8,128)(2,1)S(1)}, bf16[3,128,2,384]{3,1,2,0:T(8,128)(2,1)S(1)}, bf16[3,128,2,384]{3,1,2,0:T(8,128)(2,1)S(1)}) fusion(bf16[3,128,2,1152]{3,1,2,0:T(8,128)(2,1)} %bitcast.108), kind=kLoop, calls=%fused_computation.99 | loop fusion | bytes 3538944 | tf_op jit(solution)/shard_map/slice | solution.py:140
  146.1 0.4 copy-done.3
  146.6 0.7 copy_dynamic-update-slice_fusion.2
  147.3 0.7 copy_dynamic-update-slice_fusion.1
  148.0 0.7 copy_dynamic-update-slice_fusion
  148.8 1.4 copy-done.4
  (52 shorter events, 2.1 us)
Async XLA Ops:
  7.2 0.7 copy-start
  7.2 116.9 %all-gather.2.cloned.1.call-start = ((), (), s32[]{:S(2)}) async-start(), calls=%async_computation | async-start | bytes 8626176 | tf_op jit(solution)/shard_map/all_gather | solution.py:135
  17.5 29.3 %collective-permute-start.1 = (bf16[494,384]{1,0:T(8,128)(2,1)}, bf16[494,384]{1,0:T(8,128)(2,1)}, u32[]{:S(2)}, u32[]{:S(2)}) collective-permute-start(bf16[494,384]{1,0:T(8,128)(2,1)} %get-tuple-element.26), channel_id=1, source_target_pairs={{0,2},{1,3},{2,0},{3,1},{4,6},{5,7},{6,4},{7,5},{8,10},{9,11},{10,... | collective-permute-start | bytes 1138184 | tf_op jit(solution)/shard_map/ppermute | solution.py:79
  20.1 26.7 %collective-permute-start = (bf16[494,384]{1,0:T(8,128)(2,1)}, bf16[494,384]{1,0:T(8,128)(2,1)}, u32[]{:S(2)}, u32[]{:S(2)}) collective-permute-start(bf16[494,384]{1,0:T(8,128)(2,1)} %get-tuple-element.26), channel_id=1, source_target_pairs={{0,1},{1,2},{2,3},{3,0},{4,5},{5,6},{6,7},{7,4},{8,9},{9,10},{10,1... | collective-permute-start | bytes 1138184 | tf_op jit(solution)/shard_map/ppermute | solution.py:79
  21.6 25.6 %collective-permute-start.2 = (bf16[494,384]{1,0:T(8,128)(2,1)}, bf16[494,384]{1,0:T(8,128)(2,1)}, u32[]{:S(2)}, u32[]{:S(2)}) collective-permute-start(bf16[494,384]{1,0:T(8,128)(2,1)} %get-tuple-element.26), channel_id=1, source_target_pairs={{0,3},{1,0},{2,1},{3,2},{4,7},{5,4},{6,5},{7,6},{8,11},{9,8},{10,9... | collective-permute-start | bytes 1138184 | tf_op jit(solution)/shard_map/ppermute | solution.py:79
  31.2 2.7 %copy-start.7 = (f32[1536]{0:T(1024)S(1)}, f32[1536]{0:T(1024)}, u32[]{:S(2)}) copy-start(f32[1536]{0:T(1024)} %param.10) | copy-start | bytes 18436
  42.7 4.6 %copy-start.5 = (bf16[1,494,384]{2,1,0:T(8,128)(2,1)S(1)}, bf16[1,494,384]{2,1,0:T(8,128)(2,1)}, u32[]{:S(2)}) copy-start(bf16[1,494,384]{2,1,0:T(8,128)(2,1)} %get-tuple-element.25) | copy-start | bytes 1138180
  54.0 2.3 %copy-start.6 = (bf16[3,2,128,384]{3,2,1,0:T(8,128)(2,1)S(1)}, bf16[3,2,128,384]{3,2,1,0:T(8,128)(2,1)}, u32[]{:S(2)}) copy-start(bf16[3,2,128,384]{3,2,1,0:T(8,128)(2,1)} %shard_map.77) | copy-start | bytes 1769476
  54.2 6.2 %collective-permute-start.5 = (bf16[4,29952]{1,0:T(4,128)(2,1)S(1)}, bf16[4,29952]{1,0:T(4,128)(2,1)S(1)}, u32[]{:S(2)}, u32[]{:S(2)}) collective-permute-start(bf16[4,29952]{1,0:T(4,128)(2,1)S(1)} %bitcast.114), channel_id=1, source_target_pairs={{0,12},{4,0},{8,4},{12,8},{1,13},{5,1},{9,5},{13,9},{2,14},{6,2},{... | collective-permute-start | bytes 718856 | tf_op jit(solution)/shard_map/ppermute | solution.py:79
  54.2 11.3 %collective-permute-start.4 = (bf16[4,29952]{1,0:T(4,128)(2,1)S(1)}, bf16[4,29952]{1,0:T(4,128)(2,1)S(1)}, u32[]{:S(2)}, u32[]{:S(2)}) collective-permute-start(bf16[4,29952]{1,0:T(4,128)(2,1)S(1)} %bitcast.115), channel_id=1, source_target_pairs={{0,8},{4,12},{8,0},{12,4},{1,9},{5,13},{9,1},{13,5},{2,10},{6,14},... | collective-permute-start | bytes 718856 | tf_op jit(solution)/shard_map/ppermute | solution.py:79
  54.8 11.7 %collective-permute-start.3 = (bf16[4,29952]{1,0:T(4,128)(2,1)S(1)}, bf16[4,29952]{1,0:T(4,128)(2,1)S(1)}, u32[]{:S(2)}, u32[]{:S(2)}) collective-permute-start(bf16[4,29952]{1,0:T(4,128)(2,1)S(1)} %bitcast.116), channel_id=1, source_target_pairs={{0,4},{4,8},{8,12},{12,0},{1,5},{5,9},{9,13},{13,1},{2,6},{6,10},{... | collective-permute-start | bytes 718856 | tf_op jit(solution)/shard_map/ppermute | solution.py:79
  57.1 9.5 %copy-start.2 = (bf16[3,128,2,1536]{3,2,1,0:T(2,128)(2,1)}, bf16[3,128,2,1536]{3,2,1,0:T(2,128)(2,1)S(1)}, u32[]{:S(2)}) copy-start(bf16[3,128,2,1536]{3,2,1,0:T(2,128)(2,1)S(1)} %copy_dynamic-update-slice_fusion.3) | copy-start | bytes 7077892
  76.9 21.2 %collective-permute-start.6 = (bf16[48,3,2,384]{3,0,1,2:T(8,128)(2,1)S(1)}, bf16[48,3,2,384]{3,0,1,2:T(8,128)(2,1)S(1)}, u32[]{:S(2)}, u32[]{:S(2)}) collective-permute-start(bf16[48,3,2,384]{3,0,1,2:T(8,128)(2,1)S(1)} %bitcast.109), channel_id=1, source_target_pairs={{0,0},{1,4},{2,8},{3,12},{4,1},{5,5},{6,9},{7,13},{8,2},{9,6},{10,... | collective-permute-start | bytes 663560 | tf_op jit(solution)/shard_map/ppermute | solution.py:146
  92.2 7.5 %slice-start = ((s8[5308416]{0:T(1024)(128)(4,1)}), s8[4194304]{0:T(1024)(128)(4,1)S(1)}, s32[]{:S(2)}) async-start(s8[5308416]{0:T(1024)(128)(4,1)} %bitcast.98), calls=%async_computation.1 | async-start | bytes 8388608
  98.1 1.6 %slice-start.1 = ((s8[5308416]{0:T(1024)(128)(4,1)}), s8[1114112]{0:T(1024)(128)(4,1)S(1)}, s32[]{:S(2)}) async-start(s8[5308416]{0:T(1024)(128)(4,1)} %bitcast.98), calls=%async_computation.2 | async-start | bytes 2228224
  144.3 2.2 %copy-start.3 = (bf16[3,128,2,1536]{3,2,1,0:T(2,128)(2,1)S(1)}, bf16[3,128,2,1536]{3,2,1,0:T(2,128)(2,1)}, u32[]{:S(2)}) copy-start(bf16[3,128,2,1536]{3,2,1,0:T(2,128)(2,1)} %copy-done.2) | copy-start | bytes 7077892
  144.3 5.9 %copy-start.1 = (f32[128]{0:T(128)S(1)}, f32[128]{0:T(128)}, u32[]{:S(2)}) copy-start(f32[128]{0:T(128)} %param.9) | copy-start | bytes 1540
  148.8 1.4 copy-start.4
Sparse Core Ops, SparseCore 0:
  54.1 61.7 all-gather.1

commit v7 on v3

--- a/solution.py
+++ b/solution.py
@@ -102,9 +102,9 @@
     half_sel = jnp.einsum(
         "kmi,pmn->pikn", occ_sel, cholesky, preferred_element_type=jnp.float32
     ).astype(jnp.bfloat16)
-    half_sel = half_sel.reshape(vectors * batch * 4, orbitals)
-    gathered = gather_group(half_sel, ("aux", "pair"), (n_aux, n_pair))
-    count = gathered.shape[0] * vectors
+    by_pair = gather_group(half_sel, ("pair",), (n_pair,))
+    gathered = gather_group(by_pair, ("aux",), (n_aux,))
+    count = n_aux * n_pair * vectors
     half_rows = gathered.reshape(count * batch, 4, orbitals).transpose(1, 0, 2)
     sel_own = transform(half_rows[None], v_local[None])
     sel_own = sel_own.reshape(2, count, batch, a_width)
@@ -113,15 +113,12 @@
     rows_q = rows // n_q
     q = lax.axis_index("parts") * n_aux + lax.axis_index("aux")
     piece = lax.dynamic_slice_in_dim(v_local, q * rows_q, rows_q, 0)
-    stage1 = lax.all_gather(piece, "pair", axis=0)
+    v_full = lax.all_gather(piece, ("pair", "parts", "aux"), axis=0, tiled=True)
+    v_full = v_full.reshape(n_pair, rows, a_width)
     half = jnp.einsum(
         "kmj,pmn->pkjn", occ_left, cholesky, preferred_element_type=jnp.float32
     ).astype(jnp.bfloat16)
-    stage1, half = lax.optimization_barrier((stage1, half))
-    stage2 = lax.all_gather(stage1, ("parts", "aux"), axis=1)
-    v_full = stage2.reshape(n_pair, rows, a_width)
-    full = transform(half, v_full)
-    pair_vectors = full.transpose(0, 2, 1, 3)
+    pair_vectors = transform(half, v_full).transpose(0, 2, 1, 3)
 
     sel_a = sel_own.transpose(1, 2, 0, 3)
     if n_aux == n_pair:

time: 161 us -> 142 us (0.88); the launches traced: 158 us -> 142 us
  starting transfers between devices: 25.3 us -> 12.9 us
  waiting for transfers between devices: 41.5 us -> 32.4 us
  other arithmetic: 9.05 us -> 13.9 us
    all_gather x2 -> x1, waiting for transfers between devices: 23.1 us -> 0.01 us  [on_device(): v_full = lax.all_gather(piece, ('pair', 'parts', 'aux'), axis=0, tiled=True)]
    ppermute x15 -> x6, starting transfers between devices: 23 us -> 4.56 us  [gather_group(): blocks.append(lax.ppermute(x, axes, perm))]
    ppermute x1, waiting for transfers between devices: 11.5 us -> 21.2 us  [on_device(): sel_b = lax.ppermute(sel_a, ('aux', 'pair'), perm)]
    ppermute x1, starting transfers between devices: 2.24 us -> 8.31 us  [on_device(): sel_b = lax.ppermute(sel_a, ('aux', 'pair'), perm)]
    ppermute x15 -> x6, waiting for transfers between devices: 6.89 us -> 11.2 us  [gather_group(): blocks.append(lax.ppermute(x, axes, perm))]
    another operation x0 -> x2, other arithmetic: none -> 3.25 us  [gather_group(): stacked = jnp.stack(blocks, 0)]
    unnamed x31 -> x16, local copies, waits for them, and re-layouts: 26.4 us -> 25.3 us
  transfers between devices with their start and end apart: 18 -> 8, of which waited for: 6 -> 4; matrix products, arithmetic and copies ran while one was open for 30% -> 38% of each run, Pallas kernels for 3% -> 3%
where the time goes in v7:
time: 142 us
  local copies, waits for them, and re-layouts  36.3 us (26%)
  waiting for transfers between devices  32.4 us (23%)
  Pallas kernels  20.5 us (14%)
  between operations  14.3 us (10%)
  other arithmetic  13.9 us (10%)
  starting transfers between devices  12.9 us (9%)
  matrix products  11.2 us (8%)
    unnamed x16, local copies, waits for them, and re-layouts  25.3 us
    ppermute x1, waiting for transfers between devices, on_device(): sel_b = lax.ppermute(sel_a, ('aux', 'pair'), perm)  21.2 us
    pallas_call x2, Pallas kernels, transform(): pl.pallas_call(functools.partial(transform_kernel, n), grid=(b,), in_spec...  20.5 us
    ppermute x6, waiting for transfers between devices, gather_group(): blocks.append(lax.ppermute(x, axes, perm))  11.2 us
    ppermute x1, starting transfers between devices, on_device(): sel_b = lax.ppermute(sel_a, ('aux', 'pair'), perm)  8.31 us
    dot_general x1, matrix products, on_device(): jnp.einsum('kmj,pmn->pkjn', occ_left, cholesky, preferred_element_type=jn...  6.55 us
    div x1, other arithmetic, on_device(): amplitudes = paired / denominator  4.58 us
    ppermute x6, starting transfers between devices, gather_group(): blocks.append(lax.ppermute(x, axes, perm))  4.56 us
  transfers between devices with their start and end apart: 8, of which 4 were waited for; matrix products, arithmetic and copies ran while one was open for 38% of the time, Pallas kernels for 3%

profile of v7, /device:TPU:29, one launch (start us, length us, event | category | flops | bytes accessed | tf_op | source)
XLA Modules:
  0.0 141.5 jit_solution(5754915281273597627)
XLA Ops:
  7.2 0.0 copy-start
  7.2 0.0 all-gather.2.cloned.1.call-start
  7.2 1.7 %constant_dynamic-slice_fusion = bf16[416,384]{1,0:T(8,128)(2,1)} fusion(bf16[3328,384]{1,0:T(8,128)(2,1)} %bitcast.88, s32[]{:T(128)S(6)} %select_n.110), kind=kLoop, calls=%fused_computation.73 | loop fusion | bytes 638980 | tf_op jit(solution)/shard_map/dynamic_slice | solution.py:115
  9.0 0.0 all-gather.2.cloned.1.call-update
  9.0 1.2 slice_bitcast_fusion
  10.2 0.1 pad_maximum_fusion.1
  10.3 1.2 copy.28
  11.5 0.0 copy-start.3
  11.6 0.6 gather_fusion
  12.2 0.6 gather_fusion.3
  12.8 3.0 %fusion.8 = bf16[4,3,3,832]{3,0,2,1:T(4,128)(2,1)S(1)} fusion(bf16[3,832,832]{2,1,0:T(8,128)(2,1)} %param.6, bf16[3,4,832]{2,1,0:T(4,128)(2,1)S(1)} %gather_fusion, pred[3]{0:T(512)(128)(4,1)S(1)} %get-tuple-element.9), kind=kOutput, calls=%fused_computation.12 | convolution fusion | flops 49880064 | bytes 4233219 | tf_op jit(solution)/shard_map/kmi,pmn->pikn/dot_general | solution.py:102
  15.9 0.1 collective-permute-start
  15.9 1.3 collective-permute-start.1
  17.3 0.2 collective-permute-start.2
  17.5 0.1 fusion.31
  17.6 0.1 broadcast_add_fusion
  17.7 0.1 broadcast_subtract_fusion.1
  17.7 2.9 %broadcast_subtract_fusion = f32[384,3,3,384]{0,3,1,2:T(8,128)} fusion(f32[384]{0:T(512)S(1)} %get-tuple-element.19, f32[3,3,384]{2,0,1:T(4,128)S(1)} %broadcast_subtract_fusion.1), kind=kLoop, calls=%fused_computation.10 | loop fusion | flops 1327104 | bytes 5323776 | tf_op jit(solution)/shard_map/sub | solution.py:140
  20.6 6.6 %fusion.5 = bf16[4,128,3,832]{1,3,2,0:T(8,128)(2,1)S(1)} fusion(bf16[3,832,832]{2,1,0:T(8,128)(2,1)} %param.6, bf16[2,832,128]{2,1,0:T(8,128)(2,1)S(1)} %get-tuple-element.11, bf16[2,832,128]{2,1,0:T(8,128)(2,1)S(1)} %get-tuple-element.10), kind=kOutput, calls=%fused_computation.11 | convolution fusion | flops 2129494016 | bytes 7561216 | tf_op jit(solution)/shard_map/kmj,pmn->pkjn/dot_general | solution.py:118
  27.2 0.0 collective-permute-done
  27.2 1.1 pad_maximum_fusion.2
  28.4 0.8 gather_fusion.1
  29.1 0.2 broadcast_select_fusion
  29.3 2.5 %collective-permute-start.3 = (bf16[4,3,3,4,832]{4,3,1,2,0:T(4,128)(2,1)S(1)}, bf16[4,3,3,4,832]{4,3,1,2,0:T(4,128)(2,1)S(1)}, u32[]{:S(2)}, u32[]{:S(2)}) collective-permute-start(bf16[4,3,3,4,832]{4,3,1,2,0:T(4,128)(2,1)S(1)} %broadcast_select_fusion), channel_id=1, source_target_pairs={{0,4},{4,8},{8,12},{12,0},{1,5},{5,9},{9,13},{13,1},{2,6},{6,10},{... | collective-permute-start | bytes 718856 | tf_op jit(solution)/shard_map/ppermute | solution.py:79
  31.8 0.3 collective-permute-start.4
  32.1 0.2 collective-permute-start.5
  32.3 0.1 broadcast_in_dim.50
  32.4 0.1 broadcast_in_dim.51
  32.5 2.8 %copy.27 = bf16[4,128,3,832]{3,1,0,2:T(8,128)(2,1)} copy(bf16[4,128,3,832]{1,3,2,0:T(8,128)(2,1)S(1)} %fusion.5) | data formatting | bytes 5111808 | tf_op jit(solution)/shard_map/convert_element_type | solution.py:120
  35.3 0.2 bitcast_select_fusion
  35.5 1.8 %collective-permute-done.3 = bf16[4,3,3,4,832]{4,3,1,2,0:T(4,128)(2,1)S(1)} collective-permute-done((bf16[4,3,3,4,832]{4,3,1,2,0:T(4,128)(2,1)S(1)}, bf16[4,3,3,4,832]{4,3,1,2,0:T(4,128)(2,1)S(1)}, u32[]{:S(2)}, u32[]{:S(2)}) %collective-permute-start.3) | collective-permute-done | bytes 239648 | tf_op jit(solution)/shard_map/ppermute | solution.py:79
  37.3 7.5 %collective-permute-done.4 = bf16[4,3,3,4,832]{4,3,1,2,0:T(4,128)(2,1)} collective-permute-done((bf16[4,3,3,4,832]{4,3,1,2,0:T(4,128)(2,1)S(1)}, bf16[4,3,3,4,832]{4,3,1,2,0:T(4,128)(2,1)}, u32[]{:S(2)}, u32[]{:S(2)}) %collective-permute-start.4) | collective-permute-done | bytes 239648 | tf_op jit(solution)/shard_map/ppermute | solution.py:79
  44.8 1.8 %collective-permute-done.5 = bf16[4,3,3,4,832]{4,3,1,2,0:T(4,128)(2,1)} collective-permute-done((bf16[4,3,3,4,832]{4,3,1,2,0:T(4,128)(2,1)S(1)}, bf16[4,3,3,4,832]{4,3,1,2,0:T(4,128)(2,1)}, u32[]{:S(2)}, u32[]{:S(2)}) %collective-permute-start.5) | collective-permute-done | bytes 239648 | tf_op jit(solution)/shard_map/ppermute | solution.py:79
  46.6 2.1 %pad_maximum_fusion = bf16[4,4,3,3,4,832]{5,4,2,3,1,0:T(4,128)(2,1)S(1)} fusion(bf16[1,4,3,3,4,832]{5,4,2,3,1,0:T(4,128)(2,1)} %bitcast.22, bf16[1,4,3,3,4,832]{5,4,2,3,1,0:T(4,128)(2,1)} %bitcast.21, bf16[1,4,3,3,4,832]{5,4,2,3,1,0:T(4,128)(2,1)} %bitcast.96, bf16[1,4,3,3,4,832]{5,4,2,3,1,0:T(4,128)(2,1)S(1)} %bitcast_select_fusion), kind=kLoop, calls=%fused_computation.13 | loop fusion | flops 1437696 | bytes 1916928 | tf_op jit(solution)/shard_map/stack | solution.py:80
  48.8 1.5 %gather_fusion.2 = bf16[4,4,3,3,4,832]{5,4,2,3,1,0:T(4,128)(2,1)S(1)} fusion(bf16[4,4,3,3,4,832]{5,4,2,3,1,0:T(4,128)(2,1)S(1)} %pad_maximum_fusion, s32[1024]{0:T(1024)S(1)} %pad_clamp_fusion), kind=kCustom, calls=%fused_computation.2 | custom fusion | bytes 1916944 | tf_op jit(solution)/shard_map/jit(_take)/gather | solution.py:81
  50.3 0.4 copy.29
  50.6 1.2 fusion.11.h_ref
  51.8 4.1 %shard_map.78 = bf16[1,2,144,384]{3,2,1,0:T(8,128)(2,1)} custom-call(bf16[1,4,144,832]{3,2,1,0:T(8,128)(2,1)} %fusion.11.h_ref, bf16[1,3328,384]{2,1,0:T(8,128)(2,1)} %bitcast.89), custom_call_target="tpu_custom_call" | custom-call | flops 736100352 | bytes 3735552 | tf_op jit(solution)/shard_map/pallas_call | solution.py:46
  55.9 1.1 copy.31
  57.1 8.3 %collective-permute-start.6 = (bf16[48,3,2,384]{3,0,1,2:T(8,128)(2,1)S(1)}, bf16[48,3,2,384]{3,0,1,2:T(8,128)(2,1)S(1)}, u32[]{:S(2)}, u32[]{:S(2)}) collective-permute-start(bf16[48,3,2,384]{3,0,1,2:T(8,128)(2,1)S(1)} %bitcast.92), channel_id=1, source_target_pairs={{0,0},{1,4},{2,8},{3,12},{4,1},{5,5},{6,9},{7,13},{8,2},{9,6},{10,... | collective-permute-start | bytes 663560 | tf_op jit(solution)/shard_map/ppermute | solution.py:126
  65.4 0.0 slice-start
  65.5 21.2 %collective-permute-done.6 = bf16[48,3,2,384]{3,0,1,2:T(8,128)(2,1)S(1)} collective-permute-done((bf16[48,3,2,384]{3,0,1,2:T(8,128)(2,1)S(1)}, bf16[48,3,2,384]{3,0,1,2:T(8,128)(2,1)S(1)}, u32[]{:S(2)}, u32[]{:S(2)}) %collective-permute-start.6) | collective-permute-done | bytes 221216 | tf_op jit(solution)/shard_map/ppermute | solution.py:126
  86.8 0.0 slice-start.1
  86.8 1.6 %fusion.13 = f32[2,3,384,3,384]{4,2,3,1,0:T(8,128)S(1)} fusion(bf16[96,1,3,384]{3,0,2,1:T(8,128)(2,1)S(1)} %get-tuple-element.17, bf16[96,1,3,384]{3,0,2,1:T(8,128)(2,1)S(1)} %get-tuple-element.16, bf16[48,3,384]{2,0,1:T(8,128)(2,1)S(1)} %get-tuple-element.13, bf16[48,3,384]{2,0,1:T(8,128)(2,1)S(1)} %get-tuple-element.12), kind=kOutput, calls=%fused_computation.19 | convolution fusion | flops 510935040 | bytes 11280384 | tf_op jit(solution)/shard_map/pjb,pcia->bcija/dot_general | solution.py:64
  88.4 4.6 %fusion = f32[384,2,3,3,384]{0,4,2,3,1:T(8,128)} fusion(f32[2,3,384,3,384]{4,2,3,1,0:T(8,128)S(1)} %fusion.13, f32[384,3,3,384]{0,3,1,2:T(8,128)S(1)} %bitcast.86), kind=kLoop, calls=%fused_computation.5 | loop fusion | flops 5308416 | bytes 26542080 | tf_op jit(solution)/shard_map/div | solution.py:144
  93.0 19.8 %copy.35 = f32[384,2,3,3,384]{4,1,3,2,0:T(2,128)} copy(f32[384,2,3,3,384]{0,4,2,3,1:T(8,128)} %fusion) | data formatting | bytes 21233664
  112.7 16.4 %shard_map.77 = bf16[3,2,128,1536]{3,2,1,0:T(8,128)(2,1)} custom-call(bf16[3,4,128,832]{3,2,1,0:T(8,128)(2,1)} %bitcast.90, bf16[4,3328,384]{2,1,0:T(8,128)(2,1)} %bitcast.102), custom_call_target="tpu_custom_call" | custom-call | flops 7851737088 | bytes 15138816 | tf_op jit(solution)/shard_map/pallas_call | solution.py:46
  129.2 5.5 %copy.34 = bf16[3,128,2,1536]{3,2,1,0:T(2,128)(2,1)} copy(bf16[3,128,2,1536]{3,1,2,0:T(8,128)(2,1)} %bitcast.91) | data formatting | bytes 4718592
  (28 shorter events, 0.3 us)
Async XLA Ops:
  7.2 5.0 %copy-start = (f32[128]{0:T(128)S(1)}, f32[128]{0:T(128)}, u32[]{:S(2)}) copy-start(f32[128]{0:T(128)} %param.9) | copy-start | bytes 1540
  7.2 4.3 %copy-start.4 = (s32[3]{0:T(128)S(1)}, s32[3]{0:T(128)}, u32[]{:S(2)}) copy-start(s32[3]{0:T(128)} %param.11) | copy-start | bytes 40
  7.2 105.5 %all-gather.2.cloned.1.call-start = ((), (), s32[]{:S(2)}) async-start(), calls=%async_computation | async-start | bytes 10543104 | tf_op jit(solution)/shard_map/all_gather | solution.py:116
  11.5 6.0 %copy-start.3 = (f32[1536]{0:T(1024)S(1)}, f32[1536]{0:T(1024)}, u32[]{:S(2)}) copy-start(f32[1536]{0:T(1024)} %param.10) | copy-start | bytes 18436
  15.9 11.4 %collective-permute-start = (bf16[3,3,4,832]{3,2,0,1:T(4,128)(2,1)S(1)}, bf16[3,3,4,832]{3,2,0,1:T(4,128)(2,1)S(1)}, u32[]{:S(2)}, u32[]{:S(2)}) collective-permute-start(bf16[3,3,4,832]{3,2,0,1:T(4,128)(2,1)S(1)} %bitcast.97), channel_id=1, source_target_pairs={{0,1},{1,2},{2,3},{3,0},{4,5},{5,6},{6,7},{7,4},{8,9},{9,10},{10,1... | collective-permute-start | bytes 179720 | tf_op jit(solution)/shard_map/ppermute | solution.py:79
  15.9 11.3 %collective-permute-start.1 = (bf16[3,3,4,832]{3,2,0,1:T(4,128)(2,1)S(1)}, bf16[3,3,4,832]{3,2,0,1:T(4,128)(2,1)}, u32[]{:S(2)}, u32[]{:S(2)}) collective-permute-start(bf16[3,3,4,832]{3,2,0,1:T(4,128)(2,1)S(1)} %bitcast.98), channel_id=1, source_target_pairs={{0,2},{1,3},{2,0},{3,1},{4,6},{5,7},{6,4},{7,5},{8,10},{9,11},{10,... | collective-permute-start | bytes 179720 | tf_op jit(solution)/shard_map/ppermute | solution.py:79
  17.3 10.0 %collective-permute-start.2 = (bf16[3,3,4,832]{3,2,0,1:T(4,128)(2,1)S(1)}, bf16[3,3,4,832]{3,2,0,1:T(4,128)(2,1)}, u32[]{:S(2)}, u32[]{:S(2)}) collective-permute-start(bf16[3,3,4,832]{3,2,0,1:T(4,128)(2,1)S(1)} %bitcast.99), channel_id=1, source_target_pairs={{0,3},{1,0},{2,1},{3,2},{4,7},{5,4},{6,5},{7,6},{8,11},{9,8},{10,9... | collective-permute-start | bytes 179720 | tf_op jit(solution)/shard_map/ppermute | solution.py:79
  29.3 8.0 %collective-permute-start.3 = (bf16[4,3,3,4,832]{4,3,1,2,0:T(4,128)(2,1)S(1)}, bf16[4,3,3,4,832]{4,3,1,2,0:T(4,128)(2,1)S(1)}, u32[]{:S(2)}, u32[]{:S(2)}) collective-permute-start(bf16[4,3,3,4,832]{4,3,1,2,0:T(4,128)(2,1)S(1)} %broadcast_select_fusion), channel_id=1, source_target_pairs={{0,4},{4,8},{8,12},{12,0},{1,5},{5,9},{9,13},{13,1},{2,6},{6,10},{... | collective-permute-start | bytes 718856 | tf_op jit(solution)/shard_map/ppermute | solution.py:79
  31.8 13.0 %collective-permute-start.4 = (bf16[4,3,3,4,832]{4,3,1,2,0:T(4,128)(2,1)S(1)}, bf16[4,3,3,4,832]{4,3,1,2,0:T(4,128)(2,1)}, u32[]{:S(2)}, u32[]{:S(2)}) collective-permute-start(bf16[4,3,3,4,832]{4,3,1,2,0:T(4,128)(2,1)S(1)} %broadcast_select_fusion), channel_id=1, source_target_pairs={{0,8},{4,12},{8,0},{12,4},{1,9},{5,13},{9,1},{13,5},{2,10},{6,14},... | collective-permute-start | bytes 718856 | tf_op jit(solution)/shard_map/ppermute | solution.py:79
  32.1 14.5 %collective-permute-start.5 = (bf16[4,3,3,4,832]{4,3,1,2,0:T(4,128)(2,1)S(1)}, bf16[4,3,3,4,832]{4,3,1,2,0:T(4,128)(2,1)}, u32[]{:S(2)}, u32[]{:S(2)}) collective-permute-start(bf16[4,3,3,4,832]{4,3,1,2,0:T(4,128)(2,1)S(1)} %broadcast_select_fusion), channel_id=1, source_target_pairs={{0,12},{4,0},{8,4},{12,8},{1,13},{5,1},{9,5},{13,9},{2,14},{6,2},{... | collective-permute-start | bytes 718856 | tf_op jit(solution)/shard_map/ppermute | solution.py:79
  37.3 9.4 %copy-start.2 = (bf16[4,3,3,4,832]{4,3,1,2,0:T(4,128)(2,1)}, bf16[4,3,3,4,832]{4,3,1,2,0:T(4,128)(2,1)S(1)}, u32[]{:S(2)}) copy-start(bf16[4,3,3,4,832]{4,3,1,2,0:T(4,128)(2,1)S(1)} %collective-permute-done.3) | copy-start | bytes 718852
  57.1 29.7 %collective-permute-start.6 = (bf16[48,3,2,384]{3,0,1,2:T(8,128)(2,1)S(1)}, bf16[48,3,2,384]{3,0,1,2:T(8,128)(2,1)S(1)}, u32[]{:S(2)}, u32[]{:S(2)}) collective-permute-start(bf16[48,3,2,384]{3,0,1,2:T(8,128)(2,1)S(1)} %bitcast.92), channel_id=1, source_target_pairs={{0,0},{1,4},{2,8},{3,12},{4,1},{5,5},{6,9},{7,13},{8,2},{9,6},{10,... | collective-permute-start | bytes 663560 | tf_op jit(solution)/shard_map/ppermute | solution.py:126
  65.4 22.9 %slice-start = ((s8[5308416]{0:T(1024)(128)(4,1)}), s8[4194304]{0:T(1024)(128)(4,1)S(1)}, s32[]{:S(2)}) async-start(s8[5308416]{0:T(1024)(128)(4,1)} %bitcast.85), calls=%async_computation.1 | async-start | bytes 8388608
  86.8 1.6 %slice-start.1 = ((s8[5308416]{0:T(1024)(128)(4,1)}), s8[1114112]{0:T(1024)(128)(4,1)S(1)}, s32[]{:S(2)}) async-start(s8[5308416]{0:T(1024)(128)(4,1)} %bitcast.85), calls=%async_computation.2 | async-start | bytes 2228224
  112.7 21.9 %copy-start.1 = (f32[128]{0:T(128)S(1)}, f32[128]{0:T(128)}, u32[]{:S(2)}) copy-start(f32[128]{0:T(128)} %param.9) | copy-start | bytes 1540
Sparse Core Ops, SparseCore 0:
  10.9 92.1 all-gather.1

commit v8 on v7

v8 whole, which is shorter than its diff:
```python
import functools

import jax
import jax.numpy as jnp
from jax import lax
from jax.experimental import pallas as pl
from jax.experimental.pallas import tpu as pltpu
from jax.sharding import PartitionSpec as P


def transform_kernel(orbitals, flag_ref, h_ref, a_ref, b_ref, o_ref):
    pn, _, m, n = h_ref.shape
    terms = [None] * 4
    for s in range(2):
        hr = h_ref[:, s].reshape(pn * m, n)
        hi = h_ref[:, 2 + s].reshape(pn * m, n)
        va = a_ref[0, s * orbitals:(s + 1) * orbitals, :]
        vb = b_ref[0, s * orbitals:(s + 1) * orbitals, :]
        parts = (hr, va), (hi, vb), (hr, vb), (hi, va)
        for t, (x, y) in enumerate(parts):
            d = jnp.dot(x, y, preferred_element_type=jnp.float32)
            terms[t] = d if terms[t] is None else terms[t] + d
    straight = flag_ref[0] == 0
    real = jnp.where(straight, terms[0] - terms[1], terms[2] - terms[3])
    imag = jnp.where(straight, terms[2] + terms[3], terms[0] + terms[1])
    w = real.shape[1]
    o_ref[:, 0] = real.reshape(pn, m, w).astype(o_ref.dtype)
    o_ref[:, 1] = imag.reshape(pn, m, w).astype(o_ref.dtype)


def transform(half, a_blocks, b_blocks, flag):
    pn, _, m, n = half.shape
    b, rows, w = a_blocks.shape
    flag = jnp.asarray(flag, jnp.int32).reshape(1)
    if w % 128 != 0:
        va = a_blocks.reshape(b, 2, n, w)
        vb = b_blocks.reshape(b, 2, n, w)
        hr, hi = half[:, :2], half[:, 2:]
        dims = "pskn,bsnw->pkbw"
        t0 = jnp.einsum(dims, hr, va, preferred_element_type=jnp.float32)
        t1 = jnp.einsum(dims, hi, vb, preferred_element_type=jnp.float32)
        t2 = jnp.einsum(dims, hr, vb, preferred_element_type=jnp.float32)
        t3 = jnp.einsum(dims, hi, va, preferred_element_type=jnp.float32)
        straight = flag[0] == 0
        real = jnp.where(straight, t0 - t1, t2 - t3)
        imag = jnp.where(straight, t2 + t3, t0 + t1)
        out = jnp.stack([real, imag], 1).astype(jnp.bfloat16)
        return out.reshape(pn, 2, m, b * w)
    flops = 16 * pn * m * n * w * b
    bytes_accessed = 2 * (half.size + 2 * a_blocks.size + pn * 2 * m * b * w)
    return pl.pallas_call(
        functools.partial(transform_kernel, n),
        grid=(b,),
        in_specs=[
            pl.BlockSpec(memory_space=pltpu.SMEM),
            pl.BlockSpec((pn, 4, m, n), lambda i: (0, 0, 0, 0)),
            pl.BlockSpec((1, rows, w), lambda i: (i, 0, 0)),
            pl.BlockSpec((1, rows, w), lambda i: (i, 0, 0)),
        ],
        out_specs=pl.BlockSpec((pn, 2, m, w), lambda i: (0, 0, 0, i)),
        out_shape=jax.ShapeDtypeStruct((pn, 2, m, b * w), jnp.bfloat16),
        cost_estimate=pl.CostEstimate(flops=flops, bytes_accessed=bytes_accessed, transcendentals=0),
    )(flag, half, a_blocks, b_blocks)


def pair_terms(batch_rows, column_rows):
    left = jnp.concatenate([batch_rows[:, :, 0, :], batch_rows[:, :, 1, :]], 0)
    real_right = jnp.concatenate([column_rows[:, :, 0, :], -column_rows[:, :, 1, :]], 0)
    imag_right = jnp.concatenate([column_rows[:, :, 1, :], column_rows[:, :, 0, :]], 0)
    right = jnp.stack([real_right, imag_right], 1)
    return jnp.einsum("pjb,pcia->bcija", left, right, preferred_element_type=jnp.float32)


def gather_group(x, axes, sizes):
    n = 1
    for size in sizes:
        n *= size
    if n > 16:
        return lax.all_gather(x, axes, axis=0)
    me = lax.axis_index(axes[0])
    for name, size in zip(axes[1:], sizes[1:]):
        me = me * size + lax.axis_index(name)
    blocks = [x]
    for shift in range(1, n):
        perm = [(i, (i + shift) % n) for i in range(n)]
        blocks.append(lax.ppermute(x, axes, perm))
    stacked = jnp.stack(blocks, 0)
    return jnp.take(stacked, (me - jnp.arange(n)) % n, axis=0)


AUX = ("x", "core")


def on_device(cholesky, occ_coef, vir_coef, occ_energy, vir_energy, batch_occ):
    vectors = cholesky.shape[0]
    orbitals = cholesky.shape[1]
    occupied = occ_coef.shape[3]
    a_width = vir_coef.shape[3]
    n_pair = lax.axis_size("pair")
    n_core = lax.axis_size("core")
    n_aux = lax.axis_size("x") * n_core
    aux_index = lax.axis_index("x") * n_core + lax.axis_index("core")
    n_parts = lax.axis_size("parts")
    rows = 4 * orbitals
    virtuals = n_pair * a_width
    b_width = virtuals // n_aux
    per_b = b_width // a_width
    batch = batch_occ.shape[0]

    occ_left = jnp.concatenate([occ_coef[0], -occ_coef[1]], 0)
    v_local = vir_coef.reshape(rows, a_width)

    occ_sel = jnp.take(occ_left, batch_occ, axis=2)
    half_sel = jnp.einsum(
        "kmi,pmn->pikn", occ_sel, cholesky, preferred_element_type=jnp.float32
    ).astype(jnp.bfloat16)
    by_pair = gather_group(half_sel, ("pair",), (n_pair,))
    gathered = gather_group(by_pair, AUX, (n_aux // n_core, n_core))
    count = n_aux * n_pair * vectors
    half_rows = gathered.reshape(count * batch, 4, orbitals).transpose(1, 0, 2)
    v_halves = v_local.reshape(2, 1, rows // 2, a_width)
    sel_own = transform(half_rows[None], v_halves[0], v_halves[1], 0)
    sel_own = sel_own.reshape(2, count, batch, a_width)

    n_q = n_parts * n_aux
    rows_q = rows // n_q
    n_x = n_aux // n_core
    me_core = lax.axis_index("core")
    q = me_core * (n_parts * n_x) + lax.axis_index("parts") * n_x + lax.axis_index("x")
    piece = lax.dynamic_slice_in_dim(v_local, q * rows_q, rows_q, 0)
    mine = lax.all_gather(piece, ("pair", "parts", "x"), axis=0)
    mine = mine.reshape(n_pair, rows // n_core, a_width)
    other = lax.ppermute(mine, "core", [(c, (c + 1) % n_core) for c in range(n_core)])
    half = jnp.einsum(
        "kmj,pmn->pkjn", occ_left, cholesky, preferred_element_type=jnp.float32
    ).astype(jnp.bfloat16)
    pair_vectors = transform(half, mine, other, me_core).transpose(0, 2, 1, 3)

    sel_a = sel_own.transpose(1, 2, 0, 3)
    if n_aux == n_pair:
        perm = [(a * n_pair + z, z * n_pair + a) for a in range(n_aux) for z in range(n_pair)]
        sel_b = lax.ppermute(sel_a, AUX + ("pair",), perm)
    else:
        sel_all = lax.all_gather(sel_a, "pair", axis=0)
        sel_b = lax.dynamic_slice_in_dim(sel_all, aux_index * per_b, per_b, 0)
        sel_b = sel_b.transpose(1, 2, 3, 0, 4).reshape(count, batch, 2, b_width)
    coulomb = pair_terms(sel_b, sel_a)
    paired = coulomb - jnp.swapaxes(coulomb, 2, 3)

    a_start = lax.axis_index("pair") * a_width
    b_start = aux_index * b_width
    occ_e = jnp.take(occ_energy, batch_occ)
    vir_first = lax.dynamic_slice_in_dim(vir_energy, a_start, a_width)
    vir_second = lax.dynamic_slice_in_dim(vir_energy, b_start, b_width)
    denominator = (
        (occ_e[:, None] + occ_e[None, :])[None, None, :, :, None]
        - vir_first[None, None, None, None, :]
        - vir_second[:, None, None, None, None]
    )
    amplitudes = paired / denominator
    return (pair_vectors, amplitudes)


def solution(mesh):
    sizes = dict(zip(mesh.axis_names, mesh.devices.shape))
    cores = 2
    devices = mesh.devices.reshape(sizes["parts"], sizes["aux"] // cores, cores, sizes["pair"])
    split = jax.sharding.Mesh(devices, ("parts", "x", "core", "pair"))
    return jax.shard_map(
        on_device,
        mesh=split,
        in_specs=(
            P(("parts",) + AUX + ("pair",), None, None),
            P(),
            P(None, None, None, "pair"),
            P(),
            P(),
            P(),
        ),
        out_specs=(
            P(("parts",) + AUX + ("pair",), None, None, None),
            P(("parts",) + AUX, None, None, None, "pair"),
        ),
        check_vma=False,
    )
```

time: 142 us -> 204 us (1.44)
  waiting for transfers between devices: 32.4 us -> 96.7 us
  starting transfers between devices: 12.9 us -> 7.21 us
  local copies, waits for them, and re-layouts: 36.3 us -> 38.9 us
    all_gather x1, waiting for transfers between devices: 0.01 us -> 76.5 us  [on_device(): mine = lax.all_gather(piece, ('pair', 'parts', 'x'), axis=0)]
    ppermute x1 -> x2, waiting for transfers between devices: 21.2 us -> 11.2 us  [the longest x1 11.2 us: on_device(): sel_b = lax.ppermute(sel_a, AUX + ('pair',), perm)]
    ppermute x1 -> x2, starting transfers between devices: 8.31 us -> 4.2 us  [the longest x1 3.64 us: on_device(): sel_b = lax.ppermute(sel_a, AUX + ('pair',), perm)]
    ppermute x6, waiting for transfers between devices: 11.2 us -> 8.96 us  [gather_group(): blocks.append(lax.ppermute(x, axes, perm))]
    unnamed x16 -> x24, local copies, waits for them, and re-layouts: 25.3 us -> 26.2 us
  transfers between devices with their start and end apart: 8 -> 9, of which waited for: 4 -> 5; matrix products, arithmetic and copies ran while one was open for 38% -> 27% of each run, Pallas kernels for 3% -> 2%
where the time goes in v8:
time: 204 us; the launch traced here: 203 us
  waiting for transfers between devices  96.7 us (47%)
  local copies, waits for them, and re-layouts  38.9 us (19%)
  Pallas kernels  20.8 us (10%)
  between operations  14.3 us (7%)
  other arithmetic  13.8 us (7%)
  matrix products  11 us (5%)
  starting transfers between devices  7.21 us (4%)
    all_gather x1, waiting for transfers between devices, on_device(): mine = lax.all_gather(piece, ('pair', 'parts', 'x'), axis=0)  76.5 us
    unnamed x24, local copies, waits for them, and re-layouts  26.2 us
    pallas_call x2, Pallas kernels, transform(): pl.pallas_call(functools.partial(transform_kernel, n), grid=(b,), in_spec...  20.8 us
    ppermute x1, waiting for transfers between devices, on_device(): sel_b = lax.ppermute(sel_a, AUX + ('pair',), perm)  11.2 us
    ppermute x6, waiting for transfers between devices, gather_group(): blocks.append(lax.ppermute(x, axes, perm))  8.96 us
    dot_general x1, matrix products, on_device(): jnp.einsum('kmj,pmn->pkjn', occ_left, cholesky, preferred_element_type=jn...  6.41 us
    div x1, other arithmetic, on_device(): amplitudes = paired / denominator  4.56 us
  transfers between devices with their start and end apart: 9, of which 5 were waited for; matrix products, arithmetic and copies ran while one was open for 27% of the time, Pallas kernels for 2%

profile of v8, /device:TPU:29, one launch (start us, length us, event | category | flops | bytes accessed | tf_op | source)
XLA Modules:
  0.0 202.7 jit_solution(12135491829643437807)
XLA Ops:
  7.2 0.0 copy-start
  7.2 0.0 all-gather.3.cloned.1.call-start
  7.2 1.7 constant_dynamic-slice_fusion
  9.0 0.0 all-gather.3.cloned.1.call-update
  9.0 1.2 slice_bitcast_fusion
  10.2 0.7 copy-done.3
  11.0 0.2 copy-done.5
  11.2 0.1 pad_maximum_fusion.1
  11.2 1.2 copy.28
  12.5 0.6 gather_fusion
  13.1 0.6 gather_fusion.3
  13.7 3.0 %fusion.8 = bf16[4,3,3,832]{3,0,2,1:T(4,128)(2,1)S(1)} fusion(bf16[3,832,832]{2,1,0:T(8,128)(2,1)} %param.6, bf16[3,4,832]{2,1,0:T(4,128)(2,1)S(1)} %gather_fusion, pred[3]{0:T(512)(128)(4,1)S(1)} %get-tuple-element.9), kind=kOutput, calls=%fused_computation.12 | convolution fusion | flops 49880064 | bytes 4233219 | tf_op jit(solution)/shard_map/kmi,pmn->pikn/dot_general | solution.py:114
  16.8 0.1 collective-permute-start.1
  16.8 1.3 collective-permute-start.2
  18.2 0.2 collective-permute-start.3
  18.4 0.1 fusion.32
  18.5 0.1 broadcast_add_fusion
  18.6 0.1 broadcast_subtract_fusion.1
  18.6 1.7 fusion.31
  20.4 76.5 %all-gather.3.cloned.1.call-done = bf16[6656,384]{1,0:T(8,128)(2,1)} async-done(((bf16[416,384]{1,0:T(8,128)(2,1)}), bf16[6656,384]{1,0:T(8,128)(2,1)}) %all-gather.3.cloned.1.call-update) | async-done | bytes 5111824 | tf_op jit(solution)/shard_map/all_gather | solution.py:131
  96.9 0.6 collective-permute-start
  97.4 2.9 %broadcast_subtract_fusion = f32[384,3,3,384]{0,3,1,2:T(8,128)} fusion(f32[384]{0:T(512)S(1)} %get-tuple-element.21, f32[3,3,384]{2,0,1:T(4,128)S(1)} %broadcast_subtract_fusion.1), kind=kLoop, calls=%fused_computation.10 | loop fusion | flops 1327104 | bytes 5323776 | tf_op jit(solution)/shard_map/sub | solution.py:156
  100.3 6.4 %fusion.5 = bf16[4,128,3,832]{1,3,2,0:T(8,128)(2,1)S(1)} fusion(bf16[3,832,832]{2,1,0:T(8,128)(2,1)} %param.6, bf16[2,832,128]{2,1,0:T(8,128)(2,1)S(1)} %copy-done.6, bf16[2,832,128]{2,1,0:T(8,128)(2,1)S(1)} %copy-done.4), kind=kOutput, calls=%fused_computation.11 | convolution fusion | flops 2129494016 | bytes 7561216 | tf_op jit(solution)/shard_map/kmj,pmn->pkjn/dot_general | solution.py:134
  106.8 1.1 pad_maximum_fusion.2
  107.9 0.8 gather_fusion.1
  108.7 0.2 broadcast_select_fusion
  108.9 0.2 collective-permute-start.4
  109.1 1.2 collective-permute-start.5
  110.3 0.1 broadcast_in_dim.50
  110.4 0.1 broadcast_in_dim.51
  110.5 2.7 %copy.27 = bf16[4,128,3,832]{3,1,0,2:T(8,128)(2,1)} copy(bf16[4,128,3,832]{1,3,2,0:T(8,128)(2,1)S(1)} %fusion.5) | data formatting | bytes 5111808 | tf_op jit(solution)/shard_map/convert_element_type | solution.py:136
  113.3 0.2 bitcast_select_fusion
  113.5 0.6 collective-permute-done.4
  114.1 7.3 %collective-permute-done.5 = bf16[4,3,3,4,832]{4,3,1,2,0:T(4,128)(2,1)} collective-permute-done((bf16[4,3,3,4,832]{4,3,1,2,0:T(4,128)(2,1)S(1)}, bf16[4,3,3,4,832]{4,3,1,2,0:T(4,128)(2,1)}, u32[]{:S(2)}, u32[]{:S(2)}) %collective-permute-start.5) | collective-permute-done | bytes 239648 | tf_op jit(solution)/shard_map/ppermute | solution.py:86
  121.3 1.1 collective-permute-done.6
  122.4 2.0 pad_maximum_fusion
  124.5 1.5 gather_fusion.2
  125.9 0.4 copy.29
  126.3 1.2 fusion.11.h_ref
  127.5 4.1 %shard_map.78 = bf16[1,2,144,384]{3,2,1,0:T(8,128)(2,1)} custom-call(s32[1]{0:T(128)} %constant.97.clone.1.flag_ref, bf16[1,4,144,832]{3,2,1,0:T(8,128)(2,1)} %fusion.11.h_ref, bf16[1,1664,384]{2,1,0:T(8,128)(2,1)} %bitcast.90, bf16[1,1664,384]{2,1,0:T(8,128)(2,1)} %bitcast.89), custom_call_target="tpu_custom_call" | custom-call | flops 736100352 | bytes 3735552 | tf_op jit(solution)/shard_map/pallas_call | solution.py:51
  131.6 1.1 copy.31
  132.7 3.6 %collective-permute-start.7 = (bf16[48,3,2,384]{3,0,1,2:T(8,128)(2,1)S(1)}, bf16[48,3,2,384]{3,0,1,2:T(8,128)(2,1)S(1)}, u32[]{:S(2)}, u32[]{:S(2)}) collective-permute-start(bf16[48,3,2,384]{3,0,1,2:T(8,128)(2,1)S(1)} %bitcast.95), channel_id=1, source_target_pairs={{0,0},{1,4},{2,8},{3,12},{4,1},{5,5},{6,9},{7,13},{8,2},{9,6},{10,... | collective-permute-start | bytes 663560 | tf_op jit(solution)/shard_map/ppermute | solution.py:142
  136.5 11.2 %collective-permute-done.7 = bf16[48,3,2,384]{3,0,1,2:T(8,128)(2,1)S(1)} collective-permute-done((bf16[48,3,2,384]{3,0,1,2:T(8,128)(2,1)S(1)}, bf16[48,3,2,384]{3,0,1,2:T(8,128)(2,1)S(1)}, u32[]{:S(2)}, u32[]{:S(2)}) %collective-permute-start.7) | collective-permute-done | bytes 221216 | tf_op jit(solution)/shard_map/ppermute | solution.py:142
  147.7 1.6 fusion.13
  149.3 4.6 %fusion = f32[384,2,3,3,384]{0,4,2,3,1:T(8,128)} fusion(f32[2,3,384,3,384]{4,2,3,1,0:T(8,128)S(1)} %fusion.13, f32[384,3,3,384]{0,3,1,2:T(8,128)S(1)} %bitcast.88), kind=kLoop, calls=%fused_computation.5 | loop fusion | flops 5308416 | bytes 26542080 | tf_op jit(solution)/shard_map/div | solution.py:160
  153.9 19.7 %copy.35 = f32[384,2,3,3,384]{4,1,3,2,0:T(2,128)} copy(f32[384,2,3,3,384]{0,4,2,3,1:T(8,128)} %fusion) | data formatting | bytes 21233664
  173.6 16.7 %shard_map.77 = bf16[3,2,128,1536]{3,2,1,0:T(8,128)(2,1)} custom-call(s32[1]{0:T(128)} %bitcast.flag_ref, bf16[3,4,128,832]{3,2,1,0:T(8,128)(2,1)} %bitcast.93, bf16[4,1664,384]{2,1,0:T(8,128)(2,1)} %bitcast.105, bf16[4,1664,384]{2,1,0:T(8,128)(2,1)} %collective-permute-done.b_ref), custom_call_target="tpu_custom_call" | custom-call | flops 7851737088 | bytes 15138816 | tf_op jit(solution)/shard_map/pallas_call | solution.py:51
  190.3 5.5 %copy.34 = bf16[3,128,2,1536]{3,2,1,0:T(2,128)(2,1)} copy(bf16[3,128,2,1536]{3,1,2,0:T(8,128)(2,1)} %bitcast.94) | data formatting | bytes 4718592
  (39 shorter events, 0.3 us)
Async XLA Ops:
  7.2 5.9 %copy-start = (f32[128]{0:T(128)S(1)}, f32[128]{0:T(128)}, u32[]{:S(2)}) copy-start(f32[128]{0:T(128)} %param.9) | copy-start | bytes 1540
  7.2 5.2 %copy-start.8 = (s32[3]{0:T(128)S(1)}, s32[3]{0:T(128)}, u32[]{:S(2)}) copy-start(s32[3]{0:T(128)} %param.11) | copy-start | bytes 40
  7.2 89.7 %all-gather.3.cloned.1.call-start = ((), (), s32[]{:S(2)}) async-start(), calls=%async_computation | async-start | bytes 5431296 | tf_op jit(solution)/shard_map/all_gather | solution.py:131
  10.2 0.8 copy-start.3
  10.2 0.9 copy-start.5
  12.4 6.0 %copy-start.7 = (f32[1536]{0:T(1024)S(1)}, f32[1536]{0:T(1024)}, u32[]{:S(2)}) copy-start(f32[1536]{0:T(1024)} %param.10) | copy-start | bytes 18436
  12.4 6.2 %copy-start.2 = (bf16[2,2,832,384]{3,2,1,0:T(8,128)(2,1)S(1)}, bf16[2,2,832,384]{3,2,1,0:T(8,128)(2,1)}, u32[]{:S(2)}) copy-start(bf16[2,2,832,384]{3,2,1,0:T(8,128)(2,1)} %param.8) | copy-start | bytes 7667716
  16.8 90.0 %collective-permute-start.1 = (bf16[3,3,4,832]{3,2,0,1:T(4,128)(2,1)S(1)}, bf16[3,3,4,832]{3,2,0,1:T(4,128)(2,1)}, u32[]{:S(2)}, u32[]{:S(2)}) collective-permute-start(bf16[3,3,4,832]{3,2,0,1:T(4,128)(2,1)S(1)} %bitcast.100), channel_id=1, source_target_pairs={{0,1},{1,2},{2,3},{3,0},{4,5},{5,6},{6,7},{7,4},{8,9},{9,10},{10,1... | collective-permute-start | bytes 179720 | tf_op jit(solution)/shard_map/ppermute | solution.py:86
  16.8 89.9 %collective-permute-start.2 = (bf16[3,3,4,832]{3,2,0,1:T(4,128)(2,1)S(1)}, bf16[3,3,4,832]{3,2,0,1:T(4,128)(2,1)}, u32[]{:S(2)}, u32[]{:S(2)}) collective-permute-start(bf16[3,3,4,832]{3,2,0,1:T(4,128)(2,1)S(1)} %bitcast.101), channel_id=1, source_target_pairs={{0,2},{1,3},{2,0},{3,1},{4,6},{5,7},{6,4},{7,5},{8,10},{9,11},{10,... | collective-permute-start | bytes 179720 | tf_op jit(solution)/shard_map/ppermute | solution.py:86
  18.2 88.6 %collective-permute-start.3 = (bf16[3,3,4,832]{3,2,0,1:T(4,128)(2,1)S(1)}, bf16[3,3,4,832]{3,2,0,1:T(4,128)(2,1)}, u32[]{:S(2)}, u32[]{:S(2)}) collective-permute-start(bf16[3,3,4,832]{3,2,0,1:T(4,128)(2,1)S(1)} %bitcast.102), channel_id=1, source_target_pairs={{0,3},{1,0},{2,1},{3,2},{4,7},{5,4},{6,5},{7,6},{8,11},{9,8},{10,9... | collective-permute-start | bytes 179720 | tf_op jit(solution)/shard_map/ppermute | solution.py:86
  20.4 80.0 %copy-start.4 = (bf16[2,832,128]{2,1,0:T(8,128)(2,1)S(1)}, bf16[2,832,128]{2,1,0:T(8,128)(2,1)}, u32[]{:S(2)}) copy-start(bf16[2,832,128]{2,1,0:T(8,128)(2,1)} %copy-done.3) | copy-start | bytes 1277956
  20.4 80.0 %copy-start.6 = (bf16[2,832,128]{2,1,0:T(8,128)(2,1)S(1)}, bf16[2,832,128]{2,1,0:T(8,128)(2,1)}, u32[]{:S(2)}) copy-start(bf16[2,832,128]{2,1,0:T(8,128)(2,1)} %copy-done.5) | copy-start | bytes 1277956
  96.9 76.8 %collective-permute-start = (bf16[4,1664,384]{2,1,0:T(8,128)(2,1)}, bf16[4,1664,384]{2,1,0:T(8,128)(2,1)}, u32[]{:S(2)}, u32[]{:S(2)}) collective-permute-start(bf16[4,1664,384]{2,1,0:T(8,128)(2,1)} %bitcast.104), channel_id=1, source_target_pairs={{0,4},{4,0},{1,5},{5,1},{2,6},{6,2},{3,7},{7,3},{8,12},{12,8},{9,1... | collective-permute-start | bytes 15335432 | tf_op jit(solution)/shard_map/ppermute | solution.py:133
  108.9 5.2 %collective-permute-start.4 = (bf16[4,3,3,4,832]{4,3,1,2,0:T(4,128)(2,1)S(1)}, bf16[4,3,3,4,832]{4,3,1,2,0:T(4,128)(2,1)S(1)}, u32[]{:S(2)}, u32[]{:S(2)}) collective-permute-start(bf16[4,3,3,4,832]{4,3,1,2,0:T(4,128)(2,1)S(1)} %broadcast_select_fusion), channel_id=1, source_target_pairs={{0,4},{4,8},{8,12},{12,0},{1,5},{5,9},{9,13},{13,1},{2,6},{6,10},{... | collective-permute-start | bytes 718856 | tf_op jit(solution)/shard_map/ppermute | solution.py:86
  109.1 12.2 %collective-permute-start.5 = (bf16[4,3,3,4,832]{4,3,1,2,0:T(4,128)(2,1)S(1)}, bf16[4,3,3,4,832]{4,3,1,2,0:T(4,128)(2,1)}, u32[]{:S(2)}, u32[]{:S(2)}) collective-permute-start(bf16[4,3,3,4,832]{4,3,1,2,0:T(4,128)(2,1)S(1)} %broadcast_select_fusion), channel_id=1, source_target_pairs={{0,8},{4,12},{8,0},{12,4},{1,9},{5,13},{9,1},{13,5},{2,10},{6,14},... | collective-permute-start | bytes 718856 | tf_op jit(solution)/shard_map/ppermute | solution.py:86
  110.3 12.1 %collective-permute-start.6 = (bf16[4,3,3,4,832]{4,3,1,2,0:T(4,128)(2,1)S(1)}, bf16[4,3,3,4,832]{4,3,1,2,0:T(4,128)(2,1)}, u32[]{:S(2)}, u32[]{:S(2)}) collective-permute-start(bf16[4,3,3,4,832]{4,3,1,2,0:T(4,128)(2,1)S(1)} %broadcast_select_fusion), channel_id=1, source_target_pairs={{0,12},{4,0},{8,4},{12,8},{1,13},{5,1},{9,5},{13,9},{2,14},{6,2},{... | collective-permute-start | bytes 718856 | tf_op jit(solution)/shard_map/ppermute | solution.py:86
  132.7 15.0 %collective-permute-start.7 = (bf16[48,3,2,384]{3,0,1,2:T(8,128)(2,1)S(1)}, bf16[48,3,2,384]{3,0,1,2:T(8,128)(2,1)S(1)}, u32[]{:S(2)}, u32[]{:S(2)}) collective-permute-start(bf16[48,3,2,384]{3,0,1,2:T(8,128)(2,1)S(1)} %bitcast.95), channel_id=1, source_target_pairs={{0,0},{1,4},{2,8},{3,12},{4,1},{5,5},{6,9},{7,13},{8,2},{9,6},{10,... | collective-permute-start | bytes 663560 | tf_op jit(solution)/shard_map/ppermute | solution.py:142
  136.4 12.9 %slice-start = ((s8[5308416]{0:T(1024)(128)(4,1)}), s8[4194304]{0:T(1024)(128)(4,1)S(1)}, s32[]{:S(2)}) async-start(s8[5308416]{0:T(1024)(128)(4,1)} %bitcast.87), calls=%async_computation.1 | async-start | bytes 8388608
  147.7 1.6 slice-start.1
  173.6 22.2 %copy-start.1 = (f32[128]{0:T(128)S(1)}, f32[128]{0:T(128)}, u32[]{:S(2)}) copy-start(f32[128]{0:T(128)} %param.9) | copy-start | bytes 1540
Sparse Core Ops, SparseCore 0:
  11.4 85.4 all-gather.2

commit v9 on v7

--- a/solution.py
+++ b/solution.py
@@ -8,46 +8,46 @@
 from jax.sharding import PartitionSpec as P
 
 
-def transform_kernel(orbitals, h_ref, v_ref, o_ref):
-    pn, _, m, n = h_ref.shape
-    real = None
-    imag = None
-    for s in range(2):
-        hr = h_ref[:, s].reshape(pn * m, n)
-        hi = h_ref[:, 2 + s].reshape(pn * m, n)
-        vr = v_ref[0, s * orbitals:(s + 1) * orbitals, :]
-        vi = v_ref[0, (2 + s) * orbitals:(3 + s) * orbitals, :]
-        rr = jnp.dot(hr, vr, preferred_element_type=jnp.float32)
-        ii = jnp.dot(hi, vi, preferred_element_type=jnp.float32)
-        ri = jnp.dot(hr, vi, preferred_element_type=jnp.float32)
-        ir = jnp.dot(hi, vr, preferred_element_type=jnp.float32)
-        real = rr - ii if real is None else real + rr - ii
-        imag = ri + ir if imag is None else imag + ri + ir
+def transform_kernel(h_ref, v_ref, o_ref):
+    pn, _, m, k = h_ref.shape
+    hr = h_ref[:, 0].reshape(pn * m, k)
+    hi = h_ref[:, 1].reshape(pn * m, k)
+    vr = v_ref[0, :k, :]
+    vi = v_ref[0, k:, :]
+    real = jnp.dot(hr, vr, preferred_element_type=jnp.float32) - jnp.dot(
+        hi, vi, preferred_element_type=jnp.float32)
+    imag = jnp.dot(hr, vi, preferred_element_type=jnp.float32) + jnp.dot(
+        hi, vr, preferred_element_type=jnp.float32)
     w = real.shape[1]
     o_ref[:, 0] = real.reshape(pn, m, w).astype(o_ref.dtype)
     o_ref[:, 1] = imag.reshape(pn, m, w).astype(o_ref.dtype)
 
 
+def merge_spin(half):
+    pn, _, m, n = half.shape
+    return half.reshape(pn, 2, 2, m, n).transpose(0, 1, 3, 2, 4).reshape(pn, 2, m, 2 * n)
+
+
 def transform(half, v_blocks):
-    pn, _, m, n = half.shape
+    pn, _, m, k = half.shape
     b, rows, w = v_blocks.shape
     if w % 128 != 0:
-        v = v_blocks.reshape(b, 2, 2, n, w)
-        hr, hi = half[:, :2], half[:, 2:]
-        dims = "pskn,bsnw->pkbw"
+        v = v_blocks.reshape(b, 2, k, w)
+        hr, hi = half[:, 0], half[:, 1]
+        dims = "pmk,bkw->pmbw"
         real = jnp.einsum(dims, hr, v[:, 0], preferred_element_type=jnp.float32) - jnp.einsum(
             dims, hi, v[:, 1], preferred_element_type=jnp.float32)
         imag = jnp.einsum(dims, hr, v[:, 1], preferred_element_type=jnp.float32) + jnp.einsum(
             dims, hi, v[:, 0], preferred_element_type=jnp.float32)
         out = jnp.stack([real, imag], 1).astype(jnp.bfloat16)
         return out.reshape(pn, 2, m, b * w)
-    flops = 16 * pn * m * n * w * b
+    flops = 8 * pn * m * k * w * b
     bytes_accessed = 2 * (half.size + v_blocks.size + pn * 2 * m * b * w)
     return pl.pallas_call(
-        functools.partial(transform_kernel, n),
+        transform_kernel,
         grid=(b,),
         in_specs=[
-            pl.BlockSpec((pn, 4, m, n), lambda i: (0, 0, 0, 0)),
+            pl.BlockSpec((pn, 2, m, k), lambda i: (0, 0, 0, 0)),
             pl.BlockSpec((1, rows, w), lambda i: (i, 0, 0)),
         ],
         out_specs=pl.BlockSpec((pn, 2, m, w), lambda i: (0, 0, 0, i)),
@@ -106,7 +106,7 @@
     gathered = gather_group(by_pair, ("aux",), (n_aux,))
     count = n_aux * n_pair * vectors
     half_rows = gathered.reshape(count * batch, 4, orbitals).transpose(1, 0, 2)
-    sel_own = transform(half_rows[None], v_local[None])
+    sel_own = transform(merge_spin(half_rows[None]), v_local[None])
     sel_own = sel_own.reshape(2, count, batch, a_width)
 
     n_q = n_parts * n_aux
@@ -118,7 +118,7 @@
     half = jnp.einsum(
         "kmj,pmn->pkjn", occ_left, cholesky, preferred_element_type=jnp.float32
     ).astype(jnp.bfloat16)
-    pair_vectors = transform(half, v_full).transpose(0, 2, 1, 3)
+    pair_vectors = transform(merge_spin(half), v_full).transpose(0, 2, 1, 3)
 
     sel_a = sel_own.transpose(1, 2, 0, 3)
     if n_aux == n_pair:

time: 142 us -> 143 us (level)
  local copies, waits for them, and re-layouts: 36.3 us -> 41.1 us
  waiting for transfers between devices: 32.4 us -> 30.2 us
  other arithmetic: 13.9 us -> 12.4 us
    reshape x0 -> x3, local copies, waits for them, and re-layouts: none -> 6.6 us  [merge_spin(): half.reshape(pn, 2, 2, m, n).transpose(0, 1, 3, 2, 4)]
    convert_element_type x1 -> x0, local copies, waits for them, and re-layouts: 2.75 us -> none  [on_device(): half = jnp.einsum('kmj,pmn->pkjn', occ_left, cholesky, preferred_element_...]
    ppermute x6, waiting for transfers between devices: 11.2 us -> 9.09 us  [gather_group(): blocks.append(lax.ppermute(x, axes, perm))]
    pallas_call x2, Pallas kernels: 20.5 us -> 19.1 us  [transform(): pl.pallas_call(transform_kernel, grid=(b,), in_specs=[pl.BlockSpec((pn, 2...]
    unnamed x16 -> x14, local copies, waits for them, and re-layouts: 25.3 us -> 25.4 us
  transfers between devices with their start and end apart: 8 -> 8, of which waited for: 4 -> 3; matrix products, arithmetic and copies ran while one was open for 38% -> 41% of each run, Pallas kernels for 3% -> 3%
where the time goes in v9:
time: 143 us; the launch traced here: 142 us
  local copies, waits for them, and re-layouts  41.1 us (29%)
  waiting for transfers between devices  30.2 us (21%)
  Pallas kernels  19.1 us (13%)
  between operations  14.3 us (10%)
  starting transfers between devices  12.9 us (9%)
  other arithmetic  12.4 us (9%)
  matrix products  12.2 us (9%)
    unnamed x14, local copies, waits for them, and re-layouts  25.4 us
    ppermute x1, waiting for transfers between devices, on_device(): sel_b = lax.ppermute(sel_a, ('aux', 'pair'), perm)  21.1 us
    pallas_call x2, Pallas kernels, transform(): pl.pallas_call(transform_kernel, grid=(b,), in_specs=[pl.BlockSpec((pn, 2...  19.1 us
    ppermute x6, waiting for transfers between devices, gather_group(): blocks.append(lax.ppermute(x, axes, perm))  9.09 us
    ppermute x1, starting transfers between devices, on_device(): sel_b = lax.ppermute(sel_a, ('aux', 'pair'), perm)  8.31 us
    dot_general x1, matrix products, on_device(): jnp.einsum('kmj,pmn->pkjn', occ_left, cholesky, preferred_element_type=jn...  7.6 us
    reshape x3, local copies, waits for them, and re-layouts, merge_spin(): half.reshape(pn, 2, 2, m, n).transpose(0, 1, 3, 2, 4)  6.6 us
    div x1, other arithmetic, on_device(): amplitudes = paired / denominator  4.61 us
  transfers between devices with their start and end apart: 8, of which 3 were waited for; matrix products, arithmetic and copies ran while one was open for 41% of the time, Pallas kernels for 3%

profile of v9, /device:TPU:29, one launch (start us, length us, event | category | flops | bytes accessed | tf_op | source)
XLA Modules:
  0.0 142.2 jit_solution(2665244083232915597)
XLA Ops:
  7.2 0.0 copy-start
  7.2 0.0 all-gather.2.cloned.1.call-start
  7.2 1.7 %constant_dynamic-slice_fusion = bf16[416,384]{1,0:T(8,128)(2,1)} fusion(bf16[3328,384]{1,0:T(8,128)(2,1)} %bitcast.96, s32[]{:T(128)S(6)} %select_n.110), kind=kLoop, calls=%fused_computation.72 | loop fusion | bytes 638980 | tf_op jit(solution)/shard_map/dynamic_slice | solution.py:115
  9.0 0.0 all-gather.2.cloned.1.call-update
  9.0 1.2 slice_bitcast_fusion
  10.2 0.1 pad_maximum_fusion.1
  10.3 1.2 copy.18
  11.6 0.6 gather_fusion
  12.2 0.6 gather_fusion.3
  12.8 3.0 %fusion.8 = bf16[4,3,3,832]{3,0,2,1:T(4,128)(2,1)S(1)} fusion(bf16[3,832,832]{2,1,0:T(8,128)(2,1)} %param.6, bf16[3,4,832]{2,1,0:T(4,128)(2,1)S(1)} %gather_fusion, pred[3]{0:T(512)(128)(4,1)S(1)} %get-tuple-element.7), kind=kOutput, calls=%fused_computation.12 | convolution fusion | flops 49880064 | bytes 4233219 | tf_op jit(solution)/shard_map/kmi,pmn->pikn/dot_general | solution.py:102
  15.9 0.1 collective-permute-start
  15.9 1.3 collective-permute-start.1
  17.3 0.2 collective-permute-start.2
  17.5 0.1 fusion.30
  17.6 0.1 broadcast_add_fusion
  17.7 0.1 broadcast_subtract_fusion.1
  17.7 2.9 %broadcast_subtract_fusion = f32[384,3,3,384]{0,3,1,2:T(8,128)} fusion(f32[384]{0:T(512)S(1)} %get-tuple-element.17, f32[3,3,384]{2,0,1:T(4,128)S(1)} %broadcast_subtract_fusion.1), kind=kLoop, calls=%fused_computation.10 | loop fusion | flops 1327104 | bytes 5323776 | tf_op jit(solution)/shard_map/sub | solution.py:140
  20.6 7.6 %fusion.5 = bf16[4,128,3,832]{1,3,2,0:T(8,128)(2,1)} fusion(bf16[3,832,832]{2,1,0:T(8,128)(2,1)} %param.6, bf16[2,832,128]{2,1,0:T(8,128)(2,1)S(1)} %get-tuple-element.9, bf16[2,832,128]{2,1,0:T(8,128)(2,1)S(1)} %get-tuple-element.8), kind=kOutput, calls=%fused_computation.11 | convolution fusion | flops 2129494016 | bytes 7561216 | tf_op jit(solution)/shard_map/kmj,pmn->pkjn/dot_general | solution.py:118
  28.3 0.2 pad_maximum_fusion.2
  28.5 0.8 gather_fusion.1
  29.3 0.2 broadcast_select_fusion
  29.5 2.5 %collective-permute-start.3 = (bf16[4,3,3,4,832]{4,3,1,2,0:T(4,128)(2,1)S(1)}, bf16[4,3,3,4,832]{4,3,1,2,0:T(4,128)(2,1)S(1)}, u32[]{:S(2)}, u32[]{:S(2)}) collective-permute-start(bf16[4,3,3,4,832]{4,3,1,2,0:T(4,128)(2,1)S(1)} %broadcast_select_fusion), channel_id=1, source_target_pairs={{0,4},{4,8},{8,12},{12,0},{1,5},{5,9},{9,13},{13,1},{2,6},{6,10},{... | collective-permute-start | bytes 718856 | tf_op jit(solution)/shard_map/ppermute | solution.py:79
  32.0 0.3 collective-permute-start.4
  32.3 0.2 collective-permute-start.5
  32.5 0.1 broadcast_in_dim.47
  32.6 0.1 broadcast_in_dim.48
  32.7 1.9 %copy.16 = bf16[3,2,2,128,832]{3,4,2,1,0:T(8,128)(2,1)S(1)} copy(bf16[3,2,2,128,832]{3,4,0,2,1:T(8,128)(2,1)} %bitcast.98) | data formatting | bytes 5111808 | tf_op jit(solution)/shard_map/reshape | solution.py:28
  34.6 3.1 %copy.17.h_ref = bf16[3,2,128,1664]{3,2,1,0:T(8,128)(2,1)} copy(bf16[3,2,128,1664]{2,3,1,0:T(8,128)(2,1)S(1)} %bitcast.93) | data formatting | bytes 5111808 | tf_op jit(solution)/shard_map/reshape | solution.py:28
  37.7 0.2 bitcast_select_fusion.1
  37.9 7.3 %collective-permute-done.4 = bf16[4,3,3,4,832]{4,3,1,2,0:T(4,128)(2,1)} collective-permute-done((bf16[4,3,3,4,832]{4,3,1,2,0:T(4,128)(2,1)S(1)}, bf16[4,3,3,4,832]{4,3,1,2,0:T(4,128)(2,1)}, u32[]{:S(2)}, u32[]{:S(2)}) %collective-permute-start.4) | collective-permute-done | bytes 239648 | tf_op jit(solution)/shard_map/ppermute | solution.py:79
  45.2 1.8 %collective-permute-done.5 = bf16[4,3,3,4,832]{4,3,1,2,0:T(4,128)(2,1)} collective-permute-done((bf16[4,3,3,4,832]{4,3,1,2,0:T(4,128)(2,1)S(1)}, bf16[4,3,3,4,832]{4,3,1,2,0:T(4,128)(2,1)}, u32[]{:S(2)}, u32[]{:S(2)}) %collective-permute-start.5) | collective-permute-done | bytes 239648 | tf_op jit(solution)/shard_map/ppermute | solution.py:79
  47.0 2.0 %pad_maximum_fusion = bf16[4,4,3,3,4,832]{5,4,2,3,1,0:T(4,128)(2,1)S(1)} fusion(bf16[1,4,3,3,4,832]{5,4,2,3,1,0:T(4,128)(2,1)} %bitcast.25, bf16[1,4,3,3,4,832]{5,4,2,3,1,0:T(4,128)(2,1)} %bitcast.24, bf16[1,4,3,3,4,832]{5,4,2,3,1,0:T(4,128)(2,1)S(1)} %bitcast.104, bf16[1,4,3,3,4,832]{5,4,2,3,1,0:T(4,128)(2,1)S(1)} %bitcast_select_fusion.1), kind=kLoop, calls=%fused_computation.13 | loop fusion | flops 1437696 | bytes 1916928 | tf_op jit(solution)/shard_map/stack | solution.py:80
  49.0 1.5 %gather_fusion.2 = bf16[4,4,3,3,4,832]{5,4,2,3,1,0:T(4,128)(2,1)S(1)} fusion(bf16[4,4,3,3,4,832]{5,4,2,3,1,0:T(4,128)(2,1)S(1)} %pad_maximum_fusion, s32[1024]{0:T(1024)S(1)} %pad_clamp_fusion), kind=kCustom, calls=%fused_computation.2 | custom fusion | bytes 1916944 | tf_op jit(solution)/shard_map/jit(_take)/gather | solution.py:81
  50.5 0.4 copy.19
  50.8 0.6 bitcast_select_fusion
  51.5 0.1 copy.20
  51.6 0.8 copy.21
  52.4 1.6 %reshape.205.h_ref = bf16[1,2,144,1664]{3,2,1,0:T(8,128)(2,1)} reshape(bf16[1,2,144,2,832]{4,3,2,1,0:T(2,128)(2,1)S(1)} %copy.21) | data formatting | bytes 1916928 | tf_op jit(solution)/shard_map/reshape | solution.py:28
  54.0 4.0 %shard_map.78 = bf16[1,2,144,384]{3,2,1,0:T(8,128)(2,1)} custom-call(bf16[1,2,144,1664]{3,2,1,0:T(8,128)(2,1)} %reshape.205.h_ref, bf16[1,3328,384]{2,1,0:T(8,128)(2,1)} %bitcast.97), custom_call_target="tpu_custom_call" | custom-call | flops 736100352 | bytes 3735552 | tf_op jit(solution)/shard_map/pallas_call | solution.py:46
  58.0 1.1 copy.22
  59.2 8.3 %collective-permute-start.6 = (bf16[48,3,2,384]{3,0,1,2:T(8,128)(2,1)S(1)}, bf16[48,3,2,384]{3,0,1,2:T(8,128)(2,1)S(1)}, u32[]{:S(2)}, u32[]{:S(2)}) collective-permute-start(bf16[48,3,2,384]{3,0,1,2:T(8,128)(2,1)S(1)} %bitcast.100), channel_id=1, source_target_pairs={{0,0},{1,4},{2,8},{3,12},{4,1},{5,5},{6,9},{7,13},{8,2},{9,6},{10,... | collective-permute-start | bytes 663560 | tf_op jit(solution)/shard_map/ppermute | solution.py:126
  67.6 21.1 %collective-permute-done.6 = bf16[48,3,2,384]{3,0,1,2:T(8,128)(2,1)S(1)} collective-permute-done((bf16[48,3,2,384]{3,0,1,2:T(8,128)(2,1)S(1)}, bf16[48,3,2,384]{3,0,1,2:T(8,128)(2,1)S(1)}, u32[]{:S(2)}, u32[]{:S(2)}) %collective-permute-start.6) | collective-permute-done | bytes 221216 | tf_op jit(solution)/shard_map/ppermute | solution.py:126
  88.8 0.0 slice-start.1
  88.8 1.6 %fusion.12 = f32[2,3,384,3,384]{4,2,3,1,0:T(8,128)S(1)} fusion(bf16[96,1,3,384]{3,0,2,1:T(8,128)(2,1)S(1)} %get-tuple-element.15, bf16[96,1,3,384]{3,0,2,1:T(8,128)(2,1)S(1)} %get-tuple-element.14, bf16[48,3,384]{2,0,1:T(8,128)(2,1)S(1)} %get-tuple-element.11, bf16[48,3,384]{2,0,1:T(8,128)(2,1)S(1)} %get-tuple-element.10), kind=kOutput, calls=%fused_computation.18 | convolution fusion | flops 510935040 | bytes 11280384 | tf_op jit(solution)/shard_map/pjb,pcia->bcija/dot_general | solution.py:64
  90.4 4.6 %fusion = f32[384,2,3,3,384]{0,4,2,3,1:T(8,128)} fusion(f32[2,3,384,3,384]{4,2,3,1,0:T(8,128)S(1)} %fusion.12, f32[384,3,3,384]{0,3,1,2:T(8,128)S(1)} %bitcast.92), kind=kLoop, calls=%fused_computation.5 | loop fusion | flops 5308416 | bytes 26542080 | tf_op jit(solution)/shard_map/div | solution.py:144
  95.0 19.8 %copy.26 = f32[384,2,3,3,384]{4,1,3,2,0:T(2,128)} copy(f32[384,2,3,3,384]{0,4,2,3,1:T(8,128)} %fusion) | data formatting | bytes 21233664
  114.8 15.1 %shard_map.77 = bf16[3,2,128,1536]{3,2,1,0:T(8,128)(2,1)} custom-call(bf16[3,2,128,1664]{3,2,1,0:T(8,128)(2,1)} %copy.17.h_ref, bf16[4,3328,384]{2,1,0:T(8,128)(2,1)} %bitcast.112), custom_call_target="tpu_custom_call" | custom-call | flops 7851737088 | bytes 15138816 | tf_op jit(solution)/shard_map/pallas_call | solution.py:46
  129.9 5.5 %copy.25 = bf16[3,128,2,1536]{3,2,1,0:T(2,128)(2,1)} copy(bf16[3,128,2,1536]{3,1,2,0:T(8,128)(2,1)} %bitcast.99) | data formatting | bytes 4718592
  (30 shorter events, 0.3 us)
Async XLA Ops:
  7.2 5.0 %copy-start = (f32[128]{0:T(128)S(1)}, f32[128]{0:T(128)}, u32[]{:S(2)}) copy-start(f32[128]{0:T(128)} %param.9) | copy-start | bytes 1540
  7.2 4.3 %copy-start.3 = (s32[3]{0:T(128)S(1)}, s32[3]{0:T(128)}, u32[]{:S(2)}) copy-start(s32[3]{0:T(128)} %param.11) | copy-start | bytes 40
  7.2 107.6 %all-gather.2.cloned.1.call-start = ((), (), s32[]{:S(2)}) async-start(), calls=%async_computation | async-start | bytes 10543104 | tf_op jit(solution)/shard_map/all_gather | solution.py:116
  11.5 6.0 %copy-start.2 = (f32[1536]{0:T(1024)S(1)}, f32[1536]{0:T(1024)}, u32[]{:S(2)}) copy-start(f32[1536]{0:T(1024)} %param.10) | copy-start | bytes 18436
  15.9 12.4 %collective-permute-start = (bf16[3,3,4,832]{3,2,0,1:T(4,128)(2,1)S(1)}, bf16[3,3,4,832]{3,2,0,1:T(4,128)(2,1)S(1)}, u32[]{:S(2)}, u32[]{:S(2)}) collective-permute-start(bf16[3,3,4,832]{3,2,0,1:T(4,128)(2,1)S(1)} %bitcast.105), channel_id=1, source_target_pairs={{0,1},{1,2},{2,3},{3,0},{4,5},{5,6},{6,7},{7,4},{8,9},{9,10},{10,1... | collective-permute-start | bytes 179720 | tf_op jit(solution)/shard_map/ppermute | solution.py:79
  15.9 12.3 %collective-permute-start.1 = (bf16[3,3,4,832]{3,2,0,1:T(4,128)(2,1)S(1)}, bf16[3,3,4,832]{3,2,0,1:T(4,128)(2,1)S(1)}, u32[]{:S(2)}, u32[]{:S(2)}) collective-permute-start(bf16[3,3,4,832]{3,2,0,1:T(4,128)(2,1)S(1)} %bitcast.106), channel_id=1, source_target_pairs={{0,2},{1,3},{2,0},{3,1},{4,6},{5,7},{6,4},{7,5},{8,10},{9,11},{10,... | collective-permute-start | bytes 179720 | tf_op jit(solution)/shard_map/ppermute | solution.py:79
  17.3 11.0 %collective-permute-start.2 = (bf16[3,3,4,832]{3,2,0,1:T(4,128)(2,1)S(1)}, bf16[3,3,4,832]{3,2,0,1:T(4,128)(2,1)S(1)}, u32[]{:S(2)}, u32[]{:S(2)}) collective-permute-start(bf16[3,3,4,832]{3,2,0,1:T(4,128)(2,1)S(1)} %bitcast.107), channel_id=1, source_target_pairs={{0,3},{1,0},{2,1},{3,2},{4,7},{5,4},{6,5},{7,6},{8,11},{9,8},{10,9... | collective-permute-start | bytes 179720 | tf_op jit(solution)/shard_map/ppermute | solution.py:79
  29.5 8.4 %collective-permute-start.3 = (bf16[4,3,3,4,832]{4,3,1,2,0:T(4,128)(2,1)S(1)}, bf16[4,3,3,4,832]{4,3,1,2,0:T(4,128)(2,1)S(1)}, u32[]{:S(2)}, u32[]{:S(2)}) collective-permute-start(bf16[4,3,3,4,832]{4,3,1,2,0:T(4,128)(2,1)S(1)} %broadcast_select_fusion), channel_id=1, source_target_pairs={{0,4},{4,8},{8,12},{12,0},{1,5},{5,9},{9,13},{13,1},{2,6},{6,10},{... | collective-permute-start | bytes 718856 | tf_op jit(solution)/shard_map/ppermute | solution.py:79
  32.0 13.1 %collective-permute-start.4 = (bf16[4,3,3,4,832]{4,3,1,2,0:T(4,128)(2,1)S(1)}, bf16[4,3,3,4,832]{4,3,1,2,0:T(4,128)(2,1)}, u32[]{:S(2)}, u32[]{:S(2)}) collective-permute-start(bf16[4,3,3,4,832]{4,3,1,2,0:T(4,128)(2,1)S(1)} %broadcast_select_fusion), channel_id=1, source_target_pairs={{0,8},{4,12},{8,0},{12,4},{1,9},{5,13},{9,1},{13,5},{2,10},{6,14},... | collective-permute-start | bytes 718856 | tf_op jit(solution)/shard_map/ppermute | solution.py:79
  32.3 14.7 %collective-permute-start.5 = (bf16[4,3,3,4,832]{4,3,1,2,0:T(4,128)(2,1)S(1)}, bf16[4,3,3,4,832]{4,3,1,2,0:T(4,128)(2,1)}, u32[]{:S(2)}, u32[]{:S(2)}) collective-permute-start(bf16[4,3,3,4,832]{4,3,1,2,0:T(4,128)(2,1)S(1)} %broadcast_select_fusion), channel_id=1, source_target_pairs={{0,12},{4,0},{8,4},{12,8},{1,13},{5,1},{9,5},{13,9},{2,14},{6,2},{... | collective-permute-start | bytes 718856 | tf_op jit(solution)/shard_map/ppermute | solution.py:79
  59.2 29.5 %collective-permute-start.6 = (bf16[48,3,2,384]{3,0,1,2:T(8,128)(2,1)S(1)}, bf16[48,3,2,384]{3,0,1,2:T(8,128)(2,1)S(1)}, u32[]{:S(2)}, u32[]{:S(2)}) collective-permute-start(bf16[48,3,2,384]{3,0,1,2:T(8,128)(2,1)S(1)} %bitcast.100), channel_id=1, source_target_pairs={{0,0},{1,4},{2,8},{3,12},{4,1},{5,5},{6,9},{7,13},{8,2},{9,6},{10,... | collective-permute-start | bytes 663560 | tf_op jit(solution)/shard_map/ppermute | solution.py:126
  67.6 22.8 %slice-start = ((s8[5308416]{0:T(1024)(128)(4,1)}), s8[4194304]{0:T(1024)(128)(4,1)S(1)}, s32[]{:S(2)}) async-start(s8[5308416]{0:T(1024)(128)(4,1)} %bitcast.91), calls=%async_computation.1 | async-start | bytes 8388608
  88.8 1.6 %slice-start.1 = ((s8[5308416]{0:T(1024)(128)(4,1)}), s8[1114112]{0:T(1024)(128)(4,1)S(1)}, s32[]{:S(2)}) async-start(s8[5308416]{0:T(1024)(128)(4,1)} %bitcast.91), calls=%async_computation.2 | async-start | bytes 2228224
  114.8 20.6 %copy-start.1 = (f32[128]{0:T(128)S(1)}, f32[128]{0:T(128)}, u32[]{:S(2)}) copy-start(f32[128]{0:T(128)} %param.9) | copy-start | bytes 1540
Sparse Core Ops, SparseCore 0:
  10.9 92.4 all-gather.1

commit v10 on v9

--- a/solution.py
+++ b/solution.py
@@ -54,6 +54,31 @@
         out_shape=jax.ShapeDtypeStruct((pn, 2, m, b * w), jnp.bfloat16),
         cost_estimate=pl.CostEstimate(flops=flops, bytes_accessed=bytes_accessed, transcendentals=0),
     )(half, v_blocks)
+
+
+def transform_from(half, v_blocks, start, count):
+    pn, _, m, k = half.shape
+    b, rows, w = v_blocks.shape
+    if w % 128 != 0:
+        picked = jnp.take(v_blocks, (start + jnp.arange(count)) % b, axis=0)
+        return transform(half, picked)
+    flops = 8 * pn * m * k * w * count
+    bytes_accessed = 2 * (half.size + rows * w * count + pn * 2 * m * count * w)
+    grid_spec = pltpu.PrefetchScalarGridSpec(
+        num_scalar_prefetch=1,
+        grid=(count,),
+        in_specs=[
+            pl.BlockSpec((pn, 2, m, k), lambda i, first: (0, 0, 0, 0)),
+            pl.BlockSpec((1, rows, w), lambda i, first: ((first[0] + i) % b, 0, 0)),
+        ],
+        out_specs=pl.BlockSpec((pn, 2, m, w), lambda i, first: (0, 0, 0, i)),
+    )
+    return pl.pallas_call(
+        lambda first_ref, h_ref, v_ref, o_ref: transform_kernel(h_ref, v_ref, o_ref),
+        grid_spec=grid_spec,
+        out_shape=jax.ShapeDtypeStruct((pn, 2, m, count * w), jnp.bfloat16),
+        cost_estimate=pl.CostEstimate(flops=flops, bytes_accessed=bytes_accessed, transcendentals=0),
+    )(jnp.asarray(start, jnp.int32).reshape(1), half, v_blocks)
 
 
 def pair_terms(batch_rows, column_rows):
@@ -118,7 +143,16 @@
     half = jnp.einsum(
         "kmj,pmn->pkjn", occ_left, cholesky, preferred_element_type=jnp.float32
     ).astype(jnp.bfloat16)
-    pair_vectors = transform(merge_spin(half), v_full).transpose(0, 2, 1, 3)
+    half_m = merge_spin(half)
+    me_pair = lax.axis_index("pair")
+    own = transform(half_m, v_local[None]).transpose(0, 2, 1, 3)
+    pair_vectors = jnp.zeros((vectors, occupied, 2, n_pair * a_width), jnp.bfloat16)
+    pair_vectors = lax.dynamic_update_slice_in_dim(pair_vectors, own, me_pair * a_width, 3)
+    rest = transform_from(half_m, v_full, me_pair + 1, n_pair - 1).transpose(0, 2, 1, 3)
+    for step in range(1, n_pair):
+        block = (me_pair + step) % n_pair
+        cols = rest[..., (step - 1) * a_width:step * a_width]
+        pair_vectors = lax.dynamic_update_slice_in_dim(pair_vectors, cols, block * a_width, 3)
 
     sel_a = sel_own.transpose(1, 2, 0, 3)
     if n_aux == n_pair:

time: 143 us -> 156 us (1.091)
  waiting for transfers between devices: 30.2 us -> 43.3 us
  starting transfers between devices: 12.9 us -> 6.99 us
  Pallas kernels: 19.1 us -> 23 us
  local copies, waits for them, and re-layouts: 41.1 us -> 44.8 us
    pallas_call x0 -> x1, Pallas kernels: none -> 12.2 us  [transform_from(): pl.pallas_call(lambda first_ref, h_ref, v_ref, o_ref: transform_kernel(h_...]
    pallas_call x2, Pallas kernels: 19.1 us -> 10.8 us  [transform(): pl.pallas_call(transform_kernel, grid=(b,), in_specs=[pl.BlockSpec((pn, 2...]
    ppermute x6, waiting for transfers between devices: 9.09 us -> 17.1 us  [gather_group(): blocks.append(lax.ppermute(x, axes, perm))]
    ppermute x1, starting transfers between devices: 8.31 us -> 2.14 us  [on_device(): sel_b = lax.ppermute(sel_a, ('aux', 'pair'), perm)]
    dynamic_update_slice x0 -> x4, local copies, waits for them, and re-layouts: none -> 5.69 us  [the longest x3 4.27 us: on_device(): lax.dynamic_update_slice_in_dim(pair_vectors, cols, block * a_width, 3)]
    ppermute x1, waiting for transfers between devices: 21.1 us -> 26.1 us  [on_device(): sel_b = lax.ppermute(sel_a, ('aux', 'pair'), perm)]
    unnamed x14 -> x15, local copies, waits for them, and re-layouts: 25.4 us -> 20.8 us
    broadcast_in_dim x0 -> x1, local copies, waits for them, and re-layouts: none -> 2.62 us  [on_device(): jnp.zeros((vectors, occupied, 2, n_pair * a_width), jnp.bfloat16)]
  transfers between devices with their start and end apart: 8 -> 8, of which waited for: 3 -> 4; matrix products, arithmetic and copies ran while one was open for 41% -> 38% of each run, Pallas kernels for 3% -> 7%
where the time goes in v10:
time: 156 us; the launch traced here: 155 us
  local copies, waits for them, and re-layouts  44.8 us (29%)
  waiting for transfers between devices  43.3 us (28%)
  Pallas kernels  23 us (15%)
  between operations  14.4 us (9%)
  other arithmetic  11.2 us (7%)
  matrix products  11 us (7%)
  starting transfers between devices  6.99 us (4%)
    ppermute x1, waiting for transfers between devices, on_device(): sel_b = lax.ppermute(sel_a, ('aux', 'pair'), perm)  26.1 us
    unnamed x15, local copies, waits for them, and re-layouts  20.8 us
    ppermute x6, waiting for transfers between devices, gather_group(): blocks.append(lax.ppermute(x, axes, perm))  17.1 us
    pallas_call x1, Pallas kernels, transform_from(): pl.pallas_call(lambda first_ref, h_ref, v_ref, o_ref: transform_kernel(h_...  12.2 us
    pallas_call x2, Pallas kernels, transform(): pl.pallas_call(transform_kernel, grid=(b,), in_specs=[pl.BlockSpec((pn, 2...  10.8 us
    dot_general x1, matrix products, on_device(): jnp.einsum('kmj,pmn->pkjn', occ_left, cholesky, preferred_element_type=jn...  6.42 us
    reshape x3, local copies, waits for them, and re-layouts, merge_spin(): half.reshape(pn, 2, 2, m, n).transpose(0, 1, 3, 2, 4)  4.89 us
    ppermute x6, starting transfers between devices, gather_group(): blocks.append(lax.ppermute(x, axes, perm))  4.81 us
  transfers between devices with their start and end apart: 8, of which 4 were waited for; matrix products, arithmetic and copies ran while one was open for 38% of the time, Pallas kernels for 7%

profile of v10, /device:TPU:29, one launch (start us, length us, event | category | flops | bytes accessed | tf_op | source)
XLA Modules:
  0.0 154.6 jit_solution(14497091946041154954)
XLA Ops:
  7.2 1.7 %constant_dynamic-slice_fusion = bf16[416,384]{1,0:T(8,128)(2,1)} fusion(bf16[3328,384]{1,0:T(8,128)(2,1)} %bitcast.98, s32[]{:T(128)S(6)} %select_n.135), kind=kLoop, calls=%fused_computation.68 | loop fusion | bytes 638980 | tf_op jit(solution)/shard_map/dynamic_slice | solution.py:140
  9.0 1.2 slice_bitcast_fusion
  10.3 1.2 copy.26
  11.6 0.6 gather_fusion
  12.2 0.6 gather_fusion.3
  12.8 3.0 %fusion.8 = bf16[4,3,3,832]{3,0,2,1:T(4,128)(2,1)S(1)} fusion(bf16[3,832,832]{2,1,0:T(8,128)(2,1)} %param.6, bf16[3,4,832]{2,1,0:T(4,128)(2,1)S(1)} %gather_fusion, pred[3]{0:T(512)(128)(4,1)S(1)} %get-tuple-element.7), kind=kOutput, calls=%fused_computation.12 | convolution fusion | flops 49880064 | bytes 4233219 | tf_op jit(solution)/shard_map/kmi,pmn->pikn/dot_general | solution.py:127
  15.9 1.3 collective-permute-start.1
  17.3 0.2 collective-permute-start.2
  17.4 6.4 %fusion.5 = bf16[4,128,3,832]{1,3,2,0:T(8,128)(2,1)S(1)} fusion(bf16[3,832,832]{2,1,0:T(8,128)(2,1)} %param.6, bf16[2,832,128]{2,1,0:T(8,128)(2,1)S(1)} %get-tuple-element.12, bf16[2,832,128]{2,1,0:T(8,128)(2,1)S(1)} %get-tuple-element.11), kind=kOutput, calls=%fused_computation.11 | convolution fusion | flops 2129494016 | bytes 7561216 | tf_op jit(solution)/shard_map/kmj,pmn->pkjn/dot_general | solution.py:143
  23.9 0.2 copy.19
  24.1 3.1 %copy.20.h_ref = bf16[3,2,128,1664]{3,2,1,0:T(8,128)(2,1)} copy(bf16[3,2,128,1664]{2,3,1,0:T(8,128)(2,1)S(1)} %bitcast.95) | data formatting | bytes 5111808 | tf_op jit(solution)/shard_map/reshape | solution.py:28
  27.2 0.1 fusion.31
  27.3 6.2 %shard_map.77 = bf16[3,2,128,384]{3,2,1,0:T(8,128)(2,1)} custom-call(bf16[3,2,128,1664]{3,2,1,0:T(8,128)(2,1)} %copy.20.h_ref, bf16[1,3328,384]{2,1,0:T(8,128)(2,1)} %bitcast.99), custom_call_target="tpu_custom_call" | custom-call | flops 1962934272 | bytes 5701632 | tf_op jit(solution)/shard_map/pallas_call | solution.py:46
  33.7 2.6 %broadcast_in_dim.50 = bf16[3,128,2,1536]{3,2,1,0:T(2,128)(2,1)} broadcast(bf16[]{:T(256)} %constant.101.clone.1), dimensions={} | broadcast | bytes 2359298 | tf_op jit(solution)/shard_map/broadcast_in_dim | solution.py:149
  36.3 1.4 copy_dynamic-update-slice_fusion.3
  37.7 2.9 %broadcast_subtract_fusion = f32[384,3,3,384]{0,3,1,2:T(8,128)} fusion(f32[384]{0:T(512)S(1)} %get-tuple-element.20, f32[3,3,384]{2,0,1:T(4,128)S(1)} %broadcast_subtract_fusion.1), kind=kLoop, calls=%fused_computation.10 | loop fusion | flops 1327104 | bytes 5323776 | tf_op jit(solution)/shard_map/sub | solution.py:174
  40.7 0.2 pad_maximum_fusion.2
  40.9 0.8 gather_fusion.1
  41.7 0.2 broadcast_select_fusion
  41.9 2.8 %collective-permute-start.3 = (bf16[4,3,3,4,832]{4,3,1,2,0:T(4,128)(2,1)S(1)}, bf16[4,3,3,4,832]{4,3,1,2,0:T(4,128)(2,1)S(1)}, u32[]{:S(2)}, u32[]{:S(2)}) collective-permute-start(bf16[4,3,3,4,832]{4,3,1,2,0:T(4,128)(2,1)S(1)} %broadcast_select_fusion), channel_id=1, source_target_pairs={{0,4},{4,8},{8,12},{12,0},{1,5},{5,9},{9,13},{13,1},{2,6},{6,10},{... | collective-permute-start | bytes 718856 | tf_op jit(solution)/shard_map/ppermute | solution.py:104
  44.7 0.3 collective-permute-start.4
  44.9 0.2 collective-permute-start.5
  45.2 0.1 broadcast_in_dim.52
  45.4 0.2 bitcast_select_fusion.1
  45.5 9.7 %collective-permute-done.3 = bf16[4,3,3,4,832]{4,3,1,2,0:T(4,128)(2,1)S(1)} collective-permute-done((bf16[4,3,3,4,832]{4,3,1,2,0:T(4,128)(2,1)S(1)}, bf16[4,3,3,4,832]{4,3,1,2,0:T(4,128)(2,1)S(1)}, u32[]{:S(2)}, u32[]{:S(2)}) %collective-permute-start.3) | collective-permute-done | bytes 239648 | tf_op jit(solution)/shard_map/ppermute | solution.py:104
  55.3 7.2 %collective-permute-done.4 = bf16[4,3,3,4,832]{4,3,1,2,0:T(4,128)(2,1)S(1)} collective-permute-done((bf16[4,3,3,4,832]{4,3,1,2,0:T(4,128)(2,1)S(1)}, bf16[4,3,3,4,832]{4,3,1,2,0:T(4,128)(2,1)S(1)}, u32[]{:S(2)}, u32[]{:S(2)}) %collective-permute-start.4) | collective-permute-done | bytes 239648 | tf_op jit(solution)/shard_map/ppermute | solution.py:104
  62.4 0.2 collective-permute-done.5
  62.6 1.0 pad_maximum_fusion
  63.6 1.5 gather_fusion.2
  65.1 0.4 copy.27
  65.5 0.6 bitcast_select_fusion
  66.1 0.1 copy.28
  66.2 0.8 copy.29
  67.0 1.6 %reshape.209.h_ref = bf16[1,2,144,1664]{3,2,1,0:T(8,128)(2,1)} reshape(bf16[1,2,144,2,832]{4,3,2,1,0:T(2,128)(2,1)S(1)} %copy.29) | data formatting | bytes 1916928 | tf_op jit(solution)/shard_map/reshape | solution.py:28
  68.7 4.6 %shard_map.79 = bf16[1,2,144,384]{3,2,1,0:T(8,128)(2,1)} custom-call(bf16[1,2,144,1664]{3,2,1,0:T(8,128)(2,1)} %reshape.209.h_ref, bf16[1,3328,384]{2,1,0:T(8,128)(2,1)} %bitcast.100), custom_call_target="tpu_custom_call" | custom-call | flops 736100352 | bytes 3735552 | tf_op jit(solution)/shard_map/pallas_call | solution.py:46
  73.3 1.1 copy.30
  74.4 2.1 %collective-permute-start.6 = (bf16[48,3,2,384]{3,0,1,2:T(8,128)(2,1)S(1)}, bf16[48,3,2,384]{3,0,1,2:T(8,128)(2,1)S(1)}, u32[]{:S(2)}, u32[]{:S(2)}) collective-permute-start(bf16[48,3,2,384]{3,0,1,2:T(8,128)(2,1)S(1)} %bitcast.103), channel_id=1, source_target_pairs={{0,0},{1,4},{2,8},{3,12},{4,1},{5,5},{6,9},{7,13},{8,2},{9,6},{10,... | collective-permute-start | bytes 663560 | tf_op jit(solution)/shard_map/ppermute | solution.py:160
  76.7 26.1 %collective-permute-done.6 = bf16[48,3,2,384]{3,0,1,2:T(8,128)(2,1)S(1)} collective-permute-done((bf16[48,3,2,384]{3,0,1,2:T(8,128)(2,1)S(1)}, bf16[48,3,2,384]{3,0,1,2:T(8,128)(2,1)S(1)}, u32[]{:S(2)}, u32[]{:S(2)}) %collective-permute-start.6) | collective-permute-done | bytes 221216 | tf_op jit(solution)/shard_map/ppermute | solution.py:160
  102.8 1.6 %fusion.12 = f32[2,3,384,3,384]{4,2,3,1,0:T(8,128)S(1)} fusion(bf16[96,1,3,384]{3,0,2,1:T(8,128)(2,1)S(1)} %get-tuple-element.18, bf16[96,1,3,384]{3,0,2,1:T(8,128)(2,1)S(1)} %get-tuple-element.17, bf16[48,3,384]{2,0,1:T(8,128)(2,1)S(1)} %get-tuple-element.14, bf16[48,3,384]{2,0,1:T(8,128)(2,1)S(1)} %get-tuple-element.13), kind=kOutput, calls=%fused_computation.22 | convolution fusion | flops 510935040 | bytes 11280384 | tf_op jit(solution)/shard_map/pjb,pcia->bcija/dot_general | solution.py:89
  104.4 0.7 slice-done
  105.1 0.3 slice-done.1
  105.5 4.5 %fusion = f32[384,2,3,3,384]{0,4,2,3,1:T(8,128)} fusion(f32[2,3,384,3,384]{4,2,3,1,0:T(8,128)S(1)} %fusion.12, f32[384,3,3,384]{0,3,1,2:T(8,128)S(1)} %bitcast.94), kind=kLoop, calls=%fused_computation.5 | loop fusion | flops 5308416 | bytes 26542080 | tf_op jit(solution)/shard_map/div | solution.py:178
  109.9 19.7 %copy.33 = f32[384,2,3,3,384]{4,1,3,2,0:T(2,128)} copy(f32[384,2,3,3,384]{0,4,2,3,1:T(8,128)} %fusion) | data formatting | bytes 21233664
  129.7 12.2 %shard_map.78 = bf16[3,2,128,1152]{3,2,1,0:T(8,128)(2,1)} custom-call(s32[1]{0:T(128)} %bitcast.11.first_ref, bf16[3,2,128,1664]{3,2,1,0:T(8,128)(2,1)} %copy.20.h_ref, bf16[4,3328,384]{2,1,0:T(8,128)(2,1)} %bitcast.118), custom_call_target="tpu_custom_call" | custom-call | flops 5888802816 | bytes 11993088 | tf_op jit(solution)/shard_map/pallas_call | solution.py:76
  141.8 1.6 %fusion.30 = (bf16[3,128,2,384]{3,1,2,0:T(8,128)(2,1)S(1)}, bf16[3,128,2,384]{3,1,2,0:T(8,128)(2,1)S(1)}, bf16[3,128,2,384]{3,1,2,0:T(8,128)(2,1)S(1)}) fusion(bf16[3,128,2,1152]{3,1,2,0:T(8,128)(2,1)} %bitcast.102), kind=kLoop, calls=%fused_computation.80 | loop fusion | bytes 3538944 | tf_op jit(solution)/shard_map/slice | solution.py:154
  143.5 1.4 copy_dynamic-update-slice_fusion.2
  144.9 1.4 copy_dynamic-update-slice_fusion.1
  146.3 1.4 copy_dynamic-update-slice_fusion
  (37 shorter events, 0.7 us)
Async XLA Ops:
  7.2 5.0 %copy-start = (f32[128]{0:T(128)S(1)}, f32[128]{0:T(128)}, u32[]{:S(2)}) copy-start(f32[128]{0:T(128)} %param.9) | copy-start | bytes 1540
  7.2 122.5 %all-gather.2.cloned.1.call-start = ((), (), s32[]{:S(2)}) async-start(), calls=%async_computation | async-start | bytes 10543104 | tf_op jit(solution)/shard_map/all_gather | solution.py:141
  9.0 2.5 %copy-start.4 = (s32[3]{0:T(128)S(1)}, s32[3]{0:T(128)}, u32[]{:S(2)}) copy-start(s32[3]{0:T(128)} %param.11) | copy-start | bytes 40
  15.9 24.8 %collective-permute-start = (bf16[3,3,4,832]{3,2,0,1:T(4,128)(2,1)S(1)}, bf16[3,3,4,832]{3,2,0,1:T(4,128)(2,1)S(1)}, u32[]{:S(2)}, u32[]{:S(2)}) collective-permute-start(bf16[3,3,4,832]{3,2,0,1:T(4,128)(2,1)S(1)} %bitcast.111), channel_id=1, source_target_pairs={{0,1},{1,2},{2,3},{3,0},{4,5},{5,6},{6,7},{7,4},{8,9},{9,10},{10,1... | collective-permute-start | bytes 179720 | tf_op jit(solution)/shard_map/ppermute | solution.py:104
  15.9 24.7 %collective-permute-start.1 = (bf16[3,3,4,832]{3,2,0,1:T(4,128)(2,1)S(1)}, bf16[3,3,4,832]{3,2,0,1:T(4,128)(2,1)S(1)}, u32[]{:S(2)}, u32[]{:S(2)}) collective-permute-start(bf16[3,3,4,832]{3,2,0,1:T(4,128)(2,1)S(1)} %bitcast.112), channel_id=1, source_target_pairs={{0,2},{1,3},{2,0},{3,1},{4,6},{5,7},{6,4},{7,5},{8,10},{9,11},{10,... | collective-permute-start | bytes 179720 | tf_op jit(solution)/shard_map/ppermute | solution.py:104
  17.3 23.4 %collective-permute-start.2 = (bf16[3,3,4,832]{3,2,0,1:T(4,128)(2,1)S(1)}, bf16[3,3,4,832]{3,2,0,1:T(4,128)(2,1)S(1)}, u32[]{:S(2)}, u32[]{:S(2)}) collective-permute-start(bf16[3,3,4,832]{3,2,0,1:T(4,128)(2,1)S(1)} %bitcast.113), channel_id=1, source_target_pairs={{0,3},{1,0},{2,1},{3,2},{4,7},{5,4},{6,5},{7,6},{8,11},{9,8},{10,9... | collective-permute-start | bytes 179720 | tf_op jit(solution)/shard_map/ppermute | solution.py:104
  24.0 3.1 %copy-start.3 = (f32[1536]{0:T(1024)S(1)}, f32[1536]{0:T(1024)}, u32[]{:S(2)}) copy-start(f32[1536]{0:T(1024)} %param.10) | copy-start | bytes 18436
  33.5 2.8 %copy-start.2 = (bf16[3,2,128,384]{3,2,1,0:T(8,128)(2,1)S(1)}, bf16[3,2,128,384]{3,2,1,0:T(8,128)(2,1)}, u32[]{:S(2)}) copy-start(bf16[3,2,128,384]{3,2,1,0:T(8,128)(2,1)} %shard_map.77) | copy-start | bytes 1769476
  41.9 13.4 %collective-permute-start.3 = (bf16[4,3,3,4,832]{4,3,1,2,0:T(4,128)(2,1)S(1)}, bf16[4,3,3,4,832]{4,3,1,2,0:T(4,128)(2,1)S(1)}, u32[]{:S(2)}, u32[]{:S(2)}) collective-permute-start(bf16[4,3,3,4,832]{4,3,1,2,0:T(4,128)(2,1)S(1)} %broadcast_select_fusion), channel_id=1, source_target_pairs={{0,4},{4,8},{8,12},{12,0},{1,5},{5,9},{9,13},{13,1},{2,6},{6,10},{... | collective-permute-start | bytes 718856 | tf_op jit(solution)/shard_map/ppermute | solution.py:104
  44.7 17.8 %collective-permute-start.4 = (bf16[4,3,3,4,832]{4,3,1,2,0:T(4,128)(2,1)S(1)}, bf16[4,3,3,4,832]{4,3,1,2,0:T(4,128)(2,1)S(1)}, u32[]{:S(2)}, u32[]{:S(2)}) collective-permute-start(bf16[4,3,3,4,832]{4,3,1,2,0:T(4,128)(2,1)S(1)} %broadcast_select_fusion), channel_id=1, source_target_pairs={{0,8},{4,12},{8,0},{12,4},{1,9},{5,13},{9,1},{13,5},{2,10},{6,14},... | collective-permute-start | bytes 718856 | tf_op jit(solution)/shard_map/ppermute | solution.py:104
  44.9 17.7 %collective-permute-start.5 = (bf16[4,3,3,4,832]{4,3,1,2,0:T(4,128)(2,1)S(1)}, bf16[4,3,3,4,832]{4,3,1,2,0:T(4,128)(2,1)S(1)}, u32[]{:S(2)}, u32[]{:S(2)}) collective-permute-start(bf16[4,3,3,4,832]{4,3,1,2,0:T(4,128)(2,1)S(1)} %broadcast_select_fusion), channel_id=1, source_target_pairs={{0,12},{4,0},{8,4},{12,8},{1,13},{5,1},{9,5},{13,9},{2,14},{6,2},{... | collective-permute-start | bytes 718856 | tf_op jit(solution)/shard_map/ppermute | solution.py:104
  74.4 28.4 %collective-permute-start.6 = (bf16[48,3,2,384]{3,0,1,2:T(8,128)(2,1)S(1)}, bf16[48,3,2,384]{3,0,1,2:T(8,128)(2,1)S(1)}, u32[]{:S(2)}, u32[]{:S(2)}) collective-permute-start(bf16[48,3,2,384]{3,0,1,2:T(8,128)(2,1)S(1)} %bitcast.103), channel_id=1, source_target_pairs={{0,0},{1,4},{2,8},{3,12},{4,1},{5,5},{6,9},{7,13},{8,2},{9,6},{10,... | collective-permute-start | bytes 663560 | tf_op jit(solution)/shard_map/ppermute | solution.py:160
  102.8 2.3 %slice-start = ((s8[5308416]{0:T(1024)(128)(4,1)}), s8[4194304]{0:T(1024)(128)(4,1)S(1)}, s32[]{:S(2)}) async-start(s8[5308416]{0:T(1024)(128)(4,1)} %bitcast.93), calls=%async_computation.1 | async-start | bytes 8388608
  102.8 2.6 %slice-start.1 = ((s8[5308416]{0:T(1024)(128)(4,1)}), s8[1114112]{0:T(1024)(128)(4,1)S(1)}, s32[]{:S(2)}) async-start(s8[5308416]{0:T(1024)(128)(4,1)} %bitcast.93), calls=%async_computation.2 | async-start | bytes 2228224
  141.8 5.9 %copy-start.1 = (f32[128]{0:T(128)S(1)}, f32[128]{0:T(128)}, u32[]{:S(2)}) copy-start(f32[128]{0:T(128)} %param.9) | copy-start | bytes 1540
Sparse Core Ops, SparseCore 0:
  10.9 93.8 all-gather.1

commit v11 on v9

--- a/solution.py
+++ b/solution.py
@@ -8,16 +8,20 @@
 from jax.sharding import PartitionSpec as P
 
 
-def transform_kernel(h_ref, v_ref, o_ref):
+def transform_kernel(split, h_ref, top_ref, bot_ref, o_ref):
     pn, _, m, k = h_ref.shape
     hr = h_ref[:, 0].reshape(pn * m, k)
     hi = h_ref[:, 1].reshape(pn * m, k)
-    vr = v_ref[0, :k, :]
-    vi = v_ref[0, k:, :]
-    real = jnp.dot(hr, vr, preferred_element_type=jnp.float32) - jnp.dot(
-        hi, vi, preferred_element_type=jnp.float32)
-    imag = jnp.dot(hr, vi, preferred_element_type=jnp.float32) + jnp.dot(
-        hi, vr, preferred_element_type=jnp.float32)
+    vr = top_ref[0, :k, :]
+    vi_top = top_ref[0, k:, :]
+    vi_bot = bot_ref[0]
+
+    def times_imag(x):
+        return jnp.dot(x[:, :split], vi_top, preferred_element_type=jnp.float32) + jnp.dot(
+            x[:, split:], vi_bot, preferred_element_type=jnp.float32)
+
+    real = jnp.dot(hr, vr, preferred_element_type=jnp.float32) - times_imag(hi)
+    imag = times_imag(hr) + jnp.dot(hi, vr, preferred_element_type=jnp.float32)
     w = real.shape[1]
     o_ref[:, 0] = real.reshape(pn, m, w).astype(o_ref.dtype)
     o_ref[:, 1] = imag.reshape(pn, m, w).astype(o_ref.dtype)
@@ -28,11 +32,12 @@
     return half.reshape(pn, 2, 2, m, n).transpose(0, 1, 3, 2, 4).reshape(pn, 2, m, 2 * n)
 
 
-def transform(half, v_blocks):
+def transform(half, top, bot):
     pn, _, m, k = half.shape
-    b, rows, w = v_blocks.shape
-    if w % 128 != 0:
-        v = v_blocks.reshape(b, 2, k, w)
+    b, t_rows, w = top.shape
+    split = t_rows - k
+    if w % 128 != 0 or split % 128 != 0 or split <= 0:
+        v = jnp.concatenate([top, bot], 1).reshape(b, 2, k, w)
         hr, hi = half[:, 0], half[:, 1]
         dims = "pmk,bkw->pmbw"
         real = jnp.einsum(dims, hr, v[:, 0], preferred_element_type=jnp.float32) - jnp.einsum(
@@ -41,19 +46,21 @@
             dims, hi, v[:, 0], preferred_element_type=jnp.float32)
         out = jnp.stack([real, imag], 1).astype(jnp.bfloat16)
         return out.reshape(pn, 2, m, b * w)
+    b_rows = bot.shape[1]
     flops = 8 * pn * m * k * w * b
-    bytes_accessed = 2 * (half.size + v_blocks.size + pn * 2 * m * b * w)
+    bytes_accessed = 2 * (half.size + top.size + bot.size + pn * 2 * m * b * w)
     return pl.pallas_call(
-        transform_kernel,
+        functools.partial(transform_kernel, split),
         grid=(b,),
         in_specs=[
             pl.BlockSpec((pn, 2, m, k), lambda i: (0, 0, 0, 0)),
-            pl.BlockSpec((1, rows, w), lambda i: (i, 0, 0)),
+            pl.BlockSpec((1, t_rows, w), lambda i: (i, 0, 0)),
+            pl.BlockSpec((1, b_rows, w), lambda i: (i, 0, 0)),
         ],
         out_specs=pl.BlockSpec((pn, 2, m, w), lambda i: (0, 0, 0, i)),
         out_shape=jax.ShapeDtypeStruct((pn, 2, m, b * w), jnp.bfloat16),
         cost_estimate=pl.CostEstimate(flops=flops, bytes_accessed=bytes_accessed, transcendentals=0),
-    )(half, v_blocks)
+    )(half, top, bot)
 
 
 def pair_terms(batch_rows, column_rows):
@@ -95,6 +102,9 @@
     per_b = b_width // a_width
     batch = batch_occ.shape[0]
 
+    n_q = n_parts * n_aux
+    unit = 16 * n_q
+    top_rows = rows - (rows * 3 // 13) // unit * unit
     occ_left = jnp.concatenate([occ_coef[0], -occ_coef[1]], 0)
     v_local = vir_coef.reshape(rows, a_width)
 
@@ -106,19 +116,19 @@
     gathered = gather_group(by_pair, ("aux",), (n_aux,))
     count = n_aux * n_pair * vectors
     half_rows = gathered.reshape(count * batch, 4, orbitals).transpose(1, 0, 2)
-    sel_own = transform(merge_spin(half_rows[None]), v_local[None])
+    sel_own = transform(merge_spin(half_rows[None]), v_local[None, :top_rows], v_local[None, top_rows:])
     sel_own = sel_own.reshape(2, count, batch, a_width)
 
-    n_q = n_parts * n_aux
-    rows_q = rows // n_q
+    rows_q = top_rows // n_q
     q = lax.axis_index("parts") * n_aux + lax.axis_index("aux")
     piece = lax.dynamic_slice_in_dim(v_local, q * rows_q, rows_q, 0)
-    v_full = lax.all_gather(piece, ("pair", "parts", "aux"), axis=0, tiled=True)
-    v_full = v_full.reshape(n_pair, rows, a_width)
+    top = lax.all_gather(piece, ("pair", "parts", "aux"), axis=0, tiled=True)
+    top = top.reshape(n_pair, top_rows, a_width)
+    bot = gather_group(v_local[top_rows:], ("pair",), (n_pair,))
     half = jnp.einsum(
         "kmj,pmn->pkjn", occ_left, cholesky, preferred_element_type=jnp.float32
     ).astype(jnp.bfloat16)
-    pair_vectors = transform(merge_spin(half), v_full).transpose(0, 2, 1, 3)
+    pair_vectors = transform(merge_spin(half), top, bot).transpose(0, 2, 1, 3)
 
     sel_a = sel_own.transpose(1, 2, 0, 3)
     if n_aux == n_pair:

time: 143 us -> 163 us (1.14)
  other arithmetic: 12.4 us -> 19.5 us
  waiting for transfers between devices: 30.2 us -> 35.5 us
  local copies, waits for them, and re-layouts: 41.1 us -> 46 us
  starting transfers between devices: 12.9 us -> 15.2 us
    ppermute x1, waiting for transfers between devices: 21.1 us -> 29.9 us  [on_device(): sel_b = lax.ppermute(sel_a, ('aux', 'pair'), perm)]
    ppermute x6 -> x9, starting transfers between devices: 4.56 us -> 9.17 us  [gather_group(): blocks.append(lax.ppermute(x, axes, perm))]
    select_n x5 -> x6, other arithmetic: 1.02 us -> 5.12 us  [gather_group(): return jnp.take(stacked, (me - jnp.arange(n)) % n, axis=0)]
    ppermute x6 -> x9, waiting for transfers between devices: 9.09 us -> 5.55 us  [gather_group(): blocks.append(lax.ppermute(x, axes, perm))]
    another operation x2 -> x3, other arithmetic: 2.26 us -> 4.94 us  [gather_group(): stacked = jnp.stack(blocks, 0)]
    ppermute x1, starting transfers between devices: 8.31 us -> 5.98 us  [on_device(): sel_b = lax.ppermute(sel_a, ('aux', 'pair'), perm)]
    gather x3 -> x4, local copies, waits for them, and re-layouts: 2.61 us -> 4.89 us  [gather_group(): return jnp.take(stacked, (me - jnp.arange(n)) % n, axis=0)]
    unnamed x14 -> x18, local copies, waits for them, and re-layouts: 25.4 us -> 25.4 us
  transfers between devices with their start and end apart: 8 -> 11, of which waited for: 3 -> 3; matrix products, arithmetic and copies ran while one was open for 41% -> 44% of each run, Pallas kernels for 3% -> 2%
where the time goes in v11:
time: 163 us; the launch traced here: 162 us
  local copies, waits for them, and re-layouts  46 us (28%)
  waiting for transfers between devices  35.5 us (22%)
  other arithmetic  19.5 us (12%)
  Pallas kernels  18.9 us (12%)
  starting transfers between devices  15.2 us (9%)
  between operations  14.4 us (9%)
  matrix products  12.2 us (7%)
    ppermute x1, waiting for transfers between devices, on_device(): sel_b = lax.ppermute(sel_a, ('aux', 'pair'), perm)  29.9 us
    unnamed x18, local copies, waits for them, and re-layouts  25.4 us
    pallas_call x2, Pallas kernels, transform(): pl.pallas_call(functools.partial(transform_kernel, split), grid=(b,), in_...  18.9 us
    ppermute x9, starting transfers between devices, gather_group(): blocks.append(lax.ppermute(x, axes, perm))  9.17 us
    dot_general x1, matrix products, on_device(): jnp.einsum('kmj,pmn->pkjn', occ_left, cholesky, preferred_element_type=jn...  7.45 us
    reshape x3, local copies, waits for them, and re-layouts, merge_spin(): half.reshape(pn, 2, 2, m, n).transpose(0, 1, 3, 2, 4)  6.64 us
    ppermute x1, starting transfers between devices, on_device(): sel_b = lax.ppermute(sel_a, ('aux', 'pair'), perm)  5.98 us
    ppermute x9, waiting for transfers between devices, gather_group(): blocks.append(lax.ppermute(x, axes, perm))  5.55 us
  transfers between devices with their start and end apart: 11, of which 3 were waited for; matrix products, arithmetic and copies ran while one was open for 44% of the time, Pallas kernels for 2%

profile of v11, /device:TPU:29, one launch (start us, length us, event | category | flops | bytes accessed | tf_op | source)
XLA Modules:
  0.0 161.7 jit_solution(12913048590967755794)
XLA Ops:
  7.2 1.7 %constant_dynamic-slice_fusion = bf16[320,384]{1,0:T(8,128)(2,1)} fusion(bf16[3328,384]{1,0:T(8,128)(2,1)} %bitcast.102, s32[]{:T(128)S(6)} %select_n.118), kind=kLoop, calls=%fused_computation.76 | loop fusion | bytes 491524 | tf_op jit(solution)/shard_map/dynamic_slice | solution.py:124
  9.0 1.2 slice_bitcast_fusion.1
  10.2 0.1 pad_maximum_fusion.2
  10.3 1.2 copy.18
  11.5 0.6 gather_fusion.1
  12.1 0.6 gather_fusion.4
  12.8 3.2 %fusion.8 = bf16[4,3,3,832]{3,0,2,1:T(4,128)(2,1)S(1)} fusion(bf16[3,832,832]{2,1,0:T(8,128)(2,1)} %param.6, bf16[3,4,832]{2,1,0:T(4,128)(2,1)S(1)} %gather_fusion.1, pred[3]{0:T(512)(128)(4,1)S(1)} %get-tuple-element.7), kind=kOutput, calls=%fused_computation.16 | convolution fusion | flops 49880064 | bytes 4233219 | tf_op jit(solution)/shard_map/kmi,pmn->pikn/dot_general | solution.py:112
  16.0 1.3 collective-permute-start.4
  17.4 0.2 collective-permute-start.5
  17.5 1.2 slice_bitcast_fusion.6
  18.7 3.1 %collective-permute-start = (bf16[768,384]{1,0:T(8,128)(2,1)}, bf16[768,384]{1,0:T(8,128)(2,1)}, u32[]{:S(2)}, u32[]{:S(2)}) collective-permute-start(bf16[768,384]{1,0:T(8,128)(2,1)} %get-tuple-element.9), channel_id=1, source_target_pairs={{0,1},{1,2},{2,3},{3,0},{4,5},{5,6},{6,7},{7,4},{8,9},{9,10},{10,1... | collective-permute-start | bytes 1769480 | tf_op jit(solution)/shard_map/ppermute | solution.py:86
  21.9 0.1 fusion.30
  22.1 2.9 %broadcast_subtract_fusion = f32[384,3,3,384]{0,3,1,2:T(8,128)} fusion(f32[384]{0:T(512)S(1)} %get-tuple-element.19, f32[3,3,384]{2,0,1:T(4,128)S(1)} %broadcast_subtract_fusion.1), kind=kLoop, calls=%fused_computation.11 | loop fusion | flops 1327104 | bytes 5323776 | tf_op jit(solution)/shard_map/sub | solution.py:150
  25.0 7.5 %fusion.5 = bf16[4,128,3,832]{1,3,2,0:T(8,128)(2,1)} fusion(bf16[3,832,832]{2,1,0:T(8,128)(2,1)} %param.6, bf16[2,832,128]{2,1,0:T(8,128)(2,1)S(1)} %get-tuple-element.11, bf16[2,832,128]{2,1,0:T(8,128)(2,1)S(1)} %get-tuple-element.10), kind=kOutput, calls=%fused_computation.14 | convolution fusion | flops 2129494016 | bytes 7561216 | tf_op jit(solution)/shard_map/kmj,pmn->pkjn/dot_general | solution.py:128
  32.5 1.5 slice_bitcast_fusion.top_ref
  34.0 1.1 pad_maximum_fusion.3
  35.1 0.8 gather_fusion.2
  35.9 0.9 broadcast_select_fusion.1
  36.8 2.9 %collective-permute-start.6 = (bf16[4,3,3,4,832]{4,3,1,2,0:T(4,128)(2,1)}, bf16[4,3,3,4,832]{4,3,1,2,0:T(4,128)(2,1)}, u32[]{:S(2)}, u32[]{:S(2)}) collective-permute-start(bf16[4,3,3,4,832]{4,3,1,2,0:T(4,128)(2,1)} %broadcast_select_fusion.1), channel_id=1, source_target_pairs={{0,4},{4,8},{8,12},{12,0},{1,5},{5,9},{9,13},{13,1},{2,6},{6,10},{... | collective-permute-start | bytes 718856 | tf_op jit(solution)/shard_map/ppermute | solution.py:86
  39.7 0.3 collective-permute-start.7
  39.9 0.2 collective-permute-start.8
  40.1 0.1 broadcast_in_dim.63
  40.2 0.1 broadcast_in_dim.64
  40.3 1.9 %copy.16 = bf16[3,2,2,128,832]{3,4,2,1,0:T(8,128)(2,1)S(1)} copy(bf16[3,2,2,128,832]{3,4,0,2,1:T(8,128)(2,1)} %bitcast.105) | data formatting | bytes 5111808 | tf_op jit(solution)/shard_map/reshape | solution.py:32
  42.2 3.1 %copy.17.h_ref = bf16[3,2,128,1664]{3,2,1,0:T(8,128)(2,1)} copy(bf16[3,2,128,1664]{2,3,1,0:T(8,128)(2,1)S(1)} %bitcast.99) | data formatting | bytes 5111808 | tf_op jit(solution)/shard_map/reshape | solution.py:32
  45.3 0.2 bitcast_select_fusion.1
  45.5 1.2 collective-permute-start.2
  46.7 5.0 %collective-permute-done.7 = bf16[4,3,3,4,832]{4,3,1,2,0:T(4,128)(2,1)} collective-permute-done((bf16[4,3,3,4,832]{4,3,1,2,0:T(4,128)(2,1)}, bf16[4,3,3,4,832]{4,3,1,2,0:T(4,128)(2,1)}, u32[]{:S(2)}, u32[]{:S(2)}) %collective-permute-start.7) | collective-permute-done | bytes 239648 | tf_op jit(solution)/shard_map/ppermute | solution.py:86
  51.7 0.6 collective-permute-done.8
  52.3 2.1 %pad_maximum_fusion.1 = bf16[4,4,3,3,4,832]{5,4,2,3,1,0:T(4,128)(2,1)S(1)} fusion(bf16[1,4,3,3,4,832]{5,4,2,3,1,0:T(4,128)(2,1)} %bitcast.29, bf16[1,4,3,3,4,832]{5,4,2,3,1,0:T(4,128)(2,1)} %bitcast.28, bf16[1,4,3,3,4,832]{5,4,2,3,1,0:T(4,128)(2,1)} %bitcast.27, bf16[1,4,3,3,4,832]{5,4,2,3,1,0:T(4,128)(2,1)S(1)} %bitcast_select_fusion.1), kind=kLoop, calls=%fused_computation.17 | loop fusion | flops 1437696 | bytes 1916928 | tf_op jit(solution)/shard_map/stack | solution.py:87
  54.4 1.5 gather_fusion.3
  55.9 0.4 copy.19
  56.3 0.6 bitcast_select_fusion
  56.9 0.1 copy.20
  57.0 0.8 copy.21
  57.8 1.6 %reshape.205.h_ref = bf16[1,2,144,1664]{3,2,1,0:T(8,128)(2,1)} reshape(bf16[1,2,144,2,832]{4,3,2,1,0:T(2,128)(2,1)S(1)} %copy.21) | data formatting | bytes 1916928 | tf_op jit(solution)/shard_map/reshape | solution.py:32
  59.4 3.9 %shard_map.78 = bf16[1,2,144,384]{3,2,1,0:T(8,128)(2,1)} custom-call(bf16[1,2,144,1664]{3,2,1,0:T(8,128)(2,1)} %reshape.205.h_ref, bf16[1,2560,384]{2,1,0:T(8,128)(2,1)} %slice_bitcast_fusion.top_ref, bf16[1,768,384]{2,1,0:T(8,128)(2,1)} %get-tuple-element.8.bot_ref), custom_call_target="tpu_custom_call" | custom-call | flops 736100352 | bytes 3735552 | tf_op jit(solution)/shard_map/pallas_call | solution.py:52
  63.3 1.1 copy.22
  64.5 6.0 %collective-permute-start.9 = (bf16[48,3,2,384]{3,0,1,2:T(8,128)(2,1)S(1)}, bf16[48,3,2,384]{3,0,1,2:T(8,128)(2,1)S(1)}, u32[]{:S(2)}, u32[]{:S(2)}) collective-permute-start(bf16[48,3,2,384]{3,0,1,2:T(8,128)(2,1)S(1)} %bitcast.107), channel_id=1, source_target_pairs={{0,0},{1,4},{2,8},{3,12},{4,1},{5,5},{6,9},{7,13},{8,2},{9,6},{10,... | collective-permute-start | bytes 663560 | tf_op jit(solution)/shard_map/ppermute | solution.py:136
  70.6 29.9 %collective-permute-done.9 = bf16[48,3,2,384]{3,0,1,2:T(8,128)(2,1)S(1)} collective-permute-done((bf16[48,3,2,384]{3,0,1,2:T(8,128)(2,1)S(1)}, bf16[48,3,2,384]{3,0,1,2:T(8,128)(2,1)S(1)}, u32[]{:S(2)}, u32[]{:S(2)}) %collective-permute-start.9) | collective-permute-done | bytes 221216 | tf_op jit(solution)/shard_map/ppermute | solution.py:136
  100.5 1.6 fusion.12
  102.1 5.0 %fusion = f32[384,2,3,3,384]{0,4,2,3,1:T(8,128)} fusion(f32[2,3,384,3,384]{4,2,3,1,0:T(8,128)S(1)} %fusion.12, f32[384,3,3,384]{0,3,1,2:T(8,128)S(1)} %bitcast.98), kind=kLoop, calls=%fused_computation.6 | loop fusion | flops 5308416 | bytes 26542080 | tf_op jit(solution)/shard_map/div | solution.py:154
  107.1 19.8 %copy.26 = f32[384,2,3,3,384]{4,1,3,2,0:T(2,128)} copy(f32[384,2,3,3,384]{0,4,2,3,1:T(8,128)} %fusion) | data formatting | bytes 21233664
  127.0 1.7 %pad_maximum_fusion = bf16[4,768,384]{2,1,0:T(8,128)(2,1)S(1)} fusion(bf16[1,768,384]{2,1,0:T(8,128)(2,1)S(1)} %bitcast.111, bf16[1,768,384]{2,1,0:T(8,128)(2,1)} %bitcast.13, bf16[1,768,384]{2,1,0:T(8,128)(2,1)} %bitcast.12, bf16[1,768,384]{2,1,0:T(8,128)(2,1)S(1)} %copy-done.2), kind=kLoop, calls=%fused_computation.12 | loop fusion | flops 3538944 | bytes 4718592 | tf_op jit(solution)/shard_map/stack | solution.py:87
  128.6 2.3 %gather_fusion = bf16[4,768,384]{2,1,0:T(8,128)(2,1)} fusion(bf16[4,768,384]{2,1,0:T(8,128)(2,1)S(1)} %pad_maximum_fusion, s32[1024]{0:T(1024)S(1)} %pad_clamp_fusion.2), kind=kCustom, calls=%fused_computation | custom fusion | bytes 4718608 | tf_op jit(solution)/shard_map/jit(_take)/gather | solution.py:88
  130.9 3.4 %broadcast_select_fusion.bot_ref = bf16[4,768,384]{2,1,0:T(8,128)(2,1)} fusion(bf16[4,768,384]{2,1,0:T(8,128)(2,1)} %gather_fusion, pred[4]{0:T(512)(128)(4,1)S(1)} %compare_and_fusion.2), kind=kLoop, calls=%fused_computation.13 | loop fusion | flops 1179648 | bytes 4718596 | tf_op jit(solution)/shard_map/jit(_take)/select_n | solution.py:88
  134.3 15.0 %shard_map.77 = bf16[3,2,128,1536]{3,2,1,0:T(8,128)(2,1)} custom-call(bf16[3,2,128,1664]{3,2,1,0:T(8,128)(2,1)} %copy.17.h_ref, bf16[4,2560,384]{2,1,0:T(8,128)(2,1)} %bitcast.116, bf16[4,768,384]{2,1,0:T(8,128)(2,1)} %broadcast_select_fusion.bot_ref), custom_call_target="tpu_custom_call" | custom-call | flops 7851737088 | bytes 15138816 | tf_op jit(solution)/shard_map/pallas_call | solution.py:52
  149.4 5.5 %copy.25 = bf16[3,128,2,1536]{3,2,1,0:T(2,128)(2,1)} copy(bf16[3,128,2,1536]{3,1,2,0:T(8,128)(2,1)} %bitcast.106) | data formatting | bytes 4718592
  (45 shorter events, 0.6 us)
Async XLA Ops:
  7.2 4.9 %copy-start = (f32[128]{0:T(128)S(1)}, f32[128]{0:T(128)}, u32[]{:S(2)}) copy-start(f32[128]{0:T(128)} %param.9) | copy-start | bytes 1540
  7.2 127.1 %all-gather.2.cloned.1.call-start = ((), (), s32[]{:S(2)}) async-start(), calls=%async_computation | async-start | bytes 8110080 | tf_op jit(solution)/shard_map/all_gather | solution.py:125
  8.9 2.5 %copy-start.5 = (s32[3]{0:T(128)S(1)}, s32[3]{0:T(128)}, u32[]{:S(2)}) copy-start(s32[3]{0:T(128)} %param.11) | copy-start | bytes 40
  12.7 4.8 %copy-start.3 = (bf16[2,2,832,384]{3,2,1,0:T(8,128)(2,1)S(1)}, bf16[2,2,832,384]{3,2,1,0:T(8,128)(2,1)}, u32[]{:S(2)}) copy-start(bf16[2,2,832,384]{3,2,1,0:T(8,128)(2,1)} %param.8) | copy-start | bytes 7667716
  12.7 9.1 %copy-start.4 = (f32[1536]{0:T(1024)S(1)}, f32[1536]{0:T(1024)}, u32[]{:S(2)}) copy-start(f32[1536]{0:T(1024)} %param.10) | copy-start | bytes 18436
  16.0 18.0 %collective-permute-start.3 = (bf16[3,3,4,832]{3,2,0,1:T(4,128)(2,1)S(1)}, bf16[3,3,4,832]{3,2,0,1:T(4,128)(2,1)}, u32[]{:S(2)}, u32[]{:S(2)}) collective-permute-start(bf16[3,3,4,832]{3,2,0,1:T(4,128)(2,1)S(1)} %bitcast.112), channel_id=1, source_target_pairs={{0,1},{1,2},{2,3},{3,0},{4,5},{5,6},{6,7},{7,4},{8,9},{9,10},{10,1... | collective-permute-start | bytes 179720 | tf_op jit(solution)/shard_map/ppermute | solution.py:86
  16.0 17.9 %collective-permute-start.4 = (bf16[3,3,4,832]{3,2,0,1:T(4,128)(2,1)S(1)}, bf16[3,3,4,832]{3,2,0,1:T(4,128)(2,1)}, u32[]{:S(2)}, u32[]{:S(2)}) collective-permute-start(bf16[3,3,4,832]{3,2,0,1:T(4,128)(2,1)S(1)} %bitcast.113), channel_id=1, source_target_pairs={{0,2},{1,3},{2,0},{3,1},{4,6},{5,7},{6,4},{7,5},{8,10},{9,11},{10,... | collective-permute-start | bytes 179720 | tf_op jit(solution)/shard_map/ppermute | solution.py:86
  17.4 16.6 %collective-permute-start.5 = (bf16[3,3,4,832]{3,2,0,1:T(4,128)(2,1)S(1)}, bf16[3,3,4,832]{3,2,0,1:T(4,128)(2,1)}, u32[]{:S(2)}, u32[]{:S(2)}) collective-permute-start(bf16[3,3,4,832]{3,2,0,1:T(4,128)(2,1)S(1)} %bitcast.114), channel_id=1, source_target_pairs={{0,3},{1,0},{2,1},{3,2},{4,7},{5,4},{6,5},{7,6},{8,11},{9,8},{10,9... | collective-permute-start | bytes 179720 | tf_op jit(solution)/shard_map/ppermute | solution.py:86
  18.7 108.2 %collective-permute-start = (bf16[768,384]{1,0:T(8,128)(2,1)}, bf16[768,384]{1,0:T(8,128)(2,1)}, u32[]{:S(2)}, u32[]{:S(2)}) collective-permute-start(bf16[768,384]{1,0:T(8,128)(2,1)} %get-tuple-element.9), channel_id=1, source_target_pairs={{0,1},{1,2},{2,3},{3,0},{4,5},{5,6},{6,7},{7,4},{8,9},{9,10},{10,1... | collective-permute-start | bytes 1769480 | tf_op jit(solution)/shard_map/ppermute | solution.py:86
  21.8 105.2 %collective-permute-start.1 = (bf16[768,384]{1,0:T(8,128)(2,1)}, bf16[768,384]{1,0:T(8,128)(2,1)}, u32[]{:S(2)}, u32[]{:S(2)}) collective-permute-start(bf16[768,384]{1,0:T(8,128)(2,1)} %get-tuple-element.9), channel_id=1, source_target_pairs={{0,2},{1,3},{2,0},{3,1},{4,6},{5,7},{6,4},{7,5},{8,10},{9,11},{10,... | collective-permute-start | bytes 1769480 | tf_op jit(solution)/shard_map/ppermute | solution.py:86
  36.8 8.7 %collective-permute-start.6 = (bf16[4,3,3,4,832]{4,3,1,2,0:T(4,128)(2,1)}, bf16[4,3,3,4,832]{4,3,1,2,0:T(4,128)(2,1)}, u32[]{:S(2)}, u32[]{:S(2)}) collective-permute-start(bf16[4,3,3,4,832]{4,3,1,2,0:T(4,128)(2,1)} %broadcast_select_fusion.1), channel_id=1, source_target_pairs={{0,4},{4,8},{8,12},{12,0},{1,5},{5,9},{9,13},{13,1},{2,6},{6,10},{... | collective-permute-start | bytes 718856 | tf_op jit(solution)/shard_map/ppermute | solution.py:86
  39.7 12.0 %collective-permute-start.7 = (bf16[4,3,3,4,832]{4,3,1,2,0:T(4,128)(2,1)}, bf16[4,3,3,4,832]{4,3,1,2,0:T(4,128)(2,1)}, u32[]{:S(2)}, u32[]{:S(2)}) collective-permute-start(bf16[4,3,3,4,832]{4,3,1,2,0:T(4,128)(2,1)} %broadcast_select_fusion.1), channel_id=1, source_target_pairs={{0,8},{4,12},{8,0},{12,4},{1,9},{5,13},{9,1},{13,5},{2,10},{6,14},... | collective-permute-start | bytes 718856 | tf_op jit(solution)/shard_map/ppermute | solution.py:86
  39.9 12.3 %collective-permute-start.8 = (bf16[4,3,3,4,832]{4,3,1,2,0:T(4,128)(2,1)}, bf16[4,3,3,4,832]{4,3,1,2,0:T(4,128)(2,1)}, u32[]{:S(2)}, u32[]{:S(2)}) collective-permute-start(bf16[4,3,3,4,832]{4,3,1,2,0:T(4,128)(2,1)} %broadcast_select_fusion.1), channel_id=1, source_target_pairs={{0,12},{4,0},{8,4},{12,8},{1,13},{5,1},{9,5},{13,9},{2,14},{6,2},{... | collective-permute-start | bytes 718856 | tf_op jit(solution)/shard_map/ppermute | solution.py:86
  45.5 81.4 %collective-permute-start.2 = (bf16[768,384]{1,0:T(8,128)(2,1)}, bf16[768,384]{1,0:T(8,128)(2,1)S(1)}, u32[]{:S(2)}, u32[]{:S(2)}) collective-permute-start(bf16[768,384]{1,0:T(8,128)(2,1)} %get-tuple-element.9), channel_id=1, source_target_pairs={{0,3},{1,0},{2,1},{3,2},{4,7},{5,4},{6,5},{7,6},{8,11},{9,8},{10,9... | collective-permute-start | bytes 1769480 | tf_op jit(solution)/shard_map/ppermute | solution.py:86
  64.5 36.0 %collective-permute-start.9 = (bf16[48,3,2,384]{3,0,1,2:T(8,128)(2,1)S(1)}, bf16[48,3,2,384]{3,0,1,2:T(8,128)(2,1)S(1)}, u32[]{:S(2)}, u32[]{:S(2)}) collective-permute-start(bf16[48,3,2,384]{3,0,1,2:T(8,128)(2,1)S(1)} %bitcast.107), channel_id=1, source_target_pairs={{0,0},{1,4},{2,8},{3,12},{4,1},{5,5},{6,9},{7,13},{8,2},{9,6},{10,... | collective-permute-start | bytes 663560 | tf_op jit(solution)/shard_map/ppermute | solution.py:136
  70.5 31.6 %slice-start = ((s8[5308416]{0:T(1024)(128)(4,1)}), s8[4194304]{0:T(1024)(128)(4,1)S(1)}, s32[]{:S(2)}) async-start(s8[5308416]{0:T(1024)(128)(4,1)} %bitcast.97), calls=%async_computation.1 | async-start | bytes 8388608
  100.5 1.6 slice-start.1
  107.1 19.8 %copy-start.2 = (bf16[1,768,384]{2,1,0:T(8,128)(2,1)S(1)}, bf16[1,768,384]{2,1,0:T(8,128)(2,1)}, u32[]{:S(2)}) copy-start(bf16[1,768,384]{2,1,0:T(8,128)(2,1)} %get-tuple-element.8.bot_ref) | copy-start | bytes 1769476
  134.3 20.5 %copy-start.1 = (f32[128]{0:T(128)S(1)}, f32[128]{0:T(128)}, u32[]{:S(2)}) copy-start(f32[128]{0:T(128)} %param.9) | copy-start | bytes 1540
Sparse Core Ops, SparseCore 0:
  10.9 119.6 all-gather.1

commit v12 on v7

--- a/solution.py
+++ b/solution.py
@@ -10,13 +10,18 @@
 
 def transform_kernel(orbitals, h_ref, v_ref, o_ref):
     pn, _, m, n = h_ref.shape
+    per = orbitals // v_ref.shape[2]
+
+    def rows_of(t):
+        return jnp.concatenate([v_ref[t * per + j, 0] for j in range(per)], 0)
+
     real = None
     imag = None
     for s in range(2):
         hr = h_ref[:, s].reshape(pn * m, n)
         hi = h_ref[:, 2 + s].reshape(pn * m, n)
-        vr = v_ref[0, s * orbitals:(s + 1) * orbitals, :]
-        vi = v_ref[0, (2 + s) * orbitals:(3 + s) * orbitals, :]
+        vr = rows_of(s)
+        vi = rows_of(2 + s)
         rr = jnp.dot(hr, vr, preferred_element_type=jnp.float32)
         ii = jnp.dot(hi, vi, preferred_element_type=jnp.float32)
         ri = jnp.dot(hr, vi, preferred_element_type=jnp.float32)
@@ -28,11 +33,11 @@
     o_ref[:, 1] = imag.reshape(pn, m, w).astype(o_ref.dtype)
 
 
-def transform(half, v_blocks):
+def transform(half, pieces):
     pn, _, m, n = half.shape
-    b, rows, w = v_blocks.shape
-    if w % 128 != 0:
-        v = v_blocks.reshape(b, 2, 2, n, w)
+    q, b, r, w = pieces.shape
+    if w % 128 != 0 or n % r != 0:
+        v = pieces.transpose(1, 0, 2, 3).reshape(b, 2, 2, n, w)
         hr, hi = half[:, :2], half[:, 2:]
         dims = "pskn,bsnw->pkbw"
         real = jnp.einsum(dims, hr, v[:, 0], preferred_element_type=jnp.float32) - jnp.einsum(
@@ -42,18 +47,18 @@
         out = jnp.stack([real, imag], 1).astype(jnp.bfloat16)
         return out.reshape(pn, 2, m, b * w)
     flops = 16 * pn * m * n * w * b
-    bytes_accessed = 2 * (half.size + v_blocks.size + pn * 2 * m * b * w)
+    bytes_accessed = 2 * (half.size + pieces.size + pn * 2 * m * b * w)
     return pl.pallas_call(
         functools.partial(transform_kernel, n),
         grid=(b,),
         in_specs=[
             pl.BlockSpec((pn, 4, m, n), lambda i: (0, 0, 0, 0)),
-            pl.BlockSpec((1, rows, w), lambda i: (i, 0, 0)),
+            pl.BlockSpec((q, 1, r, w), lambda i: (0, i, 0, 0)),
         ],
         out_specs=pl.BlockSpec((pn, 2, m, w), lambda i: (0, 0, 0, i)),
         out_shape=jax.ShapeDtypeStruct((pn, 2, m, b * w), jnp.bfloat16),
         cost_estimate=pl.CostEstimate(flops=flops, bytes_accessed=bytes_accessed, transcendentals=0),
-    )(half, v_blocks)
+    )(half, pieces)
 
 
 def pair_terms(batch_rows, column_rows):
@@ -106,15 +111,15 @@
     gathered = gather_group(by_pair, ("aux",), (n_aux,))
     count = n_aux * n_pair * vectors
     half_rows = gathered.reshape(count * batch, 4, orbitals).transpose(1, 0, 2)
-    sel_own = transform(half_rows[None], v_local[None])
+    sel_own = transform(half_rows[None], v_local.reshape(8, 1, rows // 8, a_width))
     sel_own = sel_own.reshape(2, count, batch, a_width)
 
     n_q = n_parts * n_aux
     rows_q = rows // n_q
     q = lax.axis_index("parts") * n_aux + lax.axis_index("aux")
     piece = lax.dynamic_slice_in_dim(v_local, q * rows_q, rows_q, 0)
-    v_full = lax.all_gather(piece, ("pair", "parts", "aux"), axis=0, tiled=True)
-    v_full = v_full.reshape(n_pair, rows, a_width)
+    v_full = lax.all_gather(piece, ("parts", "aux", "pair"), axis=0)
+    v_full = v_full.reshape(n_q, n_pair, rows_q, a_width)
     half = jnp.einsum(
         "kmj,pmn->pkjn", occ_left, cholesky, preferred_element_type=jnp.float32
     ).astype(jnp.bfloat16)

time: 142 us -> 143 us (level)
  no operation moved by 1% of the time
where the time goes in v12:
time: 143 us; the launch traced here: 142 us
  local copies, waits for them, and re-layouts  36.3 us (25%)
  waiting for transfers between devices  32.5 us (23%)
  Pallas kernels  20.5 us (14%)
  between operations  14.3 us (10%)
  other arithmetic  13.9 us (10%)
  starting transfers between devices  12.9 us (9%)
  matrix products  11.2 us (8%)
    unnamed x16, local copies, waits for them, and re-layouts  25.4 us
    ppermute x1, waiting for transfers between devices, on_device(): sel_b = lax.ppermute(sel_a, ('aux', 'pair'), perm)  21.2 us
    pallas_call x2, Pallas kernels, transform(): pl.pallas_call(functools.partial(transform_kernel, n), grid=(b,), in_spec...  20.5 us
    ppermute x6, waiting for transfers between devices, gather_group(): blocks.append(lax.ppermute(x, axes, perm))  11.3 us
    ppermute x1, starting transfers between devices, on_device(): sel_b = lax.ppermute(sel_a, ('aux', 'pair'), perm)  8.31 us
    dot_general x1, matrix products, on_device(): jnp.einsum('kmj,pmn->pkjn', occ_left, cholesky, preferred_element_type=jn...  6.53 us
    div x1, other arithmetic, on_device(): amplitudes = paired / denominator  4.58 us
    ppermute x6, starting transfers between devices, gather_group(): blocks.append(lax.ppermute(x, axes, perm))  4.58 us
  transfers between devices with their start and end apart: 8, of which 4 were waited for; matrix products, arithmetic and copies ran while one was open for 38% of the time, Pallas kernels for 3%

profile of v12, /device:TPU:29, one launch (start us, length us, event | category | flops | bytes accessed | tf_op | source)
XLA Modules:
  0.0 141.7 jit_solution(4253576208032010934)
XLA Ops:
  7.2 0.0 copy-start
  7.2 0.0 all-gather.3.cloned.1.call-start
  7.2 1.7 %constant_dynamic-slice_fusion = bf16[416,384]{1,0:T(8,128)(2,1)} fusion(bf16[3328,384]{1,0:T(8,128)(2,1)} %bitcast.88, s32[]{:T(128)S(6)} %select_n.110), kind=kLoop, calls=%fused_computation.73 | loop fusion | bytes 638980 | tf_op jit(solution)/shard_map/dynamic_slice | solution.py:120
  9.0 0.0 all-gather.3.cloned.1.call-update
  9.0 1.2 slice_bitcast_fusion
  10.2 0.1 pad_maximum_fusion.1
  10.3 1.2 copy.28
  11.5 0.0 copy-start.3
  11.6 0.6 gather_fusion
  12.2 0.6 gather_fusion.3
  12.8 3.0 %fusion.8 = bf16[4,3,3,832]{3,0,2,1:T(4,128)(2,1)S(1)} fusion(bf16[3,832,832]{2,1,0:T(8,128)(2,1)} %param.6, bf16[3,4,832]{2,1,0:T(4,128)(2,1)S(1)} %gather_fusion, pred[3]{0:T(512)(128)(4,1)S(1)} %get-tuple-element.9), kind=kOutput, calls=%fused_computation.12 | convolution fusion | flops 49880064 | bytes 4233219 | tf_op jit(solution)/shard_map/kmi,pmn->pikn/dot_general | solution.py:107
  15.9 0.1 collective-permute-start
  15.9 1.3 collective-permute-start.1
  17.3 0.2 collective-permute-start.2
  17.5 0.1 fusion.31
  17.6 0.1 broadcast_add_fusion
  17.7 0.1 broadcast_subtract_fusion.1
  17.7 2.9 %broadcast_subtract_fusion = f32[384,3,3,384]{0,3,1,2:T(8,128)} fusion(f32[384]{0:T(512)S(1)} %get-tuple-element.19, f32[3,3,384]{2,0,1:T(4,128)S(1)} %broadcast_subtract_fusion.1), kind=kLoop, calls=%fused_computation.10 | loop fusion | flops 1327104 | bytes 5323776 | tf_op jit(solution)/shard_map/sub | solution.py:145
  20.6 6.5 %fusion.5 = bf16[4,128,3,832]{1,3,2,0:T(8,128)(2,1)S(1)} fusion(bf16[3,832,832]{2,1,0:T(8,128)(2,1)} %param.6, bf16[2,832,128]{2,1,0:T(8,128)(2,1)S(1)} %get-tuple-element.11, bf16[2,832,128]{2,1,0:T(8,128)(2,1)S(1)} %get-tuple-element.10), kind=kOutput, calls=%fused_computation.11 | convolution fusion | flops 2129494016 | bytes 7561216 | tf_op jit(solution)/shard_map/kmj,pmn->pkjn/dot_general | solution.py:123
  27.2 0.0 collective-permute-done
  27.2 1.1 pad_maximum_fusion.2
  28.3 0.8 gather_fusion.1
  29.1 0.2 broadcast_select_fusion
  29.3 2.5 %collective-permute-start.3 = (bf16[4,3,3,4,832]{4,3,1,2,0:T(4,128)(2,1)S(1)}, bf16[4,3,3,4,832]{4,3,1,2,0:T(4,128)(2,1)S(1)}, u32[]{:S(2)}, u32[]{:S(2)}) collective-permute-start(bf16[4,3,3,4,832]{4,3,1,2,0:T(4,128)(2,1)S(1)} %broadcast_select_fusion), channel_id=1, source_target_pairs={{0,4},{4,8},{8,12},{12,0},{1,5},{5,9},{9,13},{13,1},{2,6},{6,10},{... | collective-permute-start | bytes 718856 | tf_op jit(solution)/shard_map/ppermute | solution.py:84
  31.8 0.3 collective-permute-start.4
  32.1 0.2 collective-permute-start.5
  32.3 0.1 broadcast_in_dim.50
  32.4 0.1 broadcast_in_dim.51
  32.5 2.8 %copy.27 = bf16[4,128,3,832]{3,1,0,2:T(8,128)(2,1)} copy(bf16[4,128,3,832]{1,3,2,0:T(8,128)(2,1)S(1)} %fusion.5) | data formatting | bytes 5111808 | tf_op jit(solution)/shard_map/convert_element_type | solution.py:125
  35.3 0.2 bitcast_select_fusion
  35.5 1.8 %collective-permute-done.3 = bf16[4,3,3,4,832]{4,3,1,2,0:T(4,128)(2,1)S(1)} collective-permute-done((bf16[4,3,3,4,832]{4,3,1,2,0:T(4,128)(2,1)S(1)}, bf16[4,3,3,4,832]{4,3,1,2,0:T(4,128)(2,1)S(1)}, u32[]{:S(2)}, u32[]{:S(2)}) %collective-permute-start.3) | collective-permute-done | bytes 239648 | tf_op jit(solution)/shard_map/ppermute | solution.py:84
  37.3 7.7 %collective-permute-done.4 = bf16[4,3,3,4,832]{4,3,1,2,0:T(4,128)(2,1)} collective-permute-done((bf16[4,3,3,4,832]{4,3,1,2,0:T(4,128)(2,1)S(1)}, bf16[4,3,3,4,832]{4,3,1,2,0:T(4,128)(2,1)}, u32[]{:S(2)}, u32[]{:S(2)}) %collective-permute-start.4) | collective-permute-done | bytes 239648 | tf_op jit(solution)/shard_map/ppermute | solution.py:84
  45.0 1.8 %collective-permute-done.5 = bf16[4,3,3,4,832]{4,3,1,2,0:T(4,128)(2,1)} collective-permute-done((bf16[4,3,3,4,832]{4,3,1,2,0:T(4,128)(2,1)S(1)}, bf16[4,3,3,4,832]{4,3,1,2,0:T(4,128)(2,1)}, u32[]{:S(2)}, u32[]{:S(2)}) %collective-permute-start.5) | collective-permute-done | bytes 239648 | tf_op jit(solution)/shard_map/ppermute | solution.py:84
  46.8 2.1 %pad_maximum_fusion = bf16[4,4,3,3,4,832]{5,4,2,3,1,0:T(4,128)(2,1)S(1)} fusion(bf16[1,4,3,3,4,832]{5,4,2,3,1,0:T(4,128)(2,1)} %bitcast.22, bf16[1,4,3,3,4,832]{5,4,2,3,1,0:T(4,128)(2,1)} %bitcast.21, bf16[1,4,3,3,4,832]{5,4,2,3,1,0:T(4,128)(2,1)} %bitcast.96, bf16[1,4,3,3,4,832]{5,4,2,3,1,0:T(4,128)(2,1)S(1)} %bitcast_select_fusion), kind=kLoop, calls=%fused_computation.13 | loop fusion | flops 1437696 | bytes 1916928 | tf_op jit(solution)/shard_map/stack | solution.py:85
  48.9 1.5 %gather_fusion.2 = bf16[4,4,3,3,4,832]{5,4,2,3,1,0:T(4,128)(2,1)S(1)} fusion(bf16[4,4,3,3,4,832]{5,4,2,3,1,0:T(4,128)(2,1)S(1)} %pad_maximum_fusion, s32[1024]{0:T(1024)S(1)} %pad_clamp_fusion), kind=kCustom, calls=%fused_computation.2 | custom fusion | bytes 1916944 | tf_op jit(solution)/shard_map/jit(_take)/gather | solution.py:86
  50.4 0.4 copy.29
  50.8 1.2 fusion.11.h_ref
  51.9 4.1 %shard_map.78 = bf16[1,2,144,384]{3,2,1,0:T(8,128)(2,1)} custom-call(bf16[1,4,144,832]{3,2,1,0:T(8,128)(2,1)} %fusion.11.h_ref, bf16[8,1,416,384]{3,2,1,0:T(8,128)(2,1)} %bitcast.89), custom_call_target="tpu_custom_call" | custom-call | flops 736100352 | bytes 3735552 | tf_op jit(solution)/shard_map/pallas_call | solution.py:51
  56.1 1.1 copy.31
  57.2 8.3 %collective-permute-start.6 = (bf16[48,3,2,384]{3,0,1,2:T(8,128)(2,1)S(1)}, bf16[48,3,2,384]{3,0,1,2:T(8,128)(2,1)S(1)}, u32[]{:S(2)}, u32[]{:S(2)}) collective-permute-start(bf16[48,3,2,384]{3,0,1,2:T(8,128)(2,1)S(1)} %bitcast.92), channel_id=1, source_target_pairs={{0,0},{1,4},{2,8},{3,12},{4,1},{5,5},{6,9},{7,13},{8,2},{9,6},{10,... | collective-permute-start | bytes 663560 | tf_op jit(solution)/shard_map/ppermute | solution.py:131
  65.6 0.0 slice-start
  65.6 21.2 %collective-permute-done.6 = bf16[48,3,2,384]{3,0,1,2:T(8,128)(2,1)S(1)} collective-permute-done((bf16[48,3,2,384]{3,0,1,2:T(8,128)(2,1)S(1)}, bf16[48,3,2,384]{3,0,1,2:T(8,128)(2,1)S(1)}, u32[]{:S(2)}, u32[]{:S(2)}) %collective-permute-start.6) | collective-permute-done | bytes 221216 | tf_op jit(solution)/shard_map/ppermute | solution.py:131
  86.9 0.0 slice-start.1
  86.9 1.6 %fusion.13 = f32[2,3,384,3,384]{4,2,3,1,0:T(8,128)S(1)} fusion(bf16[96,1,3,384]{3,0,2,1:T(8,128)(2,1)S(1)} %get-tuple-element.17, bf16[96,1,3,384]{3,0,2,1:T(8,128)(2,1)S(1)} %get-tuple-element.16, bf16[48,3,384]{2,0,1:T(8,128)(2,1)S(1)} %get-tuple-element.13, bf16[48,3,384]{2,0,1:T(8,128)(2,1)S(1)} %get-tuple-element.12), kind=kOutput, calls=%fused_computation.19 | convolution fusion | flops 510935040 | bytes 11280384 | tf_op jit(solution)/shard_map/pjb,pcia->bcija/dot_general | solution.py:69
  88.5 4.6 %fusion = f32[384,2,3,3,384]{0,4,2,3,1:T(8,128)} fusion(f32[2,3,384,3,384]{4,2,3,1,0:T(8,128)S(1)} %fusion.13, f32[384,3,3,384]{0,3,1,2:T(8,128)S(1)} %bitcast.86), kind=kLoop, calls=%fused_computation.5 | loop fusion | flops 5308416 | bytes 26542080 | tf_op jit(solution)/shard_map/div | solution.py:149
  93.1 19.8 %copy.35 = f32[384,2,3,3,384]{4,1,3,2,0:T(2,128)} copy(f32[384,2,3,3,384]{0,4,2,3,1:T(8,128)} %fusion) | data formatting | bytes 21233664
  112.9 16.4 %shard_map.77 = bf16[3,2,128,1536]{3,2,1,0:T(8,128)(2,1)} custom-call(bf16[3,4,128,832]{3,2,1,0:T(8,128)(2,1)} %bitcast.90, bf16[8,4,416,384]{3,2,1,0:T(8,128)(2,1)} %bitcast.102), custom_call_target="tpu_custom_call" | custom-call | flops 7851737088 | bytes 15138816 | tf_op jit(solution)/shard_map/pallas_call | solution.py:51
  129.4 5.5 %copy.34 = bf16[3,128,2,1536]{3,2,1,0:T(2,128)(2,1)} copy(bf16[3,128,2,1536]{3,1,2,0:T(8,128)(2,1)} %bitcast.91) | data formatting | bytes 4718592
  (28 shorter events, 0.3 us)
Async XLA Ops:
  7.2 5.0 %copy-start = (f32[128]{0:T(128)S(1)}, f32[128]{0:T(128)}, u32[]{:S(2)}) copy-start(f32[128]{0:T(128)} %param.9) | copy-start | bytes 1540
  7.2 4.3 %copy-start.4 = (s32[3]{0:T(128)S(1)}, s32[3]{0:T(128)}, u32[]{:S(2)}) copy-start(s32[3]{0:T(128)} %param.11) | copy-start | bytes 40
  7.2 105.7 %all-gather.3.cloned.1.call-start = ((), (), s32[]{:S(2)}) async-start(), calls=%async_computation | async-start | bytes 10543104 | tf_op jit(solution)/shard_map/all_gather | solution.py:121
  11.5 6.0 %copy-start.3 = (f32[1536]{0:T(1024)S(1)}, f32[1536]{0:T(1024)}, u32[]{:S(2)}) copy-start(f32[1536]{0:T(1024)} %param.10) | copy-start | bytes 18436
  15.9 11.3 %collective-permute-start = (bf16[3,3,4,832]{3,2,0,1:T(4,128)(2,1)S(1)}, bf16[3,3,4,832]{3,2,0,1:T(4,128)(2,1)S(1)}, u32[]{:S(2)}, u32[]{:S(2)}) collective-permute-start(bf16[3,3,4,832]{3,2,0,1:T(4,128)(2,1)S(1)} %bitcast.97), channel_id=1, source_target_pairs={{0,1},{1,2},{2,3},{3,0},{4,5},{5,6},{6,7},{7,4},{8,9},{9,10},{10,1... | collective-permute-start | bytes 179720 | tf_op jit(solution)/shard_map/ppermute | solution.py:84
  15.9 11.3 %collective-permute-start.1 = (bf16[3,3,4,832]{3,2,0,1:T(4,128)(2,1)S(1)}, bf16[3,3,4,832]{3,2,0,1:T(4,128)(2,1)}, u32[]{:S(2)}, u32[]{:S(2)}) collective-permute-start(bf16[3,3,4,832]{3,2,0,1:T(4,128)(2,1)S(1)} %bitcast.98), channel_id=1, source_target_pairs={{0,2},{1,3},{2,0},{3,1},{4,6},{5,7},{6,4},{7,5},{8,10},{9,11},{10,... | collective-permute-start | bytes 179720 | tf_op jit(solution)/shard_map/ppermute | solution.py:84
  17.3 10.0 %collective-permute-start.2 = (bf16[3,3,4,832]{3,2,0,1:T(4,128)(2,1)S(1)}, bf16[3,3,4,832]{3,2,0,1:T(4,128)(2,1)}, u32[]{:S(2)}, u32[]{:S(2)}) collective-permute-start(bf16[3,3,4,832]{3,2,0,1:T(4,128)(2,1)S(1)} %bitcast.99), channel_id=1, source_target_pairs={{0,3},{1,0},{2,1},{3,2},{4,7},{5,4},{6,5},{7,6},{8,11},{9,8},{10,9... | collective-permute-start | bytes 179720 | tf_op jit(solution)/shard_map/ppermute | solution.py:84
  29.3 8.0 %collective-permute-start.3 = (bf16[4,3,3,4,832]{4,3,1,2,0:T(4,128)(2,1)S(1)}, bf16[4,3,3,4,832]{4,3,1,2,0:T(4,128)(2,1)S(1)}, u32[]{:S(2)}, u32[]{:S(2)}) collective-permute-start(bf16[4,3,3,4,832]{4,3,1,2,0:T(4,128)(2,1)S(1)} %broadcast_select_fusion), channel_id=1, source_target_pairs={{0,4},{4,8},{8,12},{12,0},{1,5},{5,9},{9,13},{13,1},{2,6},{6,10},{... | collective-permute-start | bytes 718856 | tf_op jit(solution)/shard_map/ppermute | solution.py:84
  31.8 13.1 %collective-permute-start.4 = (bf16[4,3,3,4,832]{4,3,1,2,0:T(4,128)(2,1)S(1)}, bf16[4,3,3,4,832]{4,3,1,2,0:T(4,128)(2,1)}, u32[]{:S(2)}, u32[]{:S(2)}) collective-permute-start(bf16[4,3,3,4,832]{4,3,1,2,0:T(4,128)(2,1)S(1)} %broadcast_select_fusion), channel_id=1, source_target_pairs={{0,8},{4,12},{8,0},{12,4},{1,9},{5,13},{9,1},{13,5},{2,10},{6,14},... | collective-permute-start | bytes 718856 | tf_op jit(solution)/shard_map/ppermute | solution.py:84
  32.1 14.7 %collective-permute-start.5 = (bf16[4,3,3,4,832]{4,3,1,2,0:T(4,128)(2,1)S(1)}, bf16[4,3,3,4,832]{4,3,1,2,0:T(4,128)(2,1)}, u32[]{:S(2)}, u32[]{:S(2)}) collective-permute-start(bf16[4,3,3,4,832]{4,3,1,2,0:T(4,128)(2,1)S(1)} %broadcast_select_fusion), channel_id=1, source_target_pairs={{0,12},{4,0},{8,4},{12,8},{1,13},{5,1},{9,5},{13,9},{2,14},{6,2},{... | collective-permute-start | bytes 718856 | tf_op jit(solution)/shard_map/ppermute | solution.py:84
  37.3 9.5 %copy-start.2 = (bf16[4,3,3,4,832]{4,3,1,2,0:T(4,128)(2,1)}, bf16[4,3,3,4,832]{4,3,1,2,0:T(4,128)(2,1)S(1)}, u32[]{:S(2)}) copy-start(bf16[4,3,3,4,832]{4,3,1,2,0:T(4,128)(2,1)S(1)} %collective-permute-done.3) | copy-start | bytes 718852
  57.2 29.7 %collective-permute-start.6 = (bf16[48,3,2,384]{3,0,1,2:T(8,128)(2,1)S(1)}, bf16[48,3,2,384]{3,0,1,2:T(8,128)(2,1)S(1)}, u32[]{:S(2)}, u32[]{:S(2)}) collective-permute-start(bf16[48,3,2,384]{3,0,1,2:T(8,128)(2,1)S(1)} %bitcast.92), channel_id=1, source_target_pairs={{0,0},{1,4},{2,8},{3,12},{4,1},{5,5},{6,9},{7,13},{8,2},{9,6},{10,... | collective-permute-start | bytes 663560 | tf_op jit(solution)/shard_map/ppermute | solution.py:131
  65.6 22.9 %slice-start = ((s8[5308416]{0:T(1024)(128)(4,1)}), s8[4194304]{0:T(1024)(128)(4,1)S(1)}, s32[]{:S(2)}) async-start(s8[5308416]{0:T(1024)(128)(4,1)} %bitcast.85), calls=%async_computation.1 | async-start | bytes 8388608
  86.9 1.6 %slice-start.1 = ((s8[5308416]{0:T(1024)(128)(4,1)}), s8[1114112]{0:T(1024)(128)(4,1)S(1)}, s32[]{:S(2)}) async-start(s8[5308416]{0:T(1024)(128)(4,1)} %bitcast.85), calls=%async_computation.2 | async-start | bytes 2228224
  112.9 21.9 %copy-start.1 = (f32[128]{0:T(128)S(1)}, f32[128]{0:T(128)}, u32[]{:S(2)}) copy-start(f32[128]{0:T(128)} %param.9) | copy-start | bytes 1540
Sparse Core Ops, SparseCore 0:
  10.8 92.2 all-gather.2

commit v13 on v9

--- a/solution.py
+++ b/solution.py
@@ -10,10 +10,11 @@
 
 def transform_kernel(h_ref, v_ref, o_ref):
     pn, _, m, k = h_ref.shape
+    half_q = v_ref.shape[0] // 2
+    vr = jnp.concatenate([v_ref[j, 0] for j in range(half_q)], 0)
+    vi = jnp.concatenate([v_ref[half_q + j, 0] for j in range(half_q)], 0)
     hr = h_ref[:, 0].reshape(pn * m, k)
     hi = h_ref[:, 1].reshape(pn * m, k)
-    vr = v_ref[0, :k, :]
-    vi = v_ref[0, k:, :]
     real = jnp.dot(hr, vr, preferred_element_type=jnp.float32) - jnp.dot(
         hi, vi, preferred_element_type=jnp.float32)
     imag = jnp.dot(hr, vi, preferred_element_type=jnp.float32) + jnp.dot(
@@ -28,11 +29,11 @@
     return half.reshape(pn, 2, 2, m, n).transpose(0, 1, 3, 2, 4).reshape(pn, 2, m, 2 * n)
 
 
-def transform(half, v_blocks):
+def transform(half, pieces):
     pn, _, m, k = half.shape
-    b, rows, w = v_blocks.shape
-    if w % 128 != 0:
-        v = v_blocks.reshape(b, 2, k, w)
+    q, b, r, w = pieces.shape
+    if w % 128 != 0 or q % 2 != 0 or (q // 2) * r != k:
+        v = pieces.transpose(1, 0, 2, 3).reshape(b, 2, k, w)
         hr, hi = half[:, 0], half[:, 1]
         dims = "pmk,bkw->pmbw"
         real = jnp.einsum(dims, hr, v[:, 0], preferred_element_type=jnp.float32) - jnp.einsum(
@@ -42,18 +43,18 @@
         out = jnp.stack([real, imag], 1).astype(jnp.bfloat16)
         return out.reshape(pn, 2, m, b * w)
     flops = 8 * pn * m * k * w * b
-    bytes_accessed = 2 * (half.size + v_blocks.size + pn * 2 * m * b * w)
+    bytes_accessed = 2 * (half.size + pieces.size + pn * 2 * m * b * w)
     return pl.pallas_call(
         transform_kernel,
         grid=(b,),
         in_specs=[
             pl.BlockSpec((pn, 2, m, k), lambda i: (0, 0, 0, 0)),
-            pl.BlockSpec((1, rows, w), lambda i: (i, 0, 0)),
+            pl.BlockSpec((q, 1, r, w), lambda i: (0, i, 0, 0)),
         ],
         out_specs=pl.BlockSpec((pn, 2, m, w), lambda i: (0, 0, 0, i)),
         out_shape=jax.ShapeDtypeStruct((pn, 2, m, b * w), jnp.bfloat16),
         cost_estimate=pl.CostEstimate(flops=flops, bytes_accessed=bytes_accessed, transcendentals=0),
-    )(half, v_blocks)
+    )(half, pieces)
 
 
 def pair_terms(batch_rows, column_rows):
@@ -106,15 +107,15 @@
     gathered = gather_group(by_pair, ("aux",), (n_aux,))
     count = n_aux * n_pair * vectors
     half_rows = gathered.reshape(count * batch, 4, orbitals).transpose(1, 0, 2)
-    sel_own = transform(merge_spin(half_rows[None]), v_local[None])
+    sel_own = transform(merge_spin(half_rows[None]), v_local.reshape(8, 1, rows // 8, a_width))
     sel_own = sel_own.reshape(2, count, batch, a_width)
 
     n_q = n_parts * n_aux
     rows_q = rows // n_q
     q = lax.axis_index("parts") * n_aux + lax.axis_index("aux")
     piece = lax.dynamic_slice_in_dim(v_local, q * rows_q, rows_q, 0)
-    v_full = lax.all_gather(piece, ("pair", "parts", "aux"), axis=0, tiled=True)
-    v_full = v_full.reshape(n_pair, rows, a_width)
+    v_full = lax.all_gather(piece, ("parts", "aux", "pair"), axis=0)
+    v_full = v_full.reshape(n_q, n_pair, rows_q, a_width)
     half = jnp.einsum(
         "kmj,pmn->pkjn", occ_left, cholesky, preferred_element_type=jnp.float32
     ).astype(jnp.bfloat16)

time: 143 us -> 143 us (level)
  no operation moved by 1% of the time
where the time goes in v13:
time: 143 us; the launch traced here: 142 us
  local copies, waits for them, and re-layouts  41 us (29%)
  waiting for transfers between devices  30.4 us (21%)
  Pallas kernels  19.1 us (13%)
  between operations  14.3 us (10%)
  starting transfers between devices  12.9 us (9%)
  other arithmetic  12.4 us (9%)
  matrix products  12.2 us (9%)
    unnamed x14, local copies, waits for them, and re-layouts  25.3 us
    ppermute x1, waiting for transfers between devices, on_device(): sel_b = lax.ppermute(sel_a, ('aux', 'pair'), perm)  21.1 us
    pallas_call x2, Pallas kernels, transform(): pl.pallas_call(transform_kernel, grid=(b,), in_specs=[pl.BlockSpec((pn, 2...  19.1 us
    ppermute x6, waiting for transfers between devices, gather_group(): blocks.append(lax.ppermute(x, axes, perm))  9.23 us
    ppermute x1, starting transfers between devices, on_device(): sel_b = lax.ppermute(sel_a, ('aux', 'pair'), perm)  8.3 us
    dot_general x1, matrix products, on_device(): jnp.einsum('kmj,pmn->pkjn', occ_left, cholesky, preferred_element_type=jn...  7.58 us
    reshape x3, local copies, waits for them, and re-layouts, merge_spin(): half.reshape(pn, 2, 2, m, n).transpose(0, 1, 3, 2, 4)  6.6 us
    div x1, other arithmetic, on_device(): amplitudes = paired / denominator  4.61 us
  transfers between devices with their start and end apart: 8, of which 3 were waited for; matrix products, arithmetic and copies ran while one was open for 41% of the time, Pallas kernels for 3%

profile of v13, /device:TPU:29, one launch (start us, length us, event | category | flops | bytes accessed | tf_op | source)
XLA Modules:
  0.0 142.3 jit_solution(10906324473016142054)
XLA Ops:
  7.2 0.0 copy-start
  7.2 0.0 all-gather.3.cloned.1.call-start
  7.2 1.7 %constant_dynamic-slice_fusion = bf16[416,384]{1,0:T(8,128)(2,1)} fusion(bf16[3328,384]{1,0:T(8,128)(2,1)} %bitcast.96, s32[]{:T(128)S(6)} %select_n.110), kind=kLoop, calls=%fused_computation.72 | loop fusion | bytes 638980 | tf_op jit(solution)/shard_map/dynamic_slice | solution.py:116
  9.0 0.0 all-gather.3.cloned.1.call-update
  9.0 1.2 slice_bitcast_fusion
  10.2 0.1 pad_maximum_fusion.1
  10.3 1.2 copy.18
  11.6 0.6 gather_fusion
  12.2 0.6 gather_fusion.3
  12.8 3.0 %fusion.8 = bf16[4,3,3,832]{3,0,2,1:T(4,128)(2,1)S(1)} fusion(bf16[3,832,832]{2,1,0:T(8,128)(2,1)} %param.6, bf16[3,4,832]{2,1,0:T(4,128)(2,1)S(1)} %gather_fusion, pred[3]{0:T(512)(128)(4,1)S(1)} %get-tuple-element.7), kind=kOutput, calls=%fused_computation.12 | convolution fusion | flops 49880064 | bytes 4233219 | tf_op jit(solution)/shard_map/kmi,pmn->pikn/dot_general | solution.py:103
  15.9 0.1 collective-permute-start
  15.9 1.3 collective-permute-start.1
  17.3 0.2 collective-permute-start.2
  17.5 0.1 fusion.30
  17.6 0.1 broadcast_add_fusion
  17.7 0.1 broadcast_subtract_fusion.1
  17.7 2.9 %broadcast_subtract_fusion = f32[384,3,3,384]{0,3,1,2:T(8,128)} fusion(f32[384]{0:T(512)S(1)} %get-tuple-element.17, f32[3,3,384]{2,0,1:T(4,128)S(1)} %broadcast_subtract_fusion.1), kind=kLoop, calls=%fused_computation.10 | loop fusion | flops 1327104 | bytes 5323776 | tf_op jit(solution)/shard_map/sub | solution.py:141
  20.6 7.6 %fusion.5 = bf16[4,128,3,832]{1,3,2,0:T(8,128)(2,1)} fusion(bf16[3,832,832]{2,1,0:T(8,128)(2,1)} %param.6, bf16[2,832,128]{2,1,0:T(8,128)(2,1)S(1)} %get-tuple-element.9, bf16[2,832,128]{2,1,0:T(8,128)(2,1)S(1)} %get-tuple-element.8), kind=kOutput, calls=%fused_computation.11 | convolution fusion | flops 2129494016 | bytes 7561216 | tf_op jit(solution)/shard_map/kmj,pmn->pkjn/dot_general | solution.py:119
  28.3 0.2 pad_maximum_fusion.2
  28.5 0.8 gather_fusion.1
  29.3 0.2 broadcast_select_fusion
  29.5 2.5 %collective-permute-start.3 = (bf16[4,3,3,4,832]{4,3,1,2,0:T(4,128)(2,1)S(1)}, bf16[4,3,3,4,832]{4,3,1,2,0:T(4,128)(2,1)S(1)}, u32[]{:S(2)}, u32[]{:S(2)}) collective-permute-start(bf16[4,3,3,4,832]{4,3,1,2,0:T(4,128)(2,1)S(1)} %broadcast_select_fusion), channel_id=1, source_target_pairs={{0,4},{4,8},{8,12},{12,0},{1,5},{5,9},{9,13},{13,1},{2,6},{6,10},{... | collective-permute-start | bytes 718856 | tf_op jit(solution)/shard_map/ppermute | solution.py:80
  32.0 0.3 collective-permute-start.4
  32.3 0.2 collective-permute-start.5
  32.5 0.1 broadcast_in_dim.47
  32.6 0.1 broadcast_in_dim.48
  32.7 1.9 %copy.16 = bf16[3,2,2,128,832]{3,4,2,1,0:T(8,128)(2,1)S(1)} copy(bf16[3,2,2,128,832]{3,4,0,2,1:T(8,128)(2,1)} %bitcast.98) | data formatting | bytes 5111808 | tf_op jit(solution)/shard_map/reshape | solution.py:29
  34.6 3.1 %copy.17.h_ref = bf16[3,2,128,1664]{3,2,1,0:T(8,128)(2,1)} copy(bf16[3,2,128,1664]{2,3,1,0:T(8,128)(2,1)S(1)} %bitcast.93) | data formatting | bytes 5111808 | tf_op jit(solution)/shard_map/reshape | solution.py:29
  37.7 0.2 bitcast_select_fusion.1
  37.9 7.4 %collective-permute-done.4 = bf16[4,3,3,4,832]{4,3,1,2,0:T(4,128)(2,1)} collective-permute-done((bf16[4,3,3,4,832]{4,3,1,2,0:T(4,128)(2,1)S(1)}, bf16[4,3,3,4,832]{4,3,1,2,0:T(4,128)(2,1)}, u32[]{:S(2)}, u32[]{:S(2)}) %collective-permute-start.4) | collective-permute-done | bytes 239648 | tf_op jit(solution)/shard_map/ppermute | solution.py:80
  45.3 1.8 %collective-permute-done.5 = bf16[4,3,3,4,832]{4,3,1,2,0:T(4,128)(2,1)} collective-permute-done((bf16[4,3,3,4,832]{4,3,1,2,0:T(4,128)(2,1)S(1)}, bf16[4,3,3,4,832]{4,3,1,2,0:T(4,128)(2,1)}, u32[]{:S(2)}, u32[]{:S(2)}) %collective-permute-start.5) | collective-permute-done | bytes 239648 | tf_op jit(solution)/shard_map/ppermute | solution.py:80
  47.1 2.0 %pad_maximum_fusion = bf16[4,4,3,3,4,832]{5,4,2,3,1,0:T(4,128)(2,1)S(1)} fusion(bf16[1,4,3,3,4,832]{5,4,2,3,1,0:T(4,128)(2,1)} %bitcast.25, bf16[1,4,3,3,4,832]{5,4,2,3,1,0:T(4,128)(2,1)} %bitcast.24, bf16[1,4,3,3,4,832]{5,4,2,3,1,0:T(4,128)(2,1)S(1)} %bitcast.104, bf16[1,4,3,3,4,832]{5,4,2,3,1,0:T(4,128)(2,1)S(1)} %bitcast_select_fusion.1), kind=kLoop, calls=%fused_computation.13 | loop fusion | flops 1437696 | bytes 1916928 | tf_op jit(solution)/shard_map/stack | solution.py:81
  49.2 1.5 %gather_fusion.2 = bf16[4,4,3,3,4,832]{5,4,2,3,1,0:T(4,128)(2,1)S(1)} fusion(bf16[4,4,3,3,4,832]{5,4,2,3,1,0:T(4,128)(2,1)S(1)} %pad_maximum_fusion, s32[1024]{0:T(1024)S(1)} %pad_clamp_fusion), kind=kCustom, calls=%fused_computation.2 | custom fusion | bytes 1916944 | tf_op jit(solution)/shard_map/jit(_take)/gather | solution.py:82
  50.6 0.4 copy.19
  51.0 0.6 bitcast_select_fusion
  51.6 0.1 copy.20
  51.8 0.8 copy.21
  52.6 1.6 %reshape.205.h_ref = bf16[1,2,144,1664]{3,2,1,0:T(8,128)(2,1)} reshape(bf16[1,2,144,2,832]{4,3,2,1,0:T(2,128)(2,1)S(1)} %copy.21) | data formatting | bytes 1916928 | tf_op jit(solution)/shard_map/reshape | solution.py:29
  54.2 4.0 %shard_map.78 = bf16[1,2,144,384]{3,2,1,0:T(8,128)(2,1)} custom-call(bf16[1,2,144,1664]{3,2,1,0:T(8,128)(2,1)} %reshape.205.h_ref, bf16[8,1,416,384]{3,2,1,0:T(8,128)(2,1)} %bitcast.97), custom_call_target="tpu_custom_call" | custom-call | flops 736100352 | bytes 3735552 | tf_op jit(solution)/shard_map/pallas_call | solution.py:47
  58.2 1.1 copy.22
  59.3 8.3 %collective-permute-start.6 = (bf16[48,3,2,384]{3,0,1,2:T(8,128)(2,1)S(1)}, bf16[48,3,2,384]{3,0,1,2:T(8,128)(2,1)S(1)}, u32[]{:S(2)}, u32[]{:S(2)}) collective-permute-start(bf16[48,3,2,384]{3,0,1,2:T(8,128)(2,1)S(1)} %bitcast.100), channel_id=1, source_target_pairs={{0,0},{1,4},{2,8},{3,12},{4,1},{5,5},{6,9},{7,13},{8,2},{9,6},{10,... | collective-permute-start | bytes 663560 | tf_op jit(solution)/shard_map/ppermute | solution.py:127
  67.8 21.1 %collective-permute-done.6 = bf16[48,3,2,384]{3,0,1,2:T(8,128)(2,1)S(1)} collective-permute-done((bf16[48,3,2,384]{3,0,1,2:T(8,128)(2,1)S(1)}, bf16[48,3,2,384]{3,0,1,2:T(8,128)(2,1)S(1)}, u32[]{:S(2)}, u32[]{:S(2)}) %collective-permute-start.6) | collective-permute-done | bytes 221216 | tf_op jit(solution)/shard_map/ppermute | solution.py:127
  88.9 0.0 slice-start.1
  88.9 1.6 %fusion.12 = f32[2,3,384,3,384]{4,2,3,1,0:T(8,128)S(1)} fusion(bf16[96,1,3,384]{3,0,2,1:T(8,128)(2,1)S(1)} %get-tuple-element.15, bf16[96,1,3,384]{3,0,2,1:T(8,128)(2,1)S(1)} %get-tuple-element.14, bf16[48,3,384]{2,0,1:T(8,128)(2,1)S(1)} %get-tuple-element.11, bf16[48,3,384]{2,0,1:T(8,128)(2,1)S(1)} %get-tuple-element.10), kind=kOutput, calls=%fused_computation.18 | convolution fusion | flops 510935040 | bytes 11280384 | tf_op jit(solution)/shard_map/pjb,pcia->bcija/dot_general | solution.py:65
  90.5 4.6 %fusion = f32[384,2,3,3,384]{0,4,2,3,1:T(8,128)} fusion(f32[2,3,384,3,384]{4,2,3,1,0:T(8,128)S(1)} %fusion.12, f32[384,3,3,384]{0,3,1,2:T(8,128)S(1)} %bitcast.92), kind=kLoop, calls=%fused_computation.5 | loop fusion | flops 5308416 | bytes 26542080 | tf_op jit(solution)/shard_map/div | solution.py:145
  95.1 19.7 %copy.26 = f32[384,2,3,3,384]{4,1,3,2,0:T(2,128)} copy(f32[384,2,3,3,384]{0,4,2,3,1:T(8,128)} %fusion) | data formatting | bytes 21233664
  114.9 15.1 %shard_map.77 = bf16[3,2,128,1536]{3,2,1,0:T(8,128)(2,1)} custom-call(bf16[3,2,128,1664]{3,2,1,0:T(8,128)(2,1)} %copy.17.h_ref, bf16[8,4,416,384]{3,2,1,0:T(8,128)(2,1)} %bitcast.112), custom_call_target="tpu_custom_call" | custom-call | flops 7851737088 | bytes 15138816 | tf_op jit(solution)/shard_map/pallas_call | solution.py:47
  130.0 5.5 %copy.25 = bf16[3,128,2,1536]{3,2,1,0:T(2,128)(2,1)} copy(bf16[3,128,2,1536]{3,1,2,0:T(8,128)(2,1)} %bitcast.99) | data formatting | bytes 4718592
  (30 shorter events, 0.3 us)
Async XLA Ops:
  7.2 5.0 %copy-start = (f32[128]{0:T(128)S(1)}, f32[128]{0:T(128)}, u32[]{:S(2)}) copy-start(f32[128]{0:T(128)} %param.9) | copy-start | bytes 1540
  7.2 4.3 %copy-start.3 = (s32[3]{0:T(128)S(1)}, s32[3]{0:T(128)}, u32[]{:S(2)}) copy-start(s32[3]{0:T(128)} %param.11) | copy-start | bytes 40
  7.2 107.7 %all-gather.3.cloned.1.call-start = ((), (), s32[]{:S(2)}) async-start(), calls=%async_computation | async-start | bytes 10543104 | tf_op jit(solution)/shard_map/all_gather | solution.py:117
  11.5 6.0 %copy-start.2 = (f32[1536]{0:T(1024)S(1)}, f32[1536]{0:T(1024)}, u32[]{:S(2)}) copy-start(f32[1536]{0:T(1024)} %param.10) | copy-start | bytes 18436
  15.9 12.4 %collective-permute-start = (bf16[3,3,4,832]{3,2,0,1:T(4,128)(2,1)S(1)}, bf16[3,3,4,832]{3,2,0,1:T(4,128)(2,1)S(1)}, u32[]{:S(2)}, u32[]{:S(2)}) collective-permute-start(bf16[3,3,4,832]{3,2,0,1:T(4,128)(2,1)S(1)} %bitcast.105), channel_id=1, source_target_pairs={{0,1},{1,2},{2,3},{3,0},{4,5},{5,6},{6,7},{7,4},{8,9},{9,10},{10,1... | collective-permute-start | bytes 179720 | tf_op jit(solution)/shard_map/ppermute | solution.py:80
  15.9 12.3 %collective-permute-start.1 = (bf16[3,3,4,832]{3,2,0,1:T(4,128)(2,1)S(1)}, bf16[3,3,4,832]{3,2,0,1:T(4,128)(2,1)S(1)}, u32[]{:S(2)}, u32[]{:S(2)}) collective-permute-start(bf16[3,3,4,832]{3,2,0,1:T(4,128)(2,1)S(1)} %bitcast.106), channel_id=1, source_target_pairs={{0,2},{1,3},{2,0},{3,1},{4,6},{5,7},{6,4},{7,5},{8,10},{9,11},{10,... | collective-permute-start | bytes 179720 | tf_op jit(solution)/shard_map/ppermute | solution.py:80
  17.3 11.0 %collective-permute-start.2 = (bf16[3,3,4,832]{3,2,0,1:T(4,128)(2,1)S(1)}, bf16[3,3,4,832]{3,2,0,1:T(4,128)(2,1)S(1)}, u32[]{:S(2)}, u32[]{:S(2)}) collective-permute-start(bf16[3,3,4,832]{3,2,0,1:T(4,128)(2,1)S(1)} %bitcast.107), channel_id=1, source_target_pairs={{0,3},{1,0},{2,1},{3,2},{4,7},{5,4},{6,5},{7,6},{8,11},{9,8},{10,9... | collective-permute-start | bytes 179720 | tf_op jit(solution)/shard_map/ppermute | solution.py:80
  29.5 8.4 %collective-permute-start.3 = (bf16[4,3,3,4,832]{4,3,1,2,0:T(4,128)(2,1)S(1)}, bf16[4,3,3,4,832]{4,3,1,2,0:T(4,128)(2,1)S(1)}, u32[]{:S(2)}, u32[]{:S(2)}) collective-permute-start(bf16[4,3,3,4,832]{4,3,1,2,0:T(4,128)(2,1)S(1)} %broadcast_select_fusion), channel_id=1, source_target_pairs={{0,4},{4,8},{8,12},{12,0},{1,5},{5,9},{9,13},{13,1},{2,6},{6,10},{... | collective-permute-start | bytes 718856 | tf_op jit(solution)/shard_map/ppermute | solution.py:80
  32.0 13.3 %collective-permute-start.4 = (bf16[4,3,3,4,832]{4,3,1,2,0:T(4,128)(2,1)S(1)}, bf16[4,3,3,4,832]{4,3,1,2,0:T(4,128)(2,1)}, u32[]{:S(2)}, u32[]{:S(2)}) collective-permute-start(bf16[4,3,3,4,832]{4,3,1,2,0:T(4,128)(2,1)S(1)} %broadcast_select_fusion), channel_id=1, source_target_pairs={{0,8},{4,12},{8,0},{12,4},{1,9},{5,13},{9,1},{13,5},{2,10},{6,14},... | collective-permute-start | bytes 718856 | tf_op jit(solution)/shard_map/ppermute | solution.py:80
  32.3 14.8 %collective-permute-start.5 = (bf16[4,3,3,4,832]{4,3,1,2,0:T(4,128)(2,1)S(1)}, bf16[4,3,3,4,832]{4,3,1,2,0:T(4,128)(2,1)}, u32[]{:S(2)}, u32[]{:S(2)}) collective-permute-start(bf16[4,3,3,4,832]{4,3,1,2,0:T(4,128)(2,1)S(1)} %broadcast_select_fusion), channel_id=1, source_target_pairs={{0,12},{4,0},{8,4},{12,8},{1,13},{5,1},{9,5},{13,9},{2,14},{6,2},{... | collective-permute-start | bytes 718856 | tf_op jit(solution)/shard_map/ppermute | solution.py:80
  59.3 29.5 %collective-permute-start.6 = (bf16[48,3,2,384]{3,0,1,2:T(8,128)(2,1)S(1)}, bf16[48,3,2,384]{3,0,1,2:T(8,128)(2,1)S(1)}, u32[]{:S(2)}, u32[]{:S(2)}) collective-permute-start(bf16[48,3,2,384]{3,0,1,2:T(8,128)(2,1)S(1)} %bitcast.100), channel_id=1, source_target_pairs={{0,0},{1,4},{2,8},{3,12},{4,1},{5,5},{6,9},{7,13},{8,2},{9,6},{10,... | collective-permute-start | bytes 663560 | tf_op jit(solution)/shard_map/ppermute | solution.py:127
  67.7 22.8 %slice-start = ((s8[5308416]{0:T(1024)(128)(4,1)}), s8[4194304]{0:T(1024)(128)(4,1)S(1)}, s32[]{:S(2)}) async-start(s8[5308416]{0:T(1024)(128)(4,1)} %bitcast.91), calls=%async_computation.1 | async-start | bytes 8388608
  88.9 1.6 %slice-start.1 = ((s8[5308416]{0:T(1024)(128)(4,1)}), s8[1114112]{0:T(1024)(128)(4,1)S(1)}, s32[]{:S(2)}) async-start(s8[5308416]{0:T(1024)(128)(4,1)} %bitcast.91), calls=%async_computation.2 | async-start | bytes 2228224
  114.9 20.6 %copy-start.1 = (f32[128]{0:T(128)S(1)}, f32[128]{0:T(128)}, u32[]{:S(2)}) copy-start(f32[128]{0:T(128)} %param.9) | copy-start | bytes 1540
Sparse Core Ops, SparseCore 0:
  10.8 92.5 all-gather.2
